TPU v7x, 128 devices: a whole 4x4x4 slice. The times are simulated.
128 devices in a mesh: ma: 16 (over x, z), band: 8 (over y, core).
Axes of the slice: x: 4, y: 4, z: 4, core: 2. Of those that a mesh axis runs over, the one named last changes fastest.
Arguments:
- harmonics: bfloat16 [128, 8192, 256], P(('ma', 'band')), may hold values from -6 to 6
- legendre: bfloat16 [128, 2, 8192, 512], P(('ma', 'band')), may hold values from -0.0029296875 to 0.0029296875
- m_values: int32 [128], replicated, may hold values from 1 to 8191
- cycle_cell: int32 [16384], P(('ma', 'band')), may hold values from 0 to 63, as said below
- phi_cell: int32 [16384], P(('ma', 'band')), may hold values from 3 to 123
- offsets: float32 [2, 16384], P(None, ('ma', 'band')), may hold values from 0 to 1
Outputs:
- lensed: float32 [16384, 128], P(('ma', 'band'))
Inputs may be any that keep to these rules, and one draw needn't show every extreme that they name: `cycle_cell`: Band-local cycle; every point held by device (ma, band) lies in latitude band `band`. For each device and each ma index q, at most 16 of its points have cycles q * 4 to q * 4 + 3, and in every band one q receives exactly 16 points from every device of the band.
All inputs are finite; a program needn't handle non-finite values.
Results may differ from a plain program's by a relative error of at most 0.0053.
Values may be sent and summed in bfloat16 or wider, within the bound.
No kernel may reach another device: no remote copies, remote signals or barrier semaphores. Data moves between devices by JAX's collectives and lax.ppermute only.
A program may use at most 64 MiB of HBM per device.

v0:
```python
import jax
import jax.numpy as jnp
from jax import lax
from jax.sharding import PartitionSpec as P

NPHI = 128


def with_halo(x, sides, width):
    for axis, dim in sides:
        count, length = (lax.axis_size(axis), x.shape[dim])
        up = [(i, (i + 1) % count) for i in range(count - 1)]
        down = [(j, i) for i, j in up]
        last = lax.slice_in_dim(x, length - width, length, axis=dim)
        first = lax.slice_in_dim(x, 0, width, axis=dim)
        before = lax.ppermute(last, axis, up)
        after = lax.ppermute(first, axis, down)
        x = jnp.concatenate([before, x, after], axis=dim)
    return x


def kernel_taps(shifts):
    return jnp.sinc(shifts) * jnp.sinc(shifts / 4.0)


def combine_parts(plus_part, minus_part):
    q_real = -(plus_part[:, 0, 0] - minus_part[:, 1, 1])
    q_imag = -(plus_part[:, 0, 1] + minus_part[:, 1, 0])
    u_real = -(plus_part[:, 1, 0] + minus_part[:, 0, 1])
    u_imag = -(plus_part[:, 1, 1] - minus_part[:, 0, 0])
    real_part = jnp.concatenate([q_real, u_real], axis=1)
    imag_part = jnp.concatenate([q_imag, u_imag], axis=1)
    return jnp.stack([real_part, imag_part], axis=1).astype(jnp.bfloat16)


def phase_table(m_values, cell_count, lmax_width):
    pixel_index = jnp.arange(cell_count, dtype=jnp.int32)
    period = 2 * lmax_width
    phase_turns = m_values[None, :] * pixel_index[:, None] % period
    angles = phase_turns.astype(jnp.float32) * (2.0 * jnp.pi / period)
    return jnp.stack([jnp.cos(angles), -jnp.sin(angles)], axis=-1).astype(jnp.bfloat16)


def spectral_cycles(phase_rows, spectra):
    summed = jnp.einsum("kmi,mric->rkc", phase_rows, spectra, preferred_element_type=jnp.float32)
    return (2.0 * summed).astype(jnp.bfloat16)


def spread_weights(starts, weights, length):
    tap_index = jnp.arange(8, dtype=jnp.int32)
    target = starts[:, None] + tap_index[None, :]
    cells = jnp.arange(length, dtype=jnp.int32)
    hits = (target[:, :, None] == cells[None, None, :]).astype(jnp.float32)
    return jnp.sum(weights[:, :, None] * hits, axis=1)


def on_device(harmonics, legendre, m_values, cycle_cell, phi_cell, offsets):
    evolutions = harmonics.shape[2] // 4
    cycle_total = legendre.shape[3]
    contract = (((0,), (0,)), ((), ()))
    plus_part = lax.dot_general(
        legendre[0, 0], harmonics[0], contract, preferred_element_type=jnp.float32
    )
    minus_part = lax.dot_general(
        legendre[0, 1], harmonics[0], contract, preferred_element_type=jnp.float32
    )
    spectra = combine_parts(
        plus_part.reshape(cycle_total, 2, 2, evolutions),
        minus_part.reshape(cycle_total, 2, 2, evolutions),
    )
    width_out = spectra.shape[2]
    owner_count = lax.axis_size("ma")
    band_count = lax.axis_size("band")
    cycle_depth = cycle_total // (owner_count * band_count)
    received = lax.all_to_all(
        spectra[None], ("ma", "band"), split_axis=1, concat_axis=0, tiled=True
    )
    phase_rows = phase_table(m_values, NPHI, harmonics.shape[1])
    own_grid = spectral_cycles(phase_rows, received)
    extended = with_halo(own_grid, (("ma", 0),), 4)
    ext_rows = extended.shape[0]
    flat_grid = extended.reshape(ext_rows * NPHI, width_out)
    first_cycle = lax.axis_index("ma") * cycle_depth
    capacity = cycle_cell.shape[0] // 8
    owner_index = cycle_cell // cycle_depth
    one_hot = (owner_index[:, None] == jnp.arange(owner_count, dtype=jnp.int32)[None, :]).astype(
        jnp.int32
    )
    slot_index = jnp.sum((jnp.cumsum(one_hot, axis=0) - one_hot) * one_hot, axis=1)
    flat_slot = owner_index * capacity + slot_index
    placement = (
        flat_slot[:, None] == jnp.arange(owner_count * capacity, dtype=jnp.int32)[None, :]
    ).astype(jnp.float32)
    point_table = jnp.stack(
        [cycle_cell.astype(jnp.float32), phi_cell.astype(jnp.float32), offsets[0], offsets[1]],
        axis=1,
    )
    buffers = jnp.dot(placement.T, point_table, precision=lax.Precision.HIGHEST).reshape(
        owner_count, capacity, 4
    )
    cycle_buffer = buffers[:, :, 0].astype(jnp.int32)
    phi_buffer = buffers[:, :, 1].astype(jnp.int32)
    offset_buffer = buffers[:, :, 2:4]
    cycles_here = lax.all_to_all(cycle_buffer, "ma", split_axis=0, concat_axis=0, tiled=True)
    phis_here = lax.all_to_all(phi_buffer, "ma", split_axis=0, concat_axis=0, tiled=True)
    offsets_here = lax.all_to_all(offset_buffer, "ma", split_axis=0, concat_axis=0, tiled=True)
    sources, items = cycles_here.shape
    cycles_flat = cycles_here.reshape(-1)
    phis_flat = phis_here.reshape(-1)
    pairs = offsets_here.reshape(-1, 2)
    tap_shift = jnp.arange(8).astype(jnp.float32) - 3.0
    across = kernel_taps(tap_shift[None, :] - pairs[:, 0:1])
    beside_all = kernel_taps(tap_shift[None, :] - pairs[:, 1:2])
    cycle_weights = spread_weights(cycles_flat + 1 - first_cycle, across, ext_rows)
    phi_weights = spread_weights(phis_flat - 3, beside_all, NPHI)
    dense = (cycle_weights[:, :, None] * phi_weights[:, None, :]).astype(jnp.bfloat16)
    dense = dense.reshape(cycles_flat.shape[0], ext_rows * NPHI)
    values = jnp.dot(dense, flat_grid, preferred_element_type=jnp.float32)
    values = values.reshape(sources, items, width_out)
    returned = lax.all_to_all(values, "ma", split_axis=0, concat_axis=0, tiled=True)
    return jnp.dot(
        placement,
        returned.reshape(owner_count * capacity, width_out),
        precision=lax.Precision.HIGHEST,
    )


def solution(mesh):
    in_specs = (
        P(("ma", "band"), None, None),
        P(("ma", "band"), None, None, None),
        P(),
        P(("ma", "band")),
        P(("ma", "band")),
        P(None, ("ma", "band")),
    )
    out_specs = P(("ma", "band"), None)
    return jax.shard_map(
        on_device, mesh=mesh, in_specs=in_specs, out_specs=out_specs, check_vma=False
    )
```

profile of v0, /device:TPU:0, one launch (start us, length us, event | category | flops | bytes accessed | tf_op | source)
XLA Modules:
  0.0 100.5 jit_solution(4948932564756850836)
XLA Ops:
  0.0 0.7 convert_bitcast_fusion.1
  0.8 0.2 reduce_window_sum.11
  1.0 0.2 select_reduce_fusion.2
  1.2 0.8 slice_bitcast_fusion.1
  2.0 0.7 convert_bitcast_fusion
  2.6 0.2 fusion.19
  2.9 0.6 slice_convert_fusion.1
  3.5 8.0 %all-to-all-start = ((s32[16,1,16]{2,1,0:T(1,128)}), s32[16,1,16]{2,1,0:T(1,128)S(1)}, u32[]{:S(2)}, u32[]{:S(2)}) async-start(s32[16,1,16]{2,1,0:T(1,128)} %bitcast.4), calls=%async_computation | async-start | bytes 16384 | tf_op jit(solution)/shard_map/all_to_all | solution.py:104
  11.5 6.4 %copy.40 = bf16[1,8192,256]{1,2,0:T(8,128)(2,1)} copy(bf16[1,8192,256]{2,1,0:T(8,128)(2,1)} %param.7) | data formatting | bytes 8388608 | tf_op args[0]
  17.9 7.0 %fusion = f32[512,2,2,64]{0,3,2,1:T(8,128)S(1)} fusion(bf16[2,2,64,8192]{3,2,1,0:T(8,128)(2,1)} %bitcast.73, bf16[1,2,8192,512]{3,2,1,0:T(8,128)(2,1)} %param.8), kind=kOutput, calls=%fused_computation | convolution fusion | flops 2147483648 | bytes 13107200 | tf_op jit(solution)/shard_map/dot_general | solution.py:64
  25.0 3.6 %copy-done.2 = bf16[1,2,8192,512]{3,2,1,0:T(8,128)(2,1)S(1)} copy-done((bf16[1,2,8192,512]{3,2,1,0:T(8,128)(2,1)S(1)}, bf16[1,2,8192,512]{3,2,1,0:T(8,128)(2,1)}, u32[]{:S(2)}) %copy-start.2) | copy-done | bytes 16777240
  28.5 2.3 %fusion.2 = f32[512,2,2,64]{0,3,2,1:T(8,128)S(1)} fusion(bf16[2,2,64,8192]{3,2,1,0:T(8,128)(2,1)S(1)} %bitcast.74, bf16[1,2,8192,512]{3,2,1,0:T(8,128)(2,1)S(1)} %copy-done.2), kind=kOutput, calls=%fused_computation.2 | convolution fusion | flops 2147483648 | bytes 13107200 | tf_op jit(solution)/shard_map/dot_general | solution.py:61
  30.9 0.3 cosine_convert_fusion
  31.4 7.2 %all-to-all-start.2 = ((s32[16,1,16]{2,1,0:T(1,128)}), s32[16,1,16]{2,1,0:T(1,128)S(1)}, u32[]{:S(2)}, u32[]{:S(2)}) async-start(s32[16,1,16]{2,1,0:T(1,128)} %bitcast.7), calls=%async_computation.2 | async-start | bytes 16384 | tf_op jit(solution)/shard_map/all_to_all | solution.py:105
  38.6 0.9 copy.41
  39.5 0.6 copy.35
  40.1 6.1 %all-to-all-done.2 = s32[16,1,16]{2,1,0:T(1,128)S(1)} async-done(((s32[16,1,16]{2,1,0:T(1,128)}), s32[16,1,16]{2,1,0:T(1,128)S(1)}, u32[]{:S(2)}, u32[]{:S(2)}) %all-to-all-start.2) | async-done | bytes 1056 | tf_op jit(solution)/shard_map/all_to_all | solution.py:105
  46.2 3.5 %all-to-all-start.1 = ((f32[16,16,2]{1,2,0:T(2,128)}), f32[16,16,2]{1,2,0:T(2,128)S(1)}, u32[]{:S(2)}, u32[]{:S(2)}) async-start(f32[16,16,2]{1,2,0:T(2,128)} %copy.35), calls=%async_computation.1 | async-start | bytes 32768 | tf_op jit(solution)/shard_map/all_to_all | solution.py:106
  50.0 7.2 %all-to-all-done.1 = f32[16,16,2]{1,2,0:T(2,128)S(1)} async-done(((f32[16,16,2]{1,2,0:T(2,128)}), f32[16,16,2]{1,2,0:T(2,128)S(1)}, u32[]{:S(2)}, u32[]{:S(2)}) %all-to-all-start.1) | async-done | bytes 2080 | tf_op jit(solution)/shard_map/all_to_all | solution.py:106
  57.2 6.4 %all-to-all-start.3 = ((bf16[1,512,2,128]{3,2,0,1:T(2,128)(2,1)}), bf16[1,512,2,128]{3,2,0,1:T(2,128)(2,1)S(1)}, u32[]{:S(2)}, u32[]{:S(2)}) async-start(bf16[1,512,2,128]{3,2,0,1:T(2,128)(2,1)} %copy.41), calls=%async_computation.3 | async-start | bytes 524288 | tf_op jit(solution)/shard_map/all_to_all | solution.py:75
  64.0 0.1 copy.39
  64.2 1.3 %select_reduce_fusion = f32[256,128]{1,0:T(8,128)S(1)} fusion(f32[256,8]{1,0:T(8,128)S(1)} %copy.39, s32[256,8]{1,0:T(8,128)S(1)} %iota_add_fusion), kind=kLoop, calls=%fused_computation.11 | loop fusion | flops 753664 | bytes 147456 | tf_op jit(solution)/shard_map/reduce_sum | solution.py:54
  65.4 8.9 %all-to-all-done.3 = bf16[1,512,2,128]{3,2,0,1:T(2,128)(2,1)S(1)} async-done(((bf16[1,512,2,128]{3,2,0,1:T(2,128)(2,1)}), bf16[1,512,2,128]{3,2,0,1:T(2,128)(2,1)S(1)}, u32[]{:S(2)}, u32[]{:S(2)}) %all-to-all-start.3) | async-done | bytes 262176 | tf_op jit(solution)/shard_map/all_to_all | solution.py:75
  74.4 0.2 fusion.8
  74.6 2.7 %collective-permute-start = (bf16[4,128,128]{2,1,0:T(8,128)(2,1)S(1)}, bf16[4,128,128]{2,1,0:T(8,128)(2,1)S(1)}, u32[]{:S(2)}, u32[]{:S(2)}) collective-permute-start(bf16[4,128,128]{2,1,0:T(8,128)(2,1)S(1)} %fusion.8), channel_id=1, source_target_pairs={{0,8},{8,16},{16,24},{24,32},{32,40},{40,48},{48,56},{56,64},{64,7... | collective-permute-start | bytes 393224 | tf_op jit(solution)/shard_map/ppermute | solution.py:16
  77.3 1.3 %collective-permute-start.1 = (bf16[4,128,128]{2,1,0:T(8,128)(2,1)S(1)}, bf16[4,128,128]{2,1,0:T(8,128)(2,1)S(1)}, u32[]{:S(2)}, u32[]{:S(2)}) collective-permute-start(bf16[4,128,128]{2,1,0:T(8,128)(2,1)S(1)} %fusion.8), channel_id=1, source_target_pairs={{8,0},{16,8},{24,16},{32,24},{40,32},{48,40},{56,48},{64,56},{72,6... | collective-permute-start | bytes 393224 | tf_op jit(solution)/shard_map/ppermute | solution.py:17
  78.6 0.7 multiply_convert_fusion
  79.3 0.5 convert_element_type.102
  79.9 4.3 %collective-permute-done.1 = bf16[4,128,128]{2,1,0:T(8,128)(2,1)S(1)} collective-permute-done((bf16[4,128,128]{2,1,0:T(8,128)(2,1)S(1)}, bf16[4,128,128]{2,1,0:T(8,128)(2,1)S(1)}, u32[]{:S(2)}, u32[]{:S(2)}) %collective-permute-start.1) | collective-permute-done | bytes 131104 | tf_op jit(solution)/shard_map/ppermute | solution.py:17
  84.2 0.4 fusion.131
  84.6 15.0 %all_to_all.34 = f32[16,16,128]{2,1,0:T(8,128)S(1)} all-to-all(f32[16,16,128]{2,1,0:T(8,128)S(1)} %fusion.131), channel_id=1, replica_groups=mesh['ma'=16,'band'=8] {'ma'}, dimensions={0} | all-to-all | bytes 262144 | tf_op jit(solution)/shard_map/all_to_all | solution.py:120
  99.6 0.9 fusion.18
  (27 shorter events, 1.1 us)
Async XLA Ops:
  3.5 27.8 %all-to-all-start = ((s32[16,1,16]{2,1,0:T(1,128)}), s32[16,1,16]{2,1,0:T(1,128)S(1)}, u32[]{:S(2)}, u32[]{:S(2)}) async-start(s32[16,1,16]{2,1,0:T(1,128)} %bitcast.4), calls=%async_computation | async-start | bytes 16384 | tf_op jit(solution)/shard_map/all_to_all | solution.py:104
  17.9 7.1 %copy-start = (bf16[1,8192,256]{1,2,0:T(8,128)(2,1)S(1)}, bf16[1,8192,256]{1,2,0:T(8,128)(2,1)}, u32[]{:S(2)}) copy-start(bf16[1,8192,256]{1,2,0:T(8,128)(2,1)} %copy.40) | copy-start | bytes 12582916
  17.9 10.6 %copy-start.2 = (bf16[1,2,8192,512]{3,2,1,0:T(8,128)(2,1)S(1)}, bf16[1,2,8192,512]{3,2,1,0:T(8,128)(2,1)}, u32[]{:S(2)}) copy-start(bf16[1,2,8192,512]{3,2,1,0:T(8,128)(2,1)} %param.8) | copy-start | bytes 50331652
  28.5 2.3 %copy-start.1 = (s32[128]{0:T(128)S(1)}, s32[128]{0:T(128)}, u32[]{:S(2)}) copy-start(s32[128]{0:T(128)} %param.9) | copy-start | bytes 1540
  31.4 14.8 %all-to-all-start.2 = ((s32[16,1,16]{2,1,0:T(1,128)}), s32[16,1,16]{2,1,0:T(1,128)S(1)}, u32[]{:S(2)}, u32[]{:S(2)}) async-start(s32[16,1,16]{2,1,0:T(1,128)} %bitcast.7), calls=%async_computation.2 | async-start | bytes 16384 | tf_op jit(solution)/shard_map/all_to_all | solution.py:105
  46.2 11.0 %all-to-all-start.1 = ((f32[16,16,2]{1,2,0:T(2,128)}), f32[16,16,2]{1,2,0:T(2,128)S(1)}, u32[]{:S(2)}, u32[]{:S(2)}) async-start(f32[16,16,2]{1,2,0:T(2,128)} %copy.35), calls=%async_computation.1 | async-start | bytes 32768 | tf_op jit(solution)/shard_map/all_to_all | solution.py:106
  57.2 17.2 %all-to-all-start.3 = ((bf16[1,512,2,128]{3,2,0,1:T(2,128)(2,1)}), bf16[1,512,2,128]{3,2,0,1:T(2,128)(2,1)S(1)}, u32[]{:S(2)}, u32[]{:S(2)}) async-start(bf16[1,512,2,128]{3,2,0,1:T(2,128)(2,1)} %copy.41), calls=%async_computation.3 | async-start | bytes 524288 | tf_op jit(solution)/shard_map/all_to_all | solution.py:75
  74.6 5.3 %collective-permute-start = (bf16[4,128,128]{2,1,0:T(8,128)(2,1)S(1)}, bf16[4,128,128]{2,1,0:T(8,128)(2,1)S(1)}, u32[]{:S(2)}, u32[]{:S(2)}) collective-permute-start(bf16[4,128,128]{2,1,0:T(8,128)(2,1)S(1)} %fusion.8), channel_id=1, source_target_pairs={{0,8},{8,16},{16,24},{24,32},{32,40},{40,48},{48,56},{56,64},{64,7... | collective-permute-start | bytes 393224 | tf_op jit(solution)/shard_map/ppermute | solution.py:16
  77.3 6.9 %collective-permute-start.1 = (bf16[4,128,128]{2,1,0:T(8,128)(2,1)S(1)}, bf16[4,128,128]{2,1,0:T(8,128)(2,1)S(1)}, u32[]{:S(2)}, u32[]{:S(2)}) collective-permute-start(bf16[4,128,128]{2,1,0:T(8,128)(2,1)S(1)} %fusion.8), channel_id=1, source_target_pairs={{8,0},{16,8},{24,16},{32,24},{40,32},{48,40},{56,48},{64,56},{72,6... | collective-permute-start | bytes 393224 | tf_op jit(solution)/shard_map/ppermute | solution.py:17
where the time goes:
time: 101 us
  starting transfers between devices  29.2 us (29%)
  waiting for transfers between devices  26.5 us (26%)
  blocking collectives  15 us (15%)
  local copies, waits for them, and re-layouts  13.3 us (13%)
  matrix products  11 us (11%)
  other arithmetic  5.22 us (5%)
    all_to_all x1, blocking collectives, on_device(): lax.all_to_all(values, 'ma', split_axis=0, concat_axis=0, tiled=True)  15 us
    unnamed x7, local copies, waits for them, and re-layouts  9.96 us
    all_to_all x1, waiting for transfers between devices, on_device(): lax.all_to_all(spectra[None], ('ma', 'band'), split_axis=1, concat_axis=0...  8.95 us
    all_to_all x1, starting transfers between devices, on_device(): lax.all_to_all(cycle_buffer, 'ma', split_axis=0, concat_axis=0, tiled=True)  7.99 us
    all_to_all x1, starting transfers between devices, on_device(): lax.all_to_all(phi_buffer, 'ma', split_axis=0, concat_axis=0, tiled=True)  7.22 us
    all_to_all x1, waiting for transfers between devices, on_device(): lax.all_to_all(offset_buffer, 'ma', split_axis=0, concat_axis=0, tiled=True)  7.19 us
    dot_general x1, matrix products, on_device(): lax.dot_general(legendre[0, 1], harmonics[0], contract, preferred_element...  7.04 us
    all_to_all x1, starting transfers between devices, on_device(): lax.all_to_all(spectra[None], ('ma', 'band'), split_axis=1, concat_axis=0...  6.44 us
  transfers between devices with their start and end apart: 6, of which 4 were waited for; matrix products, arithmetic and copies ran while one was open for 21% of the time, Pallas kernels for 0%

commit v1 on v0

v1 whole, which is shorter than its diff:
```python
import jax
import jax.numpy as jnp
from jax import lax
from jax.sharding import PartitionSpec as P

NPHI = 128
TAPS = 8


def kernel_taps(shifts):
    return jnp.sinc(shifts) * jnp.sinc(shifts / 4.0)


def combine_parts(plus_part, minus_part):
    q_real = -(plus_part[:, 0, 0] - minus_part[:, 1, 1])
    q_imag = -(plus_part[:, 0, 1] + minus_part[:, 1, 0])
    u_real = -(plus_part[:, 1, 0] + minus_part[:, 0, 1])
    u_imag = -(plus_part[:, 1, 1] - minus_part[:, 0, 0])
    real_part = jnp.concatenate([q_real, u_real], axis=1)
    imag_part = jnp.concatenate([q_imag, u_imag], axis=1)
    return jnp.stack([real_part, imag_part], axis=1).astype(jnp.bfloat16)


def phase_table(m_values, cell_count, lmax_width):
    pixel_index = jnp.arange(cell_count, dtype=jnp.int32)
    period = 2 * lmax_width
    phase_turns = m_values[None, :] * pixel_index[:, None] % period
    angles = phase_turns.astype(jnp.float32) * (2.0 * jnp.pi / period)
    return jnp.stack([jnp.cos(angles), -jnp.sin(angles)], axis=-1).astype(jnp.bfloat16)


def spread_weights(starts, weights, length):
    tap_index = jnp.arange(TAPS, dtype=jnp.int32)
    target = starts[:, None] + tap_index[None, :]
    cells = jnp.arange(length, dtype=jnp.int32)
    hits = (target[:, :, None] == cells[None, None, :]).astype(jnp.float32)
    return jnp.sum(weights[:, :, None] * hits, axis=1)


def on_device(harmonics, legendre, m_values, cycle_cell, phi_cell, offsets):
    evolutions = harmonics.shape[2] // 4
    cycle_total = legendre.shape[3]
    owner_count = lax.axis_size("ma")
    band_count = lax.axis_size("band")
    cycle_depth = cycle_total // (owner_count * band_count)
    band_rows = owner_count * cycle_depth

    both = lax.dot_general(
        legendre[0], harmonics[0], (((1,), (0,)), ((), ())), preferred_element_type=jnp.float32
    )
    spectra = combine_parts(
        both[0].reshape(cycle_total, 2, 2, evolutions),
        both[1].reshape(cycle_total, 2, 2, evolutions),
    )
    width_out = spectra.shape[2]
    by_band = spectra.reshape(owner_count, band_count, cycle_depth, 2, width_out)
    by_band = by_band.transpose(1, 3, 0, 2, 4).reshape(band_count, 2, band_rows, width_out)
    send = jnp.broadcast_to(by_band[None], (owner_count,) + by_band.shape)
    send = send.reshape(owner_count * band_count, 2, band_rows, width_out)
    received = lax.all_to_all(send, ("ma", "band"), split_axis=0, concat_axis=0, tiled=True)

    phase_rows = phase_table(m_values, NPHI, harmonics.shape[1])
    blocks = received.shape[0]
    field = jnp.dot(
        phase_rows.reshape(NPHI, blocks * 2),
        received.reshape(blocks * 2, band_rows * width_out),
        preferred_element_type=jnp.float32,
    )
    field = (2.0 * field).astype(jnp.bfloat16)

    tap_shift = jnp.arange(TAPS).astype(jnp.float32) - 3.0
    across = kernel_taps(tap_shift[None, :] - offsets[0][:, None])
    beside_all = kernel_taps(tap_shift[None, :] - offsets[1][:, None])
    cycle_weights = spread_weights(cycle_cell - 3, across, band_rows)
    phi_weights = spread_weights(phi_cell - 3, beside_all, NPHI)
    dense = (phi_weights[:, :, None] * cycle_weights[:, None, :]).astype(jnp.bfloat16)
    points = dense.shape[0]
    return jnp.dot(
        dense.reshape(points, NPHI * band_rows),
        field.reshape(NPHI * band_rows, width_out),
        preferred_element_type=jnp.float32,
    )


def solution(mesh):
    in_specs = (
        P(("ma", "band"), None, None),
        P(("ma", "band"), None, None, None),
        P(),
        P(("ma", "band")),
        P(("ma", "band")),
        P(None, ("ma", "band")),
    )
    out_specs = P(("ma", "band"), None)
    return jax.shard_map(
        on_device, mesh=mesh, in_specs=in_specs, out_specs=out_specs, check_vma=False
    )
```

time: 101 us -> 89.9 us (0.89)
  waiting for transfers between devices: 26.5 us -> 49.3 us
  starting transfers between devices: 29.2 us -> 11.7 us
  blocking collectives: 15 us -> 0 us
  matrix products: 11 us -> 17.9 us
  local copies, waits for them, and re-layouts: 13.3 us -> 6.96 us
  other arithmetic: 5.22 us -> 3.35 us
    all_to_all x4 -> x1, waiting for transfers between devices: 22.2 us -> 49.3 us  [on_device(): lax.all_to_all(send, ('ma', 'band'), split_axis=0, concat_axis=0, tiled=T...]
    all_to_all x1 -> x0, blocking collectives: 15 us -> none  [on_device(): lax.all_to_all(values, 'ma', split_axis=0, concat_axis=0, tiled=True)]
    all_to_all x4 -> x1, starting transfers between devices: 25.1 us -> 11.7 us  [on_device(): lax.all_to_all(send, ('ma', 'band'), split_axis=0, concat_axis=0, tiled=T...]
    unnamed x7 -> x16, local copies, waits for them, and re-layouts: 9.96 us -> 1.02 us
    dot_general x6 -> x3, matrix products: 11 us -> 17.9 us  [the longest x1 9.39 us: on_device(): lax.dot_general(legendre[0], harmonics[0], (((1,), (0,)), ((), ())), pref...]
    ppermute x2 -> x0, waiting for transfers between devices: 4.31 us -> none  [the longest x1 4.31 us: with_halo(): after = lax.ppermute(first, axis, down)]
    ppermute x2 -> x0, starting transfers between devices: 4.02 us -> none  [the longest x1 2.72 us: with_halo(): before = lax.ppermute(last, axis, up)]
    broadcast_in_dim x0 -> x2, local copies, waits for them, and re-layouts: none -> 3.08 us  [on_device(): send = jnp.broadcast_to(by_band[None], (owner_count,) + by_band.shape)]
  transfers between devices with their start and end apart: 6 -> 1, of which waited for: 4 -> 1; matrix products, arithmetic and copies ran while one was open for 21% -> 4% of each run, Pallas kernels for 0% -> 0%
where the time goes in v1:
time: 89.9 us; the launch traced here: 89.5 us
  waiting for transfers between devices  49.3 us (55%)
  matrix products  17.9 us (20%)
  starting transfers between devices  11.7 us (13%)
  local copies, waits for them, and re-layouts  6.96 us (8%)
  other arithmetic  3.35 us (4%)
    all_to_all x1, waiting for transfers between devices, on_device(): lax.all_to_all(send, ('ma', 'band'), split_axis=0, concat_axis=0, tiled=T...  49.3 us
    all_to_all x1, starting transfers between devices, on_device(): lax.all_to_all(send, ('ma', 'band'), split_axis=0, concat_axis=0, tiled=T...  11.7 us
    dot_general x1, matrix products, on_device(): lax.dot_general(legendre[0], harmonics[0], (((1,), (0,)), ((), ())), pref...  9.39 us
    dot_general x1, matrix products, on_device(): jnp.dot(phase_rows.reshape(NPHI, blocks * 2), received.reshape(blocks * 2...  4.96 us
    dot_general x1, matrix products, on_device(): jnp.dot(dense.reshape(points, NPHI * band_rows), field.reshape(NPHI * ban...  3.6 us
    broadcast_in_dim x2, local copies, waits for them, and re-layouts, on_device(): send = jnp.broadcast_to(by_band[None], (owner_count,) + by_band.shape)  3.08 us
    reshape x1, local copies, waits for them, and re-layouts, on_device(): field.reshape(NPHI * band_rows, width_out)  2.36 us
    convert_element_type x1, other arithmetic, on_device(): (phi_weights[:, :, None] * cycle_weights[:, None, :]).astype(jnp.bfloat16)  1.98 us
  transfers between devices with their start and end apart: 1, of which 1 were waited for; matrix products, arithmetic and copies ran while one was open for 4% of the time, Pallas kernels for 0%

profile of v1, /device:TPU:0, one launch (start us, length us, event | category | flops | bytes accessed | tf_op | source)
XLA Modules:
  0.0 89.5 jit_solution(4753597615785722256)
XLA Ops:
  0.0 9.4 %fusion = f32[2,512,256]{1,2,0:T(8,128)S(1)} fusion(bf16[1,2,8192,512]{3,2,1,0:T(8,128)(2,1)} %param.8, bf16[1,8192,256]{2,1,0:T(8,128)(2,1)} %param.7), kind=kOutput, calls=%fused_computation | convolution fusion | flops 4294967296 | bytes 22020096 | tf_op jit(solution)/shard_map/dot_general | solution.py:48
  9.4 0.1 fusion.98
  9.5 0.1 copy.50
  9.7 0.1 copy.51
  9.8 0.1 copy.52
  10.0 0.1 copy.53
  10.1 0.1 copy.54
  10.2 0.1 copy.55
  10.4 0.1 copy.48
  10.5 0.1 copy.49
  10.8 0.4 maximum_bitcast_fusion
  11.3 3.0 %broadcast_in_dim.8 = bf16[16,8,2,64,128]{4,3,2,1,0:T(8,128)(2,1)} broadcast(bf16[8,2,64,128]{3,2,1,0:T(8,128)(2,1)S(1)} %copy.45), dimensions={1,2,3,4} | broadcast | bytes 4456448 | tf_op jit(solution)/shard_map/broadcast_in_dim | solution.py:58
  14.3 0.0 copy-start.1
  14.3 0.0 copy-start
  14.3 0.0 copy-start.2
  14.3 11.7 %all-to-all-start = ((bf16[128,2,64,128]{3,2,1,0:T(8,128)(2,1)}), bf16[128,2,64,128]{3,2,1,0:T(8,128)(2,1)}, u32[]{:S(2)}, u32[]{:S(2)}) async-start(bf16[128,2,64,128]{3,2,1,0:T(8,128)(2,1)} %bitcast.32), calls=%async_computation | async-start | bytes 8388608 | tf_op jit(solution)/shard_map/all_to_all | solution.py:60
  26.0 0.0 copy-done.1
  26.0 0.3 cosine_convert_fusion
  26.4 0.1 copy.34
  26.5 0.0 copy-done
  26.5 0.1 fusion.36
  26.6 0.1 copy.32
  26.7 0.0 copy-done.2
  26.7 0.1 iota_add_fusion
  26.8 0.3 select_reduce_fusion
  27.2 0.1 copy.33
  27.3 0.0 copy-done.3
  27.3 2.0 %multiply_convert_fusion = bf16[128,128,64]{0,2,1:T(8,128)(2,1)} fusion(f32[128,64]{0,1:T(8,128)S(1)} %select_reduce_fusion.1, f32[128,128]{0,1:T(8,128)S(1)} %copy.33), kind=kLoop, calls=%fused_computation.7 | loop fusion | flops 2097152 | bytes 2195456 | tf_op jit(solution)/shard_map/convert_element_type | solution.py:76
  29.3 49.3 %all-to-all-done = bf16[128,2,64,128]{3,2,1,0:T(8,128)(2,1)} async-done(((bf16[128,2,64,128]{3,2,1,0:T(8,128)(2,1)}), bf16[128,2,64,128]{3,2,1,0:T(8,128)(2,1)}, u32[]{:S(2)}, u32[]{:S(2)}) %all-to-all-start) | async-done | bytes 4194336 | tf_op jit(solution)/shard_map/all_to_all | solution.py:60
  78.6 5.0 %fusion.2 = bf16[128,8192]{1,0:T(8,128)(2,1)S(1)} fusion(bf16[128,256]{0,1:T(8,128)(2,1)S(1)} %bitcast.41, bf16[32,8,64,128]{3,2,1,0:T(8,128)(2,1)} %bitcast.18), kind=kOutput, calls=%fused_computation.3 | convolution fusion | flops 538968064 | bytes 6356992 | tf_op jit(solution)/shard_map/dot_general | solution.py:64
  83.6 2.4 %reshape.260 = bf16[8192,128]{1,0:T(8,128)(2,1)} reshape(bf16[128,8192]{1,0:T(8,128)(2,1)S(1)} %fusion.2) | data formatting | bytes 4194304 | tf_op jit(solution)/shard_map/reshape | solution.py:80
  85.9 3.6 %fusion.101 = f32[128,128]{1,0:T(8,128)} fusion(bf16[128,8192]{0,1:T(8,128)(2,1)} %bitcast.33, bf16[8192,128]{1,0:T(8,128)(2,1)} %reshape.260), kind=kOutput, calls=%fused_computation.153 | convolution fusion | flops 268435456 | bytes 4259840 | tf_op jit(solution)/shard_map/dot_general | solution.py:78
  (16 shorter events, 0.4 us)
Async XLA Ops:
  14.3 11.7 %copy-start.1 = (s32[128]{0:T(128)S(1)}, s32[128]{0:T(128)}, u32[]{:S(2)}) copy-start(s32[128]{0:T(128)} %param.9) | copy-start | bytes 1540
  14.3 12.2 %copy-start = (f32[2,128]{1,0:T(2,128)S(1)}, f32[2,128]{1,0:T(2,128)}, u32[]{:S(2)}) copy-start(f32[2,128]{1,0:T(2,128)} %param.12) | copy-start | bytes 3076
  14.3 12.4 %copy-start.2 = (s32[128]{0:T(128)S(1)}, s32[128]{0:T(128)}, u32[]{:S(2)}) copy-start(s32[128]{0:T(128)} %param.11) | copy-start | bytes 1540
  14.3 13.0 %copy-start.3 = (s32[128]{0:T(128)S(1)}, s32[128]{0:T(128)}, u32[]{:S(2)}) copy-start(s32[128]{0:T(128)} %param.10) | copy-start | bytes 1540
  14.3 64.3 %all-to-all-start = ((bf16[128,2,64,128]{3,2,1,0:T(8,128)(2,1)}), bf16[128,2,64,128]{3,2,1,0:T(8,128)(2,1)}, u32[]{:S(2)}, u32[]{:S(2)}) async-start(bf16[128,2,64,128]{3,2,1,0:T(8,128)(2,1)} %bitcast.32), calls=%async_computation | async-start | bytes 8388608 | tf_op jit(solution)/shard_map/all_to_all | solution.py:60

commit v2 on v1

--- a/solution.py
+++ b/solution.py
@@ -53,31 +53,30 @@
         both[1].reshape(cycle_total, 2, 2, evolutions),
     )
     width_out = spectra.shape[2]
-    by_band = spectra.reshape(owner_count, band_count, cycle_depth, 2, width_out)
-    by_band = by_band.transpose(1, 3, 0, 2, 4).reshape(band_count, 2, band_rows, width_out)
-    send = jnp.broadcast_to(by_band[None], (owner_count,) + by_band.shape)
-    send = send.reshape(owner_count * band_count, 2, band_rows, width_out)
+    blocks = owner_count * band_count
+    send = spectra.reshape(blocks, cycle_depth, 2, width_out).transpose(0, 2, 1, 3)
     received = lax.all_to_all(send, ("ma", "band"), split_axis=0, concat_axis=0, tiled=True)
 
     phase_rows = phase_table(m_values, NPHI, harmonics.shape[1])
-    blocks = received.shape[0]
-    field = jnp.dot(
+    own = jnp.dot(
         phase_rows.reshape(NPHI, blocks * 2),
-        received.reshape(blocks * 2, band_rows * width_out),
+        received.reshape(blocks * 2, cycle_depth * width_out),
         preferred_element_type=jnp.float32,
     )
-    field = (2.0 * field).astype(jnp.bfloat16)
+    own = (2.0 * own).astype(jnp.bfloat16).reshape(NPHI, cycle_depth, width_out)
+    own = own.transpose(1, 0, 2)
+    field = lax.all_gather(own, "ma", axis=0, tiled=True)
 
     tap_shift = jnp.arange(TAPS).astype(jnp.float32) - 3.0
     across = kernel_taps(tap_shift[None, :] - offsets[0][:, None])
     beside_all = kernel_taps(tap_shift[None, :] - offsets[1][:, None])
     cycle_weights = spread_weights(cycle_cell - 3, across, band_rows)
     phi_weights = spread_weights(phi_cell - 3, beside_all, NPHI)
-    dense = (phi_weights[:, :, None] * cycle_weights[:, None, :]).astype(jnp.bfloat16)
+    dense = (cycle_weights[:, :, None] * phi_weights[:, None, :]).astype(jnp.bfloat16)
     points = dense.shape[0]
     return jnp.dot(
-        dense.reshape(points, NPHI * band_rows),
-        field.reshape(NPHI * band_rows, width_out),
+        dense.reshape(points, band_rows * NPHI),
+        field.reshape(band_rows * NPHI, width_out),
         preferred_element_type=jnp.float32,
     )
 

time: 89.9 us -> 93.2 us (1.037)
  between operations: 0.28 us -> 13.7 us
  matrix products: 17.9 us -> 13.1 us
  local copies, waits for them, and re-layouts: 6.96 us -> 2.87 us
  other arithmetic: 3.35 us -> 1.37 us
  waiting for transfers between devices: 49.3 us -> 50.8 us
    all_gather x0 -> x1, waiting for transfers between devices: none -> 40.5 us  [on_device(): field = lax.all_gather(own, 'ma', axis=0, tiled=True)]
    all_to_all x1, waiting for transfers between devices: 49.3 us -> 10.2 us  [on_device(): lax.all_to_all(send, ('ma', 'band'), split_axis=0, concat_axis=0, tiled=T...]
    dot_general x1, matrix products: 4.96 us -> 0.21 us  [on_device(): jnp.dot(phase_rows.reshape(NPHI, blocks * 2), received.reshape(blocks * 2...]
    broadcast_in_dim x2 -> x0, local copies, waits for them, and re-layouts: 3.08 us -> none  [on_device(): send = jnp.broadcast_to(by_band[None], (owner_count,) + by_band.shape)]
    convert_element_type x1 -> x0, other arithmetic: 1.98 us -> none  [on_device(): (phi_weights[:, :, None] * cycle_weights[:, None, :]).astype(jnp.bfloat16)]
    reshape x1, local copies, waits for them, and re-layouts: 2.36 us -> 0.68 us  [on_device(): own = (2.0 * own).astype(jnp.bfloat16).reshape(NPHI, cycle_depth, width_out)]
  transfers between devices with their start and end apart: 1 -> 2, of which waited for: 1 -> 2; matrix products, arithmetic and copies ran while one was open for 4% -> 1% of each run, Pallas kernels for 0% -> 0%
where the time goes in v2:
time: 93.2 us; the launch traced here: 93 us
  waiting for transfers between devices  50.8 us (55%)
  between operations  13.7 us (15%)
  matrix products  13.1 us (14%)
  starting transfers between devices  11.2 us (12%)
  local copies, waits for them, and re-layouts  2.87 us (3%)
  other arithmetic  1.37 us (1%)
    all_gather x1, waiting for transfers between devices, on_device(): field = lax.all_gather(own, 'ma', axis=0, tiled=True)  40.5 us
    all_to_all x1, starting transfers between devices, on_device(): lax.all_to_all(send, ('ma', 'band'), split_axis=0, concat_axis=0, tiled=T...  11.2 us
    all_to_all x1, waiting for transfers between devices, on_device(): lax.all_to_all(send, ('ma', 'band'), split_axis=0, concat_axis=0, tiled=T...  10.2 us
    dot_general x1, matrix products, on_device(): lax.dot_general(legendre[0], harmonics[0], (((1,), (0,)), ((), ())), pref...  9.38 us
    dot_general x1, matrix products, on_device(): jnp.dot(dense.reshape(points, band_rows * NPHI), field.reshape(band_rows...  3.5 us
  transfers between devices with their start and end apart: 2, of which 2 were waited for; matrix products, arithmetic and copies ran while one was open for 1% of the time, Pallas kernels for 0%

profile of v2, /device:TPU:0, one launch (start us, length us, event | category | flops | bytes accessed | tf_op | source)
XLA Modules:
  0.0 93.0 jit_solution(1957809153927481940)
XLA Ops:
  6.5 9.4 %fusion = f32[2,512,256]{1,2,0:T(8,128)S(1)} fusion(bf16[1,2,8192,512]{3,2,1,0:T(8,128)(2,1)} %param.8, bf16[1,8192,256]{2,1,0:T(8,128)(2,1)} %param.7), kind=kOutput, calls=%fused_computation | convolution fusion | flops 4294967296 | bytes 22020096 | tf_op jit(solution)/shard_map/dot_general | solution.py:48
  15.9 0.1 fusion.103
  16.0 0.1 copy.58
  16.2 0.0 copy-start.1
  16.2 0.0 copy-start
  16.2 0.0 copy-start.2
  16.3 0.0 copy-start.3
  16.3 0.1 copy.59
  16.4 0.1 copy.60
  16.5 0.1 copy.61
  16.7 0.1 copy.62
  16.8 0.1 copy.63
  16.9 0.1 copy.64
  17.1 0.1 copy.65
  17.4 0.4 maximum_bitcast_fusion
  17.7 0.8 copy.54
  18.5 11.2 %all-to-all-start = ((bf16[128,2,4,128]{3,2,1,0:T(4,128)(2,1)}), bf16[128,2,4,128]{3,2,1,0:T(4,128)(2,1)S(1)}, u32[]{:S(2)}, u32[]{:S(2)}) async-start(bf16[128,2,4,128]{3,2,1,0:T(4,128)(2,1)} %copy.54), calls=%async_computation | async-start | bytes 524288 | tf_op jit(solution)/shard_map/all_to_all | solution.py:58
  29.7 0.0 all-gather.2.cloned.1.call-start
  29.8 0.0 copy-done.1
  29.8 0.3 cosine_convert_fusion
  30.1 0.1 copy.44
  30.2 10.2 %all-to-all-done = bf16[128,2,4,128]{3,2,1,0:T(4,128)(2,1)S(1)} async-done(((bf16[128,2,4,128]{3,2,1,0:T(4,128)(2,1)}), bf16[128,2,4,128]{3,2,1,0:T(4,128)(2,1)S(1)}, u32[]{:S(2)}, u32[]{:S(2)}) %all-to-all-start) | async-done | bytes 262176 | tf_op jit(solution)/shard_map/all_to_all | solution.py:58
  40.4 0.2 fusion.7
  40.7 0.7 copy.73
  41.3 0.0 all-gather.2.cloned.1.call-update
  41.4 0.1 fusion.41
  41.5 0.1 copy.43
  41.7 0.0 copy-done.3
  41.7 0.1 iota_add_fusion
  41.8 0.3 select_reduce_fusion
  42.1 40.5 %all-gather.2.cloned.1.call-done = bf16[64,128,128]{2,1,0:T(8,128)(2,1)} async-done(((bf16[4,128,128]{2,1,0:T(8,128)(2,1)}), bf16[64,128,128]{2,1,0:T(8,128)(2,1)}) %all-gather.2.cloned.1.call-update) | async-done | bytes 2097168 | tf_op jit(solution)/shard_map/all_gather | solution.py:68
  82.6 3.5 %fusion.8 = f32[128,128]{1,0:T(8,128)} fusion(bf16[64,128,128]{2,1,0:T(8,128)(2,1)} %all-gather.2.cloned.1.call-done, f32[128,128]{1,0:T(8,128)S(1)} %select_reduce_fusion, f32[128,64]{0,1:T(8,128)S(1)} %select_reduce_fusion.1), kind=kOutput, calls=%fused_computation.10 | convolution fusion | flops 270532608 | bytes 2260992 | tf_op jit(solution)/shard_map/dot_general | solution.py:77
  (15 shorter events, 0.3 us)
Async XLA Ops:
  16.2 13.6 %copy-start.1 = (s32[128]{0:T(128)S(1)}, s32[128]{0:T(128)}, u32[]{:S(2)}) copy-start(s32[128]{0:T(128)} %param.9) | copy-start | bytes 1540
  16.2 25.1 %copy-start = (f32[2,128]{1,0:T(2,128)S(1)}, f32[2,128]{1,0:T(2,128)}, u32[]{:S(2)}) copy-start(f32[2,128]{1,0:T(2,128)} %param.12) | copy-start | bytes 3076
  16.2 25.3 %copy-start.2 = (s32[128]{0:T(128)S(1)}, s32[128]{0:T(128)}, u32[]{:S(2)}) copy-start(s32[128]{0:T(128)} %param.10) | copy-start | bytes 1540
  16.3 25.4 %copy-start.3 = (s32[128]{0:T(128)S(1)}, s32[128]{0:T(128)}, u32[]{:S(2)}) copy-start(s32[128]{0:T(128)} %param.11) | copy-start | bytes 1540
  18.5 21.9 %all-to-all-start = ((bf16[128,2,4,128]{3,2,1,0:T(4,128)(2,1)}), bf16[128,2,4,128]{3,2,1,0:T(4,128)(2,1)S(1)}, u32[]{:S(2)}, u32[]{:S(2)}) async-start(bf16[128,2,4,128]{3,2,1,0:T(4,128)(2,1)} %copy.54), calls=%async_computation | async-start | bytes 524288 | tf_op jit(solution)/shard_map/all_to_all | solution.py:58
  29.7 52.9 %all-gather.2.cloned.1.call-start = ((), (), s32[]{:S(2)}) async-start(), calls=%async_computation.1 | async-start | bytes 2228224 | tf_op jit(solution)/shard_map/all_gather | solution.py:68
Sparse Core Ops, SparseCore 0:
  41.5 41.1 all-gather.1

commit v3 on v1

--- a/solution.py
+++ b/solution.py
@@ -5,6 +5,7 @@
 
 NPHI = 128
 TAPS = 8
+FIELDS = 8
 
 
 def kernel_taps(shifts):
@@ -37,13 +38,24 @@
     return jnp.sum(weights[:, :, None] * hits, axis=1)
 
 
+def split_three(x):
+    hi = lax.reduce_precision(x, exponent_bits=8, mantissa_bits=7)
+    rest = x - hi
+    mid = lax.reduce_precision(rest, exponent_bits=8, mantissa_bits=7)
+    return hi, mid, rest - mid
+
+
 def on_device(harmonics, legendre, m_values, cycle_cell, phi_cell, offsets):
     evolutions = harmonics.shape[2] // 4
     cycle_total = legendre.shape[3]
     owner_count = lax.axis_size("ma")
     band_count = lax.axis_size("band")
-    cycle_depth = cycle_total // (owner_count * band_count)
-    band_rows = owner_count * cycle_depth
+    blocks = owner_count * band_count
+    cycle_depth = cycle_total // blocks
+    window = 3 * cycle_depth
+    capacity = cycle_cell.shape[0] // 8
+    me = lax.axis_index("ma")
+    my_band = lax.axis_index("band")
 
     both = lax.dot_general(
         legendre[0], harmonics[0], (((1,), (0,)), ((), ())), preferred_element_type=jnp.float32
@@ -54,32 +66,69 @@
     )
     width_out = spectra.shape[2]
     by_band = spectra.reshape(owner_count, band_count, cycle_depth, 2, width_out)
-    by_band = by_band.transpose(1, 3, 0, 2, 4).reshape(band_count, 2, band_rows, width_out)
-    send = jnp.broadcast_to(by_band[None], (owner_count,) + by_band.shape)
-    send = send.reshape(owner_count * band_count, 2, band_rows, width_out)
+    by_band = by_band.transpose(1, 0, 2, 3, 4)
+    empty = jnp.zeros((band_count, 1, cycle_depth, 2, width_out), spectra.dtype)
+    padded = jnp.concatenate([empty, by_band, empty], axis=1)
+    windows = jnp.stack(
+        [padded[:, s : s + owner_count] for s in range(3)], axis=2
+    )
+    windows = windows.transpose(1, 0, 4, 2, 3, 5).reshape(blocks, 2 * window * width_out)
+
+    owner_index = cycle_cell // cycle_depth
+    one_hot = (owner_index[:, None] == jnp.arange(owner_count, dtype=jnp.int32)[None, :]).astype(
+        jnp.int32
+    )
+    slot_index = jnp.sum((jnp.cumsum(one_hot, axis=0) - one_hot) * one_hot, axis=1)
+    flat_slot = owner_index * capacity + slot_index
+    placement = (
+        flat_slot[:, None] == jnp.arange(owner_count * capacity, dtype=jnp.int32)[None, :]
+    ).astype(jnp.bfloat16)
+    table = jnp.stack(
+        [cycle_cell.astype(jnp.float32), phi_cell.astype(jnp.float32)]
+        + list(split_three(offsets[0]))
+        + list(split_three(offsets[1])),
+        axis=1,
+    ).astype(jnp.bfloat16)
+    payload = jnp.dot(placement.T, table, preferred_element_type=jnp.float32)
+    payload = payload.astype(jnp.bfloat16).reshape(owner_count, 1, capacity * FIELDS)
+    payload = jnp.broadcast_to(payload, (owner_count, band_count, capacity * FIELDS))
+    send = jnp.concatenate(
+        [windows, payload.reshape(blocks, capacity * FIELDS)], axis=1
+    )
     received = lax.all_to_all(send, ("ma", "band"), split_axis=0, concat_axis=0, tiled=True)
 
+    spectral_part = received[:, : 2 * window * width_out].reshape(blocks * 2, window * width_out)
+    points_in = received[:, 2 * window * width_out :].reshape(
+        owner_count, band_count, capacity, FIELDS
+    )
+    points_in = lax.dynamic_index_in_dim(points_in, my_band, axis=1, keepdims=False)
+    points_in = points_in.reshape(owner_count * capacity, FIELDS).astype(jnp.float32)
+
     phase_rows = phase_table(m_values, NPHI, harmonics.shape[1])
-    blocks = received.shape[0]
-    field = jnp.dot(
-        phase_rows.reshape(NPHI, blocks * 2),
-        received.reshape(blocks * 2, band_rows * width_out),
+    rows = jnp.dot(
+        phase_rows.reshape(NPHI, blocks * 2), spectral_part, preferred_element_type=jnp.float32
+    )
+    rows = (2.0 * rows).astype(jnp.bfloat16)
+
+    cycles_here = points_in[:, 0].astype(jnp.int32)
+    phis_here = points_in[:, 1].astype(jnp.int32)
+    offset_rows = points_in[:, 2] + (points_in[:, 3] + points_in[:, 4])
+    offset_cols = points_in[:, 5] + (points_in[:, 6] + points_in[:, 7])
+    tap_shift = jnp.arange(TAPS).astype(jnp.float32) - 3.0
+    across = kernel_taps(tap_shift[None, :] - offset_rows[:, None])
+    beside_all = kernel_taps(tap_shift[None, :] - offset_cols[:, None])
+    first_row = (me - 1) * cycle_depth
+    cycle_weights = spread_weights(cycles_here - 3 - first_row, across, window)
+    phi_weights = spread_weights(phis_here - 3, beside_all, NPHI)
+    dense = (phi_weights[:, :, None] * cycle_weights[:, None, :]).astype(jnp.bfloat16)
+    values = jnp.dot(
+        dense.reshape(dense.shape[0], NPHI * window),
+        rows.reshape(NPHI * window, width_out),
         preferred_element_type=jnp.float32,
     )
-    field = (2.0 * field).astype(jnp.bfloat16)
-
-    tap_shift = jnp.arange(TAPS).astype(jnp.float32) - 3.0
-    across = kernel_taps(tap_shift[None, :] - offsets[0][:, None])
-    beside_all = kernel_taps(tap_shift[None, :] - offsets[1][:, None])
-    cycle_weights = spread_weights(cycle_cell - 3, across, band_rows)
-    phi_weights = spread_weights(phi_cell - 3, beside_all, NPHI)
-    dense = (phi_weights[:, :, None] * cycle_weights[:, None, :]).astype(jnp.bfloat16)
-    points = dense.shape[0]
-    return jnp.dot(
-        dense.reshape(points, NPHI * band_rows),
-        field.reshape(NPHI * band_rows, width_out),
-        preferred_element_type=jnp.float32,
-    )
+    values = values.reshape(owner_count, capacity, width_out)
+    returned = lax.all_to_all(values, "ma", split_axis=0, concat_axis=0, tiled=True)
+    return jnp.take(returned.reshape(owner_count * capacity, width_out), flat_slot, axis=0)
 
 
 def solution(mesh):

time: 89.9 us -> 75.5 us (0.84)
  waiting for transfers between devices: 49.3 us -> 24.1 us
  local copies, waits for them, and re-layouts: 6.96 us -> 14.4 us
  starting transfers between devices: 11.7 us -> 14.9 us
  other arithmetic: 3.35 us -> 6.26 us
  matrix products: 17.9 us -> 15.1 us
    all_to_all x1, waiting for transfers between devices: 49.3 us -> 16.4 us  [on_device(): lax.all_to_all(send, ('ma', 'band'), split_axis=0, concat_axis=0, tiled=T...]
    all_to_all x0 -> x1, waiting for transfers between devices: none -> 7.75 us  [on_device(): lax.all_to_all(values, 'ma', split_axis=0, concat_axis=0, tiled=True)]
    convert_element_type x0 -> x2, local copies, waits for them, and re-layouts: none -> 5.71 us  [the longest x1 5.59 us: on_device(): (phi_weights[:, :, None] * cycle_weights[:, None, :]).astype(jnp.bfloat16)]
    unnamed x16 -> x27, local copies, waits for them, and re-layouts: 1.02 us -> 4.79 us
    all_to_all x0 -> x1, starting transfers between devices: none -> 3.51 us  [on_device(): lax.all_to_all(values, 'ma', split_axis=0, concat_axis=0, tiled=True)]
    broadcast_in_dim x2 -> x1, local copies, waits for them, and re-layouts: 3.08 us -> 0.13 us  [on_device(): jnp.broadcast_to(payload, (owner_count, band_count, capacity * FIELDS))]
    dot_general x2 -> x3, matrix products: 8.56 us -> 5.73 us  [the longest x1 5.24 us: on_device(): jnp.dot(dense.reshape(dense.shape[0], NPHI * window), rows.reshape(NPHI *...]
    convert_element_type x1, other arithmetic: 1.98 us -> 0.34 us  [on_device(): (phi_weights[:, :, None] * cycle_weights[:, None, :]).astype(jnp.bfloat16)]
  transfers between devices with their start and end apart: 1 -> 2, of which waited for: 1 -> 2; matrix products, arithmetic and copies ran while one was open for 4% -> 1% of each run, Pallas kernels for 0% -> 0%
where the time goes in v3:
time: 75.5 us; the launch traced here: 75.3 us
  waiting for transfers between devices  24.1 us (32%)
  matrix products  15.1 us (20%)
  starting transfers between devices  14.9 us (20%)
  local copies, waits for them, and re-layouts  14.4 us (19%)
  other arithmetic  6.26 us (8%)
    all_to_all x1, waiting for transfers between devices, on_device(): lax.all_to_all(send, ('ma', 'band'), split_axis=0, concat_axis=0, tiled=T...  16.4 us
    all_to_all x1, starting transfers between devices, on_device(): lax.all_to_all(send, ('ma', 'band'), split_axis=0, concat_axis=0, tiled=T...  11.4 us
    dot_general x1, matrix products, on_device(): lax.dot_general(legendre[0], harmonics[0], (((1,), (0,)), ((), ())), pref...  9.39 us
    all_to_all x1, waiting for transfers between devices, on_device(): lax.all_to_all(values, 'ma', split_axis=0, concat_axis=0, tiled=True)  7.75 us
    convert_element_type x1, local copies, waits for them, and re-layouts, on_device(): (phi_weights[:, :, None] * cycle_weights[:, None, :]).astype(jnp.bfloat16)  5.59 us
    dot_general x1, matrix products, on_device(): jnp.dot(dense.reshape(dense.shape[0], NPHI * window), rows.reshape(NPHI *...  5.24 us
    unnamed x27, local copies, waits for them, and re-layouts  4.79 us
    all_to_all x1, starting transfers between devices, on_device(): lax.all_to_all(values, 'ma', split_axis=0, concat_axis=0, tiled=True)  3.51 us
  transfers between devices with their start and end apart: 2, of which 2 were waited for; matrix products, arithmetic and copies ran while one was open for 1% of the time, Pallas kernels for 0%

profile of v3, /device:TPU:0, one launch (start us, length us, event | category | flops | bytes accessed | tf_op | source)
XLA Modules:
  0.0 75.3 jit_solution(9651387520931384440)
XLA Ops:
  0.0 9.4 %fusion = f32[2,512,256]{1,2,0:T(8,128)S(1)} fusion(bf16[1,2,8192,512]{3,2,1,0:T(8,128)(2,1)} %param.8, bf16[1,8192,256]{2,1,0:T(8,128)(2,1)} %param.7), kind=kOutput, calls=%fused_computation.1 | convolution fusion | flops 4294967296 | bytes 22020096 | tf_op jit(solution)/shard_map/dot_general | solution.py:60
  9.9 0.1 copy.124
  10.3 0.1 copy.123
  10.8 0.4 fusion.113
  11.2 0.4 fusion.112
  11.7 0.2 reduce_window_sum.11
  11.9 0.2 select_reduce_fusion.2
  12.1 0.2 convolution_convert_fusion
  12.5 0.1 broadcast_in_dim.17
  12.6 0.2 fusion.6
  12.8 0.7 maximum_bitcast_fusion.1
  13.5 0.2 copy.102
  13.7 0.5 broadcast.239
  14.2 1.2 %reduce = bf16[128,3200]{1,0:T(8,128)(2,1)S(1)} reduce(bf16[128,1,3200]{2,0,1:T(8,128)(2,1)S(1)} %maximum_bitcast_fusion, bf16[]{:T(256)} %broadcast.239), dimensions={1}, to_apply=%copy.104.reduce_sub_computation | reduce | bytes 1638402 | tf_op jit(solution)/shard_map/all_to_all | solution.py:98
  15.4 1.8 %reshape.376 = bf16[128,2,1600]{2,1,0:T(2,128)(2,1)} reshape(bf16[128,3200]{1,0:T(8,128)(2,1)S(1)} %reduce) | data formatting | bytes 1638400
  17.3 11.4 %all-to-all-start = ((bf16[128,2,1600]{2,1,0:T(2,128)(2,1)}), bf16[128,2,1600]{2,1,0:T(2,128)(2,1)S(1)}, u32[]{:S(2)}, u32[]{:S(2)}) async-start(bf16[128,2,1600]{2,1,0:T(2,128)(2,1)} %reshape.376), calls=%async_computation | async-start | bytes 1703936 | tf_op jit(solution)/shard_map/all_to_all | solution.py:98
  28.6 0.3 cosine_convert_fusion
  29.1 16.4 %all-to-all-done = bf16[128,2,1600]{2,1,0:T(2,128)(2,1)S(1)} async-done(((bf16[128,2,1600]{2,1,0:T(2,128)(2,1)}), bf16[128,2,1600]{2,1,0:T(2,128)(2,1)S(1)}, u32[]{:S(2)}, u32[]{:S(2)}) %all-to-all-start) | async-done | bytes 819232 | tf_op jit(solution)/shard_map/all_to_all | solution.py:98
  45.5 1.2 %reshape.377 = bf16[128,1,3200]{2,1,0:T(2,128)(2,1)S(1)} reshape(bf16[128,2,1600]{2,1,0:T(2,128)(2,1)S(1)} %all-to-all-done) | data formatting | bytes 1638400
  46.9 0.3 reshape.360
  47.1 0.3 fusion.5
  47.4 0.5 reshape.374
  47.9 0.6 reshape.359
  48.6 0.3 fusion.107
  50.0 1.3 %select_reduce_fusion = f32[256,128]{1,0:T(8,128)S(1)} fusion(f32[256,8]{1,0:T(8,128)S(1)} %copy.109, s32[256,8]{1,0:T(8,128)S(1)} %iota_add_fusion), kind=kLoop, calls=%fused_computation.10 | loop fusion | flops 753664 | bytes 147456 | tf_op jit(solution)/shard_map/reduce_sum | solution.py:38
  51.4 0.3 multiply_convert_fusion
  51.8 5.6 %convert_element_type.96 = bf16[16,16,1536]{1,0,2:T(8,128)(2,1)} reshape(bf16[256,128,12]{0,2,1:T(8,128)(2,1)S(1)} %multiply_convert_fusion) | data formatting | bytes 1572864 | tf_op jit(solution)/shard_map/convert_element_type | solution.py:123
  57.4 5.2 %fusion.2 = f32[16,16,128]{2,1,0:T(8,128)} fusion(bf16[1536,128,1]{1,0,2:T(8,128)(2,1)S(1)} %reshape.374, bf16[16,16,1536]{1,0,2:T(8,128)(2,1)} %convert_element_type.96), kind=kOutput, calls=%fused_computation.3 | convolution fusion | flops 100663296 | bytes 1310720 | tf_op jit(solution)/shard_map/dot_general | solution.py:124
  62.6 3.5 %all-to-all-start.1 = ((f32[16,16,128]{2,1,0:T(8,128)}), f32[16,16,128]{2,1,0:T(8,128)S(1)}, u32[]{:S(2)}, u32[]{:S(2)}) async-start(f32[16,16,128]{2,1,0:T(8,128)} %fusion.2), calls=%async_computation.1 | async-start | bytes 262144 | tf_op jit(solution)/shard_map/all_to_all | solution.py:130
  66.1 7.8 %all-to-all-done.1 = f32[16,16,128]{2,1,0:T(8,128)S(1)} async-done(((f32[16,16,128]{2,1,0:T(8,128)}), f32[16,16,128]{2,1,0:T(8,128)S(1)}, u32[]{:S(2)}, u32[]{:S(2)}) %all-to-all-start.1) | async-done | bytes 131104 | tf_op jit(solution)/shard_map/all_to_all | solution.py:130
  73.9 0.6 gather_fusion
  74.5 0.7 broadcast_select_fusion
  (57 shorter events, 3.0 us)
Async XLA Ops:
  9.5 2.1 %copy-start.2 = (s32[128]{0:T(128)S(1)}, s32[128]{0:T(128)}, u32[]{:S(2)}) copy-start(s32[128]{0:T(128)} %param.10) | copy-start | bytes 1540
  9.5 2.1 %copy-start.3 = (s32[128]{0:T(128)S(1)}, s32[128]{0:T(128)}, u32[]{:S(2)}) copy-start(s32[128]{0:T(128)} %param.11) | copy-start | bytes 1540
  9.5 2.1 %copy-start = (f32[2,128]{1,0:T(2,128)S(1)}, f32[2,128]{1,0:T(2,128)}, u32[]{:S(2)}) copy-start(f32[2,128]{1,0:T(2,128)} %param.12) | copy-start | bytes 3076
  13.4 15.2 %copy-start.1 = (s32[128]{0:T(128)S(1)}, s32[128]{0:T(128)}, u32[]{:S(2)}) copy-start(s32[128]{0:T(128)} %param.9) | copy-start | bytes 1540
  17.3 28.2 %all-to-all-start = ((bf16[128,2,1600]{2,1,0:T(2,128)(2,1)}), bf16[128,2,1600]{2,1,0:T(2,128)(2,1)S(1)}, u32[]{:S(2)}, u32[]{:S(2)}) async-start(bf16[128,2,1600]{2,1,0:T(2,128)(2,1)} %reshape.376), calls=%async_computation | async-start | bytes 1703936 | tf_op jit(solution)/shard_map/all_to_all | solution.py:98
  62.6 11.3 %all-to-all-start.1 = ((f32[16,16,128]{2,1,0:T(8,128)}), f32[16,16,128]{2,1,0:T(8,128)S(1)}, u32[]{:S(2)}, u32[]{:S(2)}) async-start(f32[16,16,128]{2,1,0:T(8,128)} %fusion.2), calls=%async_computation.1 | async-start | bytes 262144 | tf_op jit(solution)/shard_map/all_to_all | solution.py:130

commit v4 on v3

--- a/solution.py
+++ b/solution.py
@@ -72,7 +72,7 @@
     windows = jnp.stack(
         [padded[:, s : s + owner_count] for s in range(3)], axis=2
     )
-    windows = windows.transpose(1, 0, 4, 2, 3, 5).reshape(blocks, 2 * window * width_out)
+    windows = windows.transpose(1, 0, 4, 2, 3, 5).reshape(blocks, 2, window, width_out)
 
     owner_index = cycle_cell // cycle_depth
     one_hot = (owner_index[:, None] == jnp.arange(owner_count, dtype=jnp.int32)[None, :]).astype(
@@ -90,23 +90,20 @@
         axis=1,
     ).astype(jnp.bfloat16)
     payload = jnp.dot(placement.T, table, preferred_element_type=jnp.float32)
-    payload = payload.astype(jnp.bfloat16).reshape(owner_count, 1, capacity * FIELDS)
-    payload = jnp.broadcast_to(payload, (owner_count, band_count, capacity * FIELDS))
-    send = jnp.concatenate(
-        [windows, payload.reshape(blocks, capacity * FIELDS)], axis=1
-    )
+    payload = payload.astype(jnp.bfloat16).reshape(owner_count, 1, 1, 1, capacity * FIELDS)
+    payload = jnp.broadcast_to(payload, (owner_count, band_count, 1, 1, capacity * FIELDS))
+    payload = payload.reshape(blocks, 1, 1, capacity * FIELDS)
+    payload = jnp.concatenate([payload, jnp.zeros_like(payload)], axis=1)
+    send = jnp.concatenate([windows, payload], axis=2)
     received = lax.all_to_all(send, ("ma", "band"), split_axis=0, concat_axis=0, tiled=True)
 
-    spectral_part = received[:, : 2 * window * width_out].reshape(blocks * 2, window * width_out)
-    points_in = received[:, 2 * window * width_out :].reshape(
-        owner_count, band_count, capacity, FIELDS
-    )
+    points_in = received[:, 0, window].reshape(owner_count, band_count, capacity, FIELDS)
     points_in = lax.dynamic_index_in_dim(points_in, my_band, axis=1, keepdims=False)
     points_in = points_in.reshape(owner_count * capacity, FIELDS).astype(jnp.float32)
 
     phase_rows = phase_table(m_values, NPHI, harmonics.shape[1])
-    rows = jnp.dot(
-        phase_rows.reshape(NPHI, blocks * 2), spectral_part, preferred_element_type=jnp.float32
+    rows = jnp.einsum(
+        "kgi,gitc->tkc", phase_rows, received[:, :, :window], preferred_element_type=jnp.float32
     )
     rows = (2.0 * rows).astype(jnp.bfloat16)
 
@@ -120,10 +117,10 @@
     first_row = (me - 1) * cycle_depth
     cycle_weights = spread_weights(cycles_here - 3 - first_row, across, window)
     phi_weights = spread_weights(phis_here - 3, beside_all, NPHI)
-    dense = (phi_weights[:, :, None] * cycle_weights[:, None, :]).astype(jnp.bfloat16)
+    dense = (cycle_weights[:, :, None] * phi_weights[:, None, :]).astype(jnp.bfloat16)
     values = jnp.dot(
-        dense.reshape(dense.shape[0], NPHI * window),
-        rows.reshape(NPHI * window, width_out),
+        dense.reshape(dense.shape[0], window * NPHI),
+        rows.reshape(window * NPHI, width_out),
         preferred_element_type=jnp.float32,
     )
     values = values.reshape(owner_count, capacity, width_out)

time: 75.5 us -> 63.5 us (0.84)
  local copies, waits for them, and re-layouts: 14.4 us -> 7.28 us
  matrix products: 15.1 us -> 10.9 us
  other arithmetic: 6.26 us -> 5.45 us
    convert_element_type x2, local copies, waits for them, and re-layouts: 5.71 us -> 0.65 us  [the longest x1 0.52 us: on_device(): (cycle_weights[:, :, None] * phi_weights[:, None, :]).astype(jnp.bfloat16)]
    dot_general x2, matrix products: 5.53 us -> 1.29 us  [the longest x1 1.02 us: on_device(): jnp.dot(dense.reshape(dense.shape[0], window * NPHI), rows.reshape(window...]
    unnamed x27 -> x24, local copies, waits for them, and re-layouts: 4.79 us -> 1.7 us
    concatenate x0 -> x1, local copies, waits for them, and re-layouts: none -> 1.79 us  [on_device(): send = jnp.concatenate([windows, payload], axis=2)]
    reshape x4 -> x0, local copies, waits for them, and re-layouts: 1.34 us -> none  [the longest x1 0.61 us: on_device(): received[:, 2 * window * width_out:]]
    all_to_all x2 -> x0, other arithmetic: 1.24 us -> none  [on_device(): lax.all_to_all(send, ('ma', 'band'), split_axis=0, concat_axis=0, tiled=T...]
  transfers between devices with their start and end apart: 2 -> 2, of which waited for: 2 -> 2; matrix products, arithmetic and copies ran while one was open for 1% -> 0% of each run, Pallas kernels for 0% -> 0%
where the time goes in v4:
time: 63.5 us; the launch traced here: 63.2 us
  waiting for transfers between devices  24.5 us (39%)
  starting transfers between devices  14.7 us (23%)
  matrix products  10.9 us (17%)
  local copies, waits for them, and re-layouts  7.28 us (11%)
  other arithmetic  5.45 us (9%)
    all_to_all x1, waiting for transfers between devices, on_device(): lax.all_to_all(send, ('ma', 'band'), split_axis=0, concat_axis=0, tiled=T...  16.7 us
    all_to_all x1, starting transfers between devices, on_device(): lax.all_to_all(send, ('ma', 'band'), split_axis=0, concat_axis=0, tiled=T...  11.2 us
    dot_general x1, matrix products, on_device(): lax.dot_general(legendre[0], harmonics[0], (((1,), (0,)), ((), ())), pref...  9.39 us
    all_to_all x1, waiting for transfers between devices, on_device(): lax.all_to_all(values, 'ma', split_axis=0, concat_axis=0, tiled=True)  7.75 us
    all_to_all x1, starting transfers between devices, on_device(): lax.all_to_all(values, 'ma', split_axis=0, concat_axis=0, tiled=True)  3.51 us
    concatenate x1, local copies, waits for them, and re-layouts, on_device(): send = jnp.concatenate([windows, payload], axis=2)  1.79 us
    unnamed x24, local copies, waits for them, and re-layouts  1.7 us
    reduce_sum x2, other arithmetic, spread_weights(): return jnp.sum(weights[:, :, None] * hits, axis=1)  1.29 us
  transfers between devices with their start and end apart: 2, of which 2 were waited for; matrix products, arithmetic and copies ran while one was open for 0% of the time, Pallas kernels for 0%

profile of v4, /device:TPU:0, one launch (start us, length us, event | category | flops | bytes accessed | tf_op | source)
XLA Modules:
  0.0 63.2 jit_solution(12942949096036747399)
XLA Ops:
  0.0 9.4 %fusion = f32[2,512,256]{1,2,0:T(8,128)S(1)} fusion(bf16[1,2,8192,512]{3,2,1,0:T(8,128)(2,1)} %param.8, bf16[1,8192,256]{2,1,0:T(8,128)(2,1)} %param.7), kind=kOutput, calls=%fused_computation.1 | convolution fusion | flops 4294967296 | bytes 22020096 | tf_op jit(solution)/shard_map/dot_general | solution.py:60
  9.7 0.1 copy.120
  9.9 0.1 copy.125
  10.0 0.1 copy.123
  10.1 0.1 copy.127
  10.3 0.1 copy.124
  10.8 0.4 fusion.117
  11.2 0.4 fusion.118
  11.7 0.2 reduce_window_sum.11
  11.9 0.2 select_reduce_fusion.2
  12.1 0.2 convolution_convert_fusion
  12.5 0.1 broadcast_in_dim.19
  12.6 0.2 fusion.8
  12.8 0.7 %maximum_bitcast_fusion = bf16[16,8,2,3,4,128]{5,4,1,0,2,3:T(4,128)(2,1)S(1)} fusion(bf16[8,16,1,4,2,128]{5,3,0,1,4,2:T(4,128)(2,1)S(1)} %get-tuple-element.19, bf16[8,16,1,4,2,128]{5,3,0,1,4,2:T(4,128)(2,1)S(1)} %fusion.117, bf16[8,16,1,4,2,128]{5,3,0,1,4,2:T(4,128)(2,1)S(1)} %get-tuple-element.18), kind=kLoop, calls=%fused_computation.14 | loop fusion | flops 786432 | bytes 1572864 | tf_op jit(solution)/shard_map/transpose | solution.py:75
  13.5 0.2 copy.103
  13.7 1.8 %copy.105 = bf16[128,2,13,128]{3,1,2,0:T(2,128)(2,1)} copy(bf16[128,2,13,128]{3,0,2,1:T(8,128)(2,1)S(1)} %fusion.6) | data formatting | bytes 1703936 | tf_op jit(solution)/shard_map/concatenate | solution.py:97
  15.5 11.2 %all-to-all-start = ((bf16[128,2,13,128]{3,1,2,0:T(2,128)(2,1)}), bf16[128,2,13,128]{3,1,2,0:T(2,128)(2,1)S(1)}, u32[]{:S(2)}, u32[]{:S(2)}) async-start(bf16[128,2,13,128]{3,1,2,0:T(2,128)(2,1)} %copy.105), calls=%async_computation | async-start | bytes 1703936 | tf_op jit(solution)/shard_map/all_to_all | solution.py:98
  26.7 0.3 cosine_convert_fusion
  27.0 16.7 %all-to-all-done = bf16[128,2,13,128]{3,1,2,0:T(2,128)(2,1)S(1)} async-done(((bf16[128,2,13,128]{3,1,2,0:T(2,128)(2,1)}), bf16[128,2,13,128]{3,1,2,0:T(2,128)(2,1)S(1)}, u32[]{:S(2)}, u32[]{:S(2)}) %all-to-all-start) | async-done | bytes 852000 | tf_op jit(solution)/shard_map/all_to_all | solution.py:98
  43.7 0.2 slice_reduce_fusion
  43.9 0.6 reshape_squeeze.11
  44.6 0.3 fusion.112
  46.2 1.3 %select_reduce_fusion = f32[256,128]{1,0:T(8,128)S(1)} fusion(f32[256,8]{1,0:T(8,128)S(1)} %copy.115, s32[256,8]{1,0:T(8,128)S(1)} %iota_add_fusion), kind=kLoop, calls=%fused_computation.11 | loop fusion | flops 753664 | bytes 147456 | tf_op jit(solution)/shard_map/reduce_sum | solution.py:38
  47.5 0.7 %multiply_convert_fusion = bf16[256,12,128]{2,1,0:T(8,128)(2,1)S(1)} fusion(f32[256,128]{1,0:T(8,128)S(1)} %select_reduce_fusion, f32[256,12]{1,0:T(8,128)S(1)} %copy.110), kind=kLoop, calls=%fused_computation.4 | loop fusion | flops 786432 | bytes 929792 | tf_op jit(solution)/shard_map/convert_element_type | solution.py:120
  48.2 0.5 convert_element_type.89
  48.7 0.5 slice.119
  49.2 0.3 fusion.5
  49.5 1.0 %fusion.113 = f32[16,16,128]{2,1,0:T(8,128)} fusion(bf16[16,16,1536]{2,1,0:T(8,128)(2,1)S(1)} %convert_element_type.89, bf16[1536,128,1]{1,0,2:T(8,128)(2,1)S(1)} %bitcast.84), kind=kOutput, calls=%fused_computation.197 | convolution fusion | flops 100663296 | bytes 1310720 | tf_op jit(solution)/shard_map/dot_general | solution.py:121
  50.6 3.5 %all-to-all-start.1 = ((f32[16,16,128]{2,1,0:T(8,128)}), f32[16,16,128]{2,1,0:T(8,128)S(1)}, u32[]{:S(2)}, u32[]{:S(2)}) async-start(f32[16,16,128]{2,1,0:T(8,128)} %fusion.113), calls=%async_computation.1 | async-start | bytes 262144 | tf_op jit(solution)/shard_map/all_to_all | solution.py:127
  54.1 7.8 %all-to-all-done.1 = f32[16,16,128]{2,1,0:T(8,128)S(1)} async-done(((f32[16,16,128]{2,1,0:T(8,128)}), f32[16,16,128]{2,1,0:T(8,128)S(1)}, u32[]{:S(2)}, u32[]{:S(2)}) %all-to-all-start.1) | async-done | bytes 131104 | tf_op jit(solution)/shard_map/all_to_all | solution.py:127
  61.8 0.6 %gather_fusion = f32[128,128]{1,0:T(8,128)S(1)} fusion(f32[256,128]{1,0:T(8,128)S(1)} %bitcast.72, s32[1024]{0:T(1024)S(1)} %pad_clamp_fusion), kind=kCustom, calls=%fused_computation | custom fusion | bytes 131584 | tf_op jit(solution)/shard_map/jit(_take)/gather | solution.py:128
  62.5 0.7 %broadcast_select_fusion = f32[128,128]{1,0:T(8,128)} fusion(f32[128,128]{1,0:T(8,128)S(1)} %gather_fusion, pred[128]{0:T(512)(128)(4,1)S(1)} %get-tuple-element.6), kind=kLoop, calls=%fused_computation.51 | loop fusion | flops 16384 | bytes 131200 | tf_op jit(solution)/shard_map/jit(_take)/select_n | solution.py:128
  (49 shorter events, 2.4 us)
Async XLA Ops:
  9.5 2.1 %copy-start.2 = (s32[128]{0:T(128)S(1)}, s32[128]{0:T(128)}, u32[]{:S(2)}) copy-start(s32[128]{0:T(128)} %param.11) | copy-start | bytes 1540
  9.5 2.1 %copy-start.3 = (s32[128]{0:T(128)S(1)}, s32[128]{0:T(128)}, u32[]{:S(2)}) copy-start(s32[128]{0:T(128)} %param.10) | copy-start | bytes 1540
  9.5 2.1 %copy-start = (f32[2,128]{1,0:T(2,128)S(1)}, f32[2,128]{1,0:T(2,128)}, u32[]{:S(2)}) copy-start(f32[2,128]{1,0:T(2,128)} %param.12) | copy-start | bytes 3076
  12.8 13.9 %copy-start.1 = (s32[128]{0:T(128)S(1)}, s32[128]{0:T(128)}, u32[]{:S(2)}) copy-start(s32[128]{0:T(128)} %param.9) | copy-start | bytes 1540
  15.5 28.2 %all-to-all-start = ((bf16[128,2,13,128]{3,1,2,0:T(2,128)(2,1)}), bf16[128,2,13,128]{3,1,2,0:T(2,128)(2,1)S(1)}, u32[]{:S(2)}, u32[]{:S(2)}) async-start(bf16[128,2,13,128]{3,1,2,0:T(2,128)(2,1)} %copy.105), calls=%async_computation | async-start | bytes 1703936 | tf_op jit(solution)/shard_map/all_to_all | solution.py:98
  50.6 11.3 %all-to-all-start.1 = ((f32[16,16,128]{2,1,0:T(8,128)}), f32[16,16,128]{2,1,0:T(8,128)S(1)}, u32[]{:S(2)}, u32[]{:S(2)}) async-start(f32[16,16,128]{2,1,0:T(8,128)} %fusion.113), calls=%async_computation.1 | async-start | bytes 262144 | tf_op jit(solution)/shard_map/all_to_all | solution.py:127

commit v5 on v4

--- a/solution.py
+++ b/solution.py
@@ -95,7 +95,10 @@
     payload = payload.reshape(blocks, 1, 1, capacity * FIELDS)
     payload = jnp.concatenate([payload, jnp.zeros_like(payload)], axis=1)
     send = jnp.concatenate([windows, payload], axis=2)
-    received = lax.all_to_all(send, ("ma", "band"), split_axis=0, concat_axis=0, tiled=True)
+    send = send.reshape((owner_count, band_count) + send.shape[1:])
+    staged = lax.all_to_all(send, "band", split_axis=1, concat_axis=1, tiled=True)
+    received = lax.all_to_all(staged, "ma", split_axis=0, concat_axis=0, tiled=True)
+    received = received.reshape((blocks,) + received.shape[2:])
 
     points_in = received[:, 0, window].reshape(owner_count, band_count, capacity, FIELDS)
     points_in = lax.dynamic_index_in_dim(points_in, my_band, axis=1, keepdims=False)

time: 63.5 us -> 75.8 us (1.19)
  blocking collectives: 0 us -> 18.2 us
  starting transfers between devices: 14.7 us -> 11.4 us
  waiting for transfers between devices: 24.5 us -> 22.6 us
  local copies, waits for them, and re-layouts: 7.28 us -> 6.48 us
    all_to_all x0 -> x1, blocking collectives: none -> 18.2 us  [on_device(): lax.all_to_all(send, 'band', split_axis=1, concat_axis=1, tiled=True)]
    all_to_all x1, starting transfers between devices: 11.2 us -> 7.88 us  [on_device(): lax.all_to_all(staged, 'ma', split_axis=0, concat_axis=0, tiled=True)]
    all_to_all x1, waiting for transfers between devices: 16.7 us -> 14.8 us  [on_device(): lax.all_to_all(staged, 'ma', split_axis=0, concat_axis=0, tiled=True)]
    concatenate x1, local copies, waits for them, and re-layouts: 1.79 us -> 0.22 us  [on_device(): send = jnp.concatenate([windows, payload], axis=2)]
    all_to_all x0 -> x2, local copies, waits for them, and re-layouts: none -> 1.46 us  [the longest x1 1.24 us: on_device(): lax.all_to_all(send, 'band', split_axis=1, concat_axis=1, tiled=True)]
where the time goes in v5:
time: 75.8 us; the launch traced here: 75.5 us
  waiting for transfers between devices  22.6 us (30%)
  blocking collectives  18.2 us (24%)
  starting transfers between devices  11.4 us (15%)
  matrix products  10.9 us (14%)
  local copies, waits for them, and re-layouts  6.48 us (9%)
  other arithmetic  5.42 us (7%)
    all_to_all x1, blocking collectives, on_device(): lax.all_to_all(send, 'band', split_axis=1, concat_axis=1, tiled=True)  18.2 us
    all_to_all x1, waiting for transfers between devices, on_device(): lax.all_to_all(staged, 'ma', split_axis=0, concat_axis=0, tiled=True)  14.8 us
    dot_general x1, matrix products, on_device(): lax.dot_general(legendre[0], harmonics[0], (((1,), (0,)), ((), ())), pref...  9.39 us
    all_to_all x1, starting transfers between devices, on_device(): lax.all_to_all(staged, 'ma', split_axis=0, concat_axis=0, tiled=True)  7.88 us
    all_to_all x1, waiting for transfers between devices, on_device(): lax.all_to_all(values, 'ma', split_axis=0, concat_axis=0, tiled=True)  7.75 us
    all_to_all x1, starting transfers between devices, on_device(): lax.all_to_all(values, 'ma', split_axis=0, concat_axis=0, tiled=True)  3.51 us
    unnamed x24, local copies, waits for them, and re-layouts  1.7 us
  transfers between devices with their start and end apart: 2, of which 2 were waited for; matrix products, arithmetic and copies ran while one was open for 0% of the time, Pallas kernels for 0%

profile of v5, /device:TPU:0, one launch (start us, length us, event | category | flops | bytes accessed | tf_op | source)
XLA Modules:
  0.0 75.5 jit_solution(9448772656602781338)
XLA Ops:
  0.0 9.4 %fusion = f32[2,512,256]{1,2,0:T(8,128)S(1)} fusion(bf16[1,2,8192,512]{3,2,1,0:T(8,128)(2,1)} %param.8, bf16[1,8192,256]{2,1,0:T(8,128)(2,1)} %param.7), kind=kOutput, calls=%fused_computation.1 | convolution fusion | flops 4294967296 | bytes 22020096 | tf_op jit(solution)/shard_map/dot_general | solution.py:60
  9.7 0.1 copy.166
  9.9 0.1 copy.171
  10.0 0.1 copy.169
  10.1 0.1 copy.173
  10.8 0.4 fusion.115
  11.2 0.4 fusion.116
  11.7 0.2 reduce_window_sum.11
  11.9 0.2 select_reduce_fusion.2
  12.1 0.2 convolution_convert_fusion
  12.5 0.1 broadcast_in_dim.19
  12.6 0.2 fusion.6
  12.8 0.7 maximum_bitcast_fusion
  13.5 0.2 copy.147
  13.7 0.2 copy.150
  14.0 18.2 %all_to_all.15 = bf16[16,8,2,13,128]{4,0,3,2,1:T(8,128)(2,1)S(1)} all-to-all(bf16[16,8,2,13,128]{4,0,3,2,1:T(8,128)(2,1)S(1)} %copy.150), channel_id=1, replica_groups=mesh['ma'=16,'band'=8] {'band'}, dimensions={1} | all-to-all | bytes 1703936 | tf_op jit(solution)/shard_map/all_to_all | solution.py:99
  32.2 1.2 %copy.151 = bf16[16,8,2,13,128]{4,1,3,2,0:T(8,128)(2,1)} copy(bf16[16,8,2,13,128]{4,0,3,2,1:T(8,128)(2,1)S(1)} %all_to_all.15) | data formatting | bytes 1703936 | tf_op jit(solution)/shard_map/all_to_all | solution.py:99
  33.5 7.9 %all-to-all-start.1 = ((bf16[16,8,2,13,128]{4,1,3,2,0:T(8,128)(2,1)}), bf16[16,8,2,13,128]{4,1,3,2,0:T(8,128)(2,1)S(1)}, u32[]{:S(2)}, u32[]{:S(2)}) async-start(bf16[16,8,2,13,128]{4,1,3,2,0:T(8,128)(2,1)} %copy.151), calls=%async_computation.1 | async-start | bytes 1703936 | tf_op jit(solution)/shard_map/all_to_all | solution.py:100
  41.4 0.3 cosine_convert_fusion
  41.7 14.8 %all-to-all-done.1 = bf16[16,8,2,13,128]{4,1,3,2,0:T(8,128)(2,1)S(1)} async-done(((bf16[16,8,2,13,128]{4,1,3,2,0:T(8,128)(2,1)}), bf16[16,8,2,13,128]{4,1,3,2,0:T(8,128)(2,1)S(1)}, u32[]{:S(2)}, u32[]{:S(2)}) %all-to-all-start.1) | async-done | bytes 852000 | tf_op jit(solution)/shard_map/all_to_all | solution.py:100
  56.5 0.2 copy.187
  56.7 0.6 reshape_squeeze.11
  57.4 0.3 fusion.110
  59.0 1.3 %select_reduce_fusion = f32[256,128]{1,0:T(8,128)S(1)} fusion(f32[256,8]{1,0:T(8,128)S(1)} %copy.162, s32[256,8]{1,0:T(8,128)S(1)} %iota_add_fusion), kind=kLoop, calls=%fused_computation.9 | loop fusion | flops 753664 | bytes 147456 | tf_op jit(solution)/shard_map/reduce_sum | solution.py:38
  60.2 0.7 multiply_convert_fusion
  61.0 0.5 convert_element_type.89
  61.5 0.3 fusion.4
  61.8 1.0 %fusion.111 = f32[16,16,128]{2,1,0:T(8,128)} fusion(bf16[16,16,1536]{2,1,0:T(8,128)(2,1)S(1)} %convert_element_type.89, bf16[1536,128,1]{1,0,2:T(8,128)(2,1)S(1)} %bitcast.97), kind=kOutput, calls=%fused_computation.196 | convolution fusion | flops 100663296 | bytes 1310720 | tf_op jit(solution)/shard_map/dot_general | solution.py:124
  62.8 3.5 %all-to-all-start.2 = ((f32[16,16,128]{2,1,0:T(8,128)}), f32[16,16,128]{2,1,0:T(8,128)S(1)}, u32[]{:S(2)}, u32[]{:S(2)}) async-start(f32[16,16,128]{2,1,0:T(8,128)} %fusion.111), calls=%async_computation.2 | async-start | bytes 262144 | tf_op jit(solution)/shard_map/all_to_all | solution.py:130
  66.3 7.8 %all-to-all-done.2 = f32[16,16,128]{2,1,0:T(8,128)S(1)} async-done(((f32[16,16,128]{2,1,0:T(8,128)}), f32[16,16,128]{2,1,0:T(8,128)S(1)}, u32[]{:S(2)}, u32[]{:S(2)}) %all-to-all-start.2) | async-done | bytes 131104 | tf_op jit(solution)/shard_map/all_to_all | solution.py:130
  74.1 0.6 gather_fusion
  74.7 0.7 broadcast_select_fusion
  (51 shorter events, 2.5 us)
Async XLA Ops:
  9.5 2.1 %copy-start.2 = (s32[128]{0:T(128)S(1)}, s32[128]{0:T(128)}, u32[]{:S(2)}) copy-start(s32[128]{0:T(128)} %param.11) | copy-start | bytes 1540
  9.5 2.1 %copy-start.3 = (s32[128]{0:T(128)S(1)}, s32[128]{0:T(128)}, u32[]{:S(2)}) copy-start(s32[128]{0:T(128)} %param.10) | copy-start | bytes 1540
  9.5 2.1 %copy-start = (f32[2,128]{1,0:T(2,128)S(1)}, f32[2,128]{1,0:T(2,128)}, u32[]{:S(2)}) copy-start(f32[2,128]{1,0:T(2,128)} %param.12) | copy-start | bytes 3076
  13.7 27.7 %copy-start.1 = (s32[128]{0:T(128)S(1)}, s32[128]{0:T(128)}, u32[]{:S(2)}) copy-start(s32[128]{0:T(128)} %param.9) | copy-start | bytes 1540
  33.5 23.0 %all-to-all-start.1 = ((bf16[16,8,2,13,128]{4,1,3,2,0:T(8,128)(2,1)}), bf16[16,8,2,13,128]{4,1,3,2,0:T(8,128)(2,1)S(1)}, u32[]{:S(2)}, u32[]{:S(2)}) async-start(bf16[16,8,2,13,128]{4,1,3,2,0:T(8,128)(2,1)} %copy.151), calls=%async_computation.1 | async-start | bytes 1703936 | tf_op jit(solution)/shard_map/all_to_all | solution.py:100
  62.8 11.3 %all-to-all-start.2 = ((f32[16,16,128]{2,1,0:T(8,128)}), f32[16,16,128]{2,1,0:T(8,128)S(1)}, u32[]{:S(2)}, u32[]{:S(2)}) async-start(f32[16,16,128]{2,1,0:T(8,128)} %fusion.111), calls=%async_computation.2 | async-start | bytes 262144 | tf_op jit(solution)/shard_map/all_to_all | solution.py:130

commit v6 on v4

--- a/solution.py
+++ b/solution.py
@@ -1,11 +1,49 @@
 import jax
 import jax.numpy as jnp
 from jax import lax
+from jax.experimental import pallas as pl
+from jax.experimental.pallas import tpu as pltpu
 from jax.sharding import PartitionSpec as P
 
 NPHI = 128
 TAPS = 8
 FIELDS = 8
+DEPTH_TILE = 1024
+
+
+def synthesis_kernel(table_ref, harm_ref, out_ref):
+    @pl.when(pl.program_id(0) == 0)
+    def _():
+        out_ref[...] = jnp.zeros_like(out_ref)
+
+    harm = harm_ref[...]
+    contract = (((0,), (0,)), ((), ()))
+    for part in range(2):
+        out_ref[part] += lax.dot_general(
+            harm, table_ref[part], contract, preferred_element_type=jnp.float32
+        )
+
+
+def synthesize(harmonics, legendre):
+    _, depth, columns = harmonics.shape
+    cycles = legendre.shape[3]
+    steps = depth // DEPTH_TILE
+    return pl.pallas_call(
+        synthesis_kernel,
+        grid=(steps,),
+        in_specs=[
+            pl.BlockSpec((None, 2, DEPTH_TILE, cycles), lambda k: (0, 0, k, 0)),
+            pl.BlockSpec((None, DEPTH_TILE, columns), lambda k: (0, k, 0)),
+        ],
+        out_specs=pl.BlockSpec((2, columns, cycles), lambda k: (0, 0, 0)),
+        out_shape=jax.ShapeDtypeStruct((2, columns, cycles), jnp.float32),
+        compiler_params=pltpu.CompilerParams(dimension_semantics=("arbitrary",)),
+        cost_estimate=pl.CostEstimate(
+            flops=4 * depth * cycles * columns,
+            transcendentals=0,
+            bytes_accessed=2 * (2 * depth * cycles + depth * columns) + 8 * cycles * columns,
+        ),
+    )(legendre, harmonics)
 
 
 def kernel_taps(shifts):
@@ -57,22 +95,25 @@
     me = lax.axis_index("ma")
     my_band = lax.axis_index("band")
 
-    both = lax.dot_general(
-        legendre[0], harmonics[0], (((1,), (0,)), ((), ())), preferred_element_type=jnp.float32
-    )
-    spectra = combine_parts(
-        both[0].reshape(cycle_total, 2, 2, evolutions),
-        both[1].reshape(cycle_total, 2, 2, evolutions),
-    )
+    both = synthesize(harmonics, legendre)
+    plus_part = both[0].reshape(2, 2, evolutions, cycle_total)
+    minus_part = both[1].reshape(2, 2, evolutions, cycle_total)
+    q_real = -(plus_part[0, 0] - minus_part[1, 1])
+    q_imag = -(plus_part[0, 1] + minus_part[1, 0])
+    u_real = -(plus_part[1, 0] + minus_part[0, 1])
+    u_imag = -(plus_part[1, 1] - minus_part[0, 0])
+    real_part = jnp.concatenate([q_real, u_real], axis=0)
+    imag_part = jnp.concatenate([q_imag, u_imag], axis=0)
+    spectra = jnp.stack([real_part, imag_part], axis=0).astype(jnp.bfloat16).transpose(0, 2, 1)
     width_out = spectra.shape[2]
-    by_band = spectra.reshape(owner_count, band_count, cycle_depth, 2, width_out)
-    by_band = by_band.transpose(1, 0, 2, 3, 4)
-    empty = jnp.zeros((band_count, 1, cycle_depth, 2, width_out), spectra.dtype)
+    by_band = spectra.reshape(2, owner_count, band_count, cycle_depth, width_out)
+    by_band = by_band.transpose(2, 1, 0, 3, 4)
+    empty = jnp.zeros((band_count, 1, 2, cycle_depth, width_out), spectra.dtype)
     padded = jnp.concatenate([empty, by_band, empty], axis=1)
     windows = jnp.stack(
-        [padded[:, s : s + owner_count] for s in range(3)], axis=2
+        [padded[:, s : s + owner_count] for s in range(3)], axis=3
     )
-    windows = windows.transpose(1, 0, 4, 2, 3, 5).reshape(blocks, 2, window, width_out)
+    windows = windows.transpose(1, 0, 2, 3, 4, 5).reshape(blocks, 2, window, width_out)
 
     owner_index = cycle_cell // cycle_depth
     one_hot = (owner_index[:, None] == jnp.arange(owner_count, dtype=jnp.int32)[None, :]).astype(

time: 63.5 us -> 69 us (1.087)
  Pallas kernels: 0 us -> 12.1 us
  matrix products: 10.9 us -> 1.49 us
  other arithmetic: 5.45 us -> 7.09 us
  local copies, waits for them, and re-layouts: 7.28 us -> 8.46 us
    pallas_call x0 -> x1, Pallas kernels: none -> 12.1 us  [synthesize(): pl.pallas_call(synthesis_kernel, grid=(steps,), in_specs=[pl.BlockSpec((N...]
    dot_general x1 -> x0, matrix products: 9.39 us -> none  [on_device(): lax.dot_general(legendre[0], harmonics[0], (((1,), (0,)), ((), ())), pref...]
    slice x3, local copies, waits for them, and re-layouts: 0.14 us -> 1.34 us  [the longest x1 1.27 us: on_device(): minus_part = both[1].reshape(2, 2, evolutions, cycle_total)]
    select_n x1, other arithmetic: 0.01 us -> 0.74 us  [on_device(): owner_index = cycle_cell // cycle_depth]
    unnamed x24 -> x18, local copies, waits for them, and re-layouts: 1.7 us -> 1.68 us
where the time goes in v6:
time: 69 us; the launch traced here: 68.6 us
  waiting for transfers between devices  24.5 us (36%)
  starting transfers between devices  14.7 us (21%)
  Pallas kernels  12.1 us (18%)
  local copies, waits for them, and re-layouts  8.46 us (12%)
  other arithmetic  7.09 us (10%)
  matrix products  1.49 us (2%)
    all_to_all x1, waiting for transfers between devices, on_device(): lax.all_to_all(send, ('ma', 'band'), split_axis=0, concat_axis=0, tiled=T...  16.7 us
    pallas_call x1, Pallas kernels, synthesize(): pl.pallas_call(synthesis_kernel, grid=(steps,), in_specs=[pl.BlockSpec((N...  12.1 us
    all_to_all x1, starting transfers between devices, on_device(): lax.all_to_all(send, ('ma', 'band'), split_axis=0, concat_axis=0, tiled=T...  11.2 us
    all_to_all x1, waiting for transfers between devices, on_device(): lax.all_to_all(values, 'ma', split_axis=0, concat_axis=0, tiled=True)  7.75 us
    all_to_all x1, starting transfers between devices, on_device(): lax.all_to_all(values, 'ma', split_axis=0, concat_axis=0, tiled=True)  3.51 us
    concatenate x1, local copies, waits for them, and re-layouts, on_device(): send = jnp.concatenate([windows, payload], axis=2)  1.79 us
    unnamed x18, local copies, waits for them, and re-layouts  1.68 us
  transfers between devices with their start and end apart: 2, of which 2 were waited for; matrix products, arithmetic and copies ran while one was open for 0% of the time, Pallas kernels for 0%

profile of v6, /device:TPU:0, one launch (start us, length us, event | category | flops | bytes accessed | tf_op | source)
XLA Modules:
  0.0 68.6 jit_solution(1378504257045165665)
XLA Ops:
  0.0 0.7 convert_bitcast_fusion
  0.7 0.7 %and_select_fusion = (s32[128]{0:T(128)S(1)}, bf16[128,1]{0,1:T(2,128)(2,1)S(1)}) fusion(s32[128]{0:T(128)} %param.10), kind=kLoop, calls=%fused_computation.174 | loop fusion | flops 2176 | bytes 1280 | tf_op jit(solution)/shard_map/jit(floor_divide)/jit(_where)/select_n | solution.py:118
  1.4 0.8 %fusion.108 = (bf16[128,1]{0,1:T(2,128)(2,1)S(1)}, bf16[128,1]{0,1:T(2,128)(2,1)S(1)}, bf16[128,1]{0,1:T(2,128)(2,1)S(1)}, bf16[128,1]{0,1:T(2,128)(2,1)S(1)}, b...) fusion(f32[2,128]{1,0:T(2,128)} %param.12), kind=kLoop, calls=%fused_computation.189 | loop fusion | flops 1792 | bytes 2560 | tf_op jit(solution)/shard_map/convert.10
  2.2 0.2 reduce_window_sum.11
  2.4 0.2 select_reduce_fusion.2
  2.6 0.2 convolution_convert_fusion
  3.0 0.1 broadcast_in_dim.19
  3.1 12.1 %shard_map.64 = f32[2,256,512]{2,1,0:T(8,128)} custom-call(bf16[1,2,8192,512]{3,2,1,0:T(8,128)(2,1)} %table_ref.1, bf16[1,8192,256]{2,1,0:T(8,128)(2,1)} %harm_ref.1), custom_call_target="tpu_custom_call" | custom-call | flops 4294967296 | bytes 22020096 | tf_op jit(solution)/shard_map/pallas_call | solution.py:31
  15.2 1.3 %fusion.110 = (f32[1,256,512]{2,1,0:T(8,128)S(1)}, f32[1,256,512]{2,1,0:T(8,128)S(1)}) fusion(f32[2,256,512]{2,1,0:T(8,128)} %shard_map.64), kind=kLoop, calls=%fused_computation.196 | loop fusion | bytes 2097152 | tf_op jit(solution)/shard_map/slice | solution.py:100
  16.7 0.1 copy.109
  16.8 0.1 copy.114
  17.0 0.1 copy.112
  18.0 0.2 fusion.5
  18.2 0.7 maximum_bitcast_fusion
  18.9 0.2 copy.94
  19.2 1.8 %copy.96 = bf16[128,2,13,128]{3,1,2,0:T(2,128)(2,1)} copy(bf16[128,2,13,128]{3,0,2,1:T(8,128)(2,1)S(1)} %fusion.3) | data formatting | bytes 1703936 | tf_op jit(solution)/shard_map/concatenate | solution.py:138
  20.9 11.2 %all-to-all-start = ((bf16[128,2,13,128]{3,1,2,0:T(2,128)(2,1)}), bf16[128,2,13,128]{3,1,2,0:T(2,128)(2,1)S(1)}, u32[]{:S(2)}, u32[]{:S(2)}) async-start(bf16[128,2,13,128]{3,1,2,0:T(2,128)(2,1)} %copy.96), calls=%async_computation | async-start | bytes 1703936 | tf_op jit(solution)/shard_map/all_to_all | solution.py:139
  32.1 0.3 cosine_convert_fusion
  32.4 16.7 %all-to-all-done = bf16[128,2,13,128]{3,1,2,0:T(2,128)(2,1)S(1)} async-done(((bf16[128,2,13,128]{3,1,2,0:T(2,128)(2,1)}), bf16[128,2,13,128]{3,1,2,0:T(2,128)(2,1)S(1)}, u32[]{:S(2)}, u32[]{:S(2)}) %all-to-all-start) | async-done | bytes 852000 | tf_op jit(solution)/shard_map/all_to_all | solution.py:139
  49.2 0.2 slice_reduce_fusion
  49.3 0.6 reshape_squeeze.11
  50.0 0.3 fusion.113
  51.6 1.3 %select_reduce_fusion = f32[256,128]{1,0:T(8,128)S(1)} fusion(f32[256,8]{1,0:T(8,128)S(1)} %copy.106, s32[256,8]{1,0:T(8,128)S(1)} %iota_add_fusion), kind=kLoop, calls=%fused_computation.8 | loop fusion | flops 753664 | bytes 147456 | tf_op jit(solution)/shard_map/reduce_sum | solution.py:76
  52.9 0.7 %multiply_convert_fusion = bf16[256,12,128]{2,1,0:T(8,128)(2,1)S(1)} fusion(f32[256,128]{1,0:T(8,128)S(1)} %select_reduce_fusion, f32[256,12]{1,0:T(8,128)S(1)} %copy.101), kind=kLoop, calls=%fused_computation.1 | loop fusion | flops 786432 | bytes 929792 | tf_op jit(solution)/shard_map/convert_element_type | solution.py:161
  53.6 0.5 convert_element_type.88
  54.1 0.5 slice.119
  54.7 0.3 fusion.2
  55.0 1.0 %fusion.114 = f32[16,16,128]{2,1,0:T(8,128)} fusion(bf16[16,16,1536]{2,1,0:T(8,128)(2,1)S(1)} %convert_element_type.88, bf16[1536,128,1]{1,0,2:T(8,128)(2,1)S(1)} %bitcast.80), kind=kOutput, calls=%fused_computation.200 | convolution fusion | flops 100663296 | bytes 1310720 | tf_op jit(solution)/shard_map/dot_general | solution.py:162
  56.0 3.5 %all-to-all-start.1 = ((f32[16,16,128]{2,1,0:T(8,128)}), f32[16,16,128]{2,1,0:T(8,128)S(1)}, u32[]{:S(2)}, u32[]{:S(2)}) async-start(f32[16,16,128]{2,1,0:T(8,128)} %fusion.114), calls=%async_computation.1 | async-start | bytes 262144 | tf_op jit(solution)/shard_map/all_to_all | solution.py:168
  59.5 7.8 %all-to-all-done.1 = f32[16,16,128]{2,1,0:T(8,128)S(1)} async-done(((f32[16,16,128]{2,1,0:T(8,128)}), f32[16,16,128]{2,1,0:T(8,128)S(1)}, u32[]{:S(2)}, u32[]{:S(2)}) %all-to-all-start.1) | async-done | bytes 131104 | tf_op jit(solution)/shard_map/all_to_all | solution.py:168
  67.3 0.6 gather_fusion
  67.9 0.7 %broadcast_select_fusion = f32[128,128]{1,0:T(8,128)} fusion(f32[128,128]{1,0:T(8,128)S(1)} %gather_fusion, pred[128]{0:T(512)(128)(4,1)S(1)} %get-tuple-element.6), kind=kLoop, calls=%fused_computation.54 | loop fusion | flops 16384 | bytes 131200 | tf_op jit(solution)/shard_map/jit(_take)/select_n | solution.py:169
  (42 shorter events, 2.8 us)
Async XLA Ops:
  19.1 13.0 %copy-start = (s32[128]{0:T(128)S(1)}, s32[128]{0:T(128)}, u32[]{:S(2)}) copy-start(s32[128]{0:T(128)} %param.9) | copy-start | bytes 1540
  20.9 28.2 %all-to-all-start = ((bf16[128,2,13,128]{3,1,2,0:T(2,128)(2,1)}), bf16[128,2,13,128]{3,1,2,0:T(2,128)(2,1)S(1)}, u32[]{:S(2)}, u32[]{:S(2)}) async-start(bf16[128,2,13,128]{3,1,2,0:T(2,128)(2,1)} %copy.96), calls=%async_computation | async-start | bytes 1703936 | tf_op jit(solution)/shard_map/all_to_all | solution.py:139
  56.0 11.3 %all-to-all-start.1 = ((f32[16,16,128]{2,1,0:T(8,128)}), f32[16,16,128]{2,1,0:T(8,128)S(1)}, u32[]{:S(2)}, u32[]{:S(2)}) async-start(f32[16,16,128]{2,1,0:T(8,128)} %fusion.114), calls=%async_computation.1 | async-start | bytes 262144 | tf_op jit(solution)/shard_map/all_to_all | solution.py:168

commit v7 on v4

--- a/solution.py
+++ b/solution.py
@@ -53,6 +53,7 @@
     blocks = owner_count * band_count
     cycle_depth = cycle_total // blocks
     window = 3 * cycle_depth
+    lead = 1
     capacity = cycle_cell.shape[0] // 8
     me = lax.axis_index("ma")
     my_band = lax.axis_index("band")
@@ -73,6 +74,7 @@
         [padded[:, s : s + owner_count] for s in range(3)], axis=2
     )
     windows = windows.transpose(1, 0, 4, 2, 3, 5).reshape(blocks, 2, window, width_out)
+    windows = windows[:, :, lead:]
 
     owner_index = cycle_cell // cycle_depth
     one_hot = (owner_index[:, None] == jnp.arange(owner_count, dtype=jnp.int32)[None, :]).astype(
@@ -97,13 +99,13 @@
     send = jnp.concatenate([windows, payload], axis=2)
     received = lax.all_to_all(send, ("ma", "band"), split_axis=0, concat_axis=0, tiled=True)
 
-    points_in = received[:, 0, window].reshape(owner_count, band_count, capacity, FIELDS)
+    points_in = received[:, 0, window - lead].reshape(owner_count, band_count, capacity, FIELDS)
     points_in = lax.dynamic_index_in_dim(points_in, my_band, axis=1, keepdims=False)
     points_in = points_in.reshape(owner_count * capacity, FIELDS).astype(jnp.float32)
 
     phase_rows = phase_table(m_values, NPHI, harmonics.shape[1])
     rows = jnp.einsum(
-        "kgi,gitc->tkc", phase_rows, received[:, :, :window], preferred_element_type=jnp.float32
+        "kgi,gitc->tkc", phase_rows, received, preferred_element_type=jnp.float32
     )
     rows = (2.0 * rows).astype(jnp.bfloat16)
 
@@ -114,7 +116,7 @@
     tap_shift = jnp.arange(TAPS).astype(jnp.float32) - 3.0
     across = kernel_taps(tap_shift[None, :] - offset_rows[:, None])
     beside_all = kernel_taps(tap_shift[None, :] - offset_cols[:, None])
-    first_row = (me - 1) * cycle_depth
+    first_row = (me - 1) * cycle_depth + lead
     cycle_weights = spread_weights(cycles_here - 3 - first_row, across, window)
     phi_weights = spread_weights(phis_here - 3, beside_all, NPHI)
     dense = (cycle_weights[:, :, None] * phi_weights[:, None, :]).astype(jnp.bfloat16)

time: 63.5 us -> 62.2 us (0.980)
  waiting for transfers between devices: 24.5 us -> 23.8 us
    all_to_all x1, waiting for transfers between devices: 16.7 us -> 16 us  [on_device(): lax.all_to_all(send, ('ma', 'band'), split_axis=0, concat_axis=0, tiled=T...]
where the time goes in v7:
time: 62.2 us; the launch traced here: 61.9 us
  waiting for transfers between devices  23.8 us (38%)
  starting transfers between devices  14.7 us (24%)
  matrix products  10.9 us (18%)
  local copies, waits for them, and re-layouts  6.72 us (11%)
  other arithmetic  5.43 us (9%)
    all_to_all x1, waiting for transfers between devices, on_device(): lax.all_to_all(send, ('ma', 'band'), split_axis=0, concat_axis=0, tiled=T...  16 us
    all_to_all x1, starting transfers between devices, on_device(): lax.all_to_all(send, ('ma', 'band'), split_axis=0, concat_axis=0, tiled=T...  11.2 us
    dot_general x1, matrix products, on_device(): lax.dot_general(legendre[0], harmonics[0], (((1,), (0,)), ((), ())), pref...  9.39 us
    all_to_all x1, waiting for transfers between devices, on_device(): lax.all_to_all(values, 'ma', split_axis=0, concat_axis=0, tiled=True)  7.75 us
    all_to_all x1, starting transfers between devices, on_device(): lax.all_to_all(values, 'ma', split_axis=0, concat_axis=0, tiled=True)  3.51 us
    concatenate x1, local copies, waits for them, and re-layouts, on_device(): send = jnp.concatenate([windows, payload], axis=2)  1.7 us
    unnamed x24, local copies, waits for them, and re-layouts  1.7 us
    reduce_sum x2, other arithmetic, spread_weights(): return jnp.sum(weights[:, :, None] * hits, axis=1)  1.29 us
  transfers between devices with their start and end apart: 2, of which 2 were waited for; matrix products, arithmetic and copies ran while one was open for 0% of the time, Pallas kernels for 0%

profile of v7, /device:TPU:0, one launch (start us, length us, event | category | flops | bytes accessed | tf_op | source)
XLA Modules:
  0.0 61.9 jit_solution(5444847094686228786)
XLA Ops:
  0.0 9.4 %fusion = f32[2,512,256]{1,2,0:T(8,128)S(1)} fusion(bf16[1,2,8192,512]{3,2,1,0:T(8,128)(2,1)} %param.8, bf16[1,8192,256]{2,1,0:T(8,128)(2,1)} %param.7), kind=kOutput, calls=%fused_computation.1 | convolution fusion | flops 4294967296 | bytes 22020096 | tf_op jit(solution)/shard_map/dot_general | solution.py:61
  9.7 0.1 copy.120
  9.9 0.1 copy.125
  10.0 0.1 copy.123
  10.1 0.1 copy.127
  10.3 0.1 copy.124
  10.4 0.1 copy.122
  10.8 0.4 fusion.117
  11.2 0.4 fusion.118
  11.7 0.2 reduce_window_sum.11
  11.9 0.2 select_reduce_fusion.2
  12.1 0.2 convolution_convert_fusion
  12.5 0.1 broadcast_in_dim.19
  12.6 0.2 fusion.8
  12.8 0.7 %maximum_bitcast_fusion = bf16[16,8,2,3,4,128]{5,4,1,0,2,3:T(4,128)(2,1)S(1)} fusion(bf16[8,16,1,4,2,128]{5,3,0,1,4,2:T(4,128)(2,1)S(1)} %get-tuple-element.19, bf16[8,16,1,4,2,128]{5,3,0,1,4,2:T(4,128)(2,1)S(1)} %fusion.117, bf16[8,16,1,4,2,128]{5,3,0,1,4,2:T(4,128)(2,1)S(1)} %get-tuple-element.18), kind=kLoop, calls=%fused_computation.14 | loop fusion | flops 786432 | bytes 1572864 | tf_op jit(solution)/shard_map/transpose | solution.py:76
  13.5 0.2 copy.103
  13.8 1.7 %copy.105 = bf16[128,2,12,128]{3,1,2,0:T(2,128)(2,1)} copy(bf16[128,2,12,128]{3,0,2,1:T(8,128)(2,1)S(1)} %fusion.6) | data formatting | bytes 1572864 | tf_op jit(solution)/shard_map/concatenate | solution.py:99
  15.5 11.2 %all-to-all-start = ((bf16[128,2,12,128]{3,1,2,0:T(2,128)(2,1)}), bf16[128,2,12,128]{3,1,2,0:T(2,128)(2,1)S(1)}, u32[]{:S(2)}, u32[]{:S(2)}) async-start(bf16[128,2,12,128]{3,1,2,0:T(2,128)(2,1)} %copy.105), calls=%async_computation | async-start | bytes 1572864 | tf_op jit(solution)/shard_map/all_to_all | solution.py:100
  26.7 0.3 cosine_convert_fusion
  27.0 16.0 %all-to-all-done = bf16[128,2,12,128]{3,1,2,0:T(2,128)(2,1)S(1)} async-done(((bf16[128,2,12,128]{3,1,2,0:T(2,128)(2,1)}), bf16[128,2,12,128]{3,1,2,0:T(2,128)(2,1)S(1)}, u32[]{:S(2)}, u32[]{:S(2)}) %all-to-all-start) | async-done | bytes 786464 | tf_op jit(solution)/shard_map/all_to_all | solution.py:100
  43.0 0.2 slice_reduce_fusion
  43.2 0.6 reshape_squeeze.11
  43.9 0.3 fusion.112
  45.5 1.3 %select_reduce_fusion = f32[256,128]{1,0:T(8,128)S(1)} fusion(f32[256,8]{1,0:T(8,128)S(1)} %copy.115, s32[256,8]{1,0:T(8,128)S(1)} %iota_add_fusion), kind=kLoop, calls=%fused_computation.11 | loop fusion | flops 753664 | bytes 147456 | tf_op jit(solution)/shard_map/reduce_sum | solution.py:38
  46.7 0.7 %multiply_convert_fusion = bf16[256,12,128]{2,1,0:T(8,128)(2,1)S(1)} fusion(f32[256,128]{1,0:T(8,128)S(1)} %select_reduce_fusion, f32[256,12]{1,0:T(8,128)S(1)} %copy.110), kind=kLoop, calls=%fused_computation.4 | loop fusion | flops 786432 | bytes 929792 | tf_op jit(solution)/shard_map/convert_element_type | solution.py:122
  47.4 0.5 convert_element_type.89
  48.0 0.3 fusion.5
  48.2 1.0 %fusion.113 = f32[16,16,128]{2,1,0:T(8,128)} fusion(bf16[16,16,1536]{2,1,0:T(8,128)(2,1)S(1)} %convert_element_type.89, bf16[1536,128,1]{1,0,2:T(8,128)(2,1)S(1)} %bitcast.84), kind=kOutput, calls=%fused_computation.197 | convolution fusion | flops 100663296 | bytes 1310720 | tf_op jit(solution)/shard_map/dot_general | solution.py:123
  49.3 3.5 %all-to-all-start.1 = ((f32[16,16,128]{2,1,0:T(8,128)}), f32[16,16,128]{2,1,0:T(8,128)S(1)}, u32[]{:S(2)}, u32[]{:S(2)}) async-start(f32[16,16,128]{2,1,0:T(8,128)} %fusion.113), calls=%async_computation.1 | async-start | bytes 262144 | tf_op jit(solution)/shard_map/all_to_all | solution.py:129
  52.8 7.8 %all-to-all-done.1 = f32[16,16,128]{2,1,0:T(8,128)S(1)} async-done(((f32[16,16,128]{2,1,0:T(8,128)}), f32[16,16,128]{2,1,0:T(8,128)S(1)}, u32[]{:S(2)}, u32[]{:S(2)}) %all-to-all-start.1) | async-done | bytes 131104 | tf_op jit(solution)/shard_map/all_to_all | solution.py:129
  60.6 0.6 %gather_fusion = f32[128,128]{1,0:T(8,128)S(1)} fusion(f32[256,128]{1,0:T(8,128)S(1)} %bitcast.72, s32[1024]{0:T(1024)S(1)} %pad_clamp_fusion), kind=kCustom, calls=%fused_computation | custom fusion | bytes 131584 | tf_op jit(solution)/shard_map/jit(_take)/gather | solution.py:130
  61.2 0.7 %broadcast_select_fusion = f32[128,128]{1,0:T(8,128)} fusion(f32[128,128]{1,0:T(8,128)S(1)} %gather_fusion, pred[128]{0:T(512)(128)(4,1)S(1)} %get-tuple-element.6), kind=kLoop, calls=%fused_computation.51 | loop fusion | flops 16384 | bytes 131200 | tf_op jit(solution)/shard_map/jit(_take)/select_n | solution.py:130
  (49 shorter events, 2.3 us)
Async XLA Ops:
  9.5 2.1 %copy-start.2 = (s32[128]{0:T(128)S(1)}, s32[128]{0:T(128)}, u32[]{:S(2)}) copy-start(s32[128]{0:T(128)} %param.11) | copy-start | bytes 1540
  9.5 2.1 %copy-start.3 = (s32[128]{0:T(128)S(1)}, s32[128]{0:T(128)}, u32[]{:S(2)}) copy-start(s32[128]{0:T(128)} %param.10) | copy-start | bytes 1540
  9.5 2.1 %copy-start = (f32[2,128]{1,0:T(2,128)S(1)}, f32[2,128]{1,0:T(2,128)}, u32[]{:S(2)}) copy-start(f32[2,128]{1,0:T(2,128)} %param.12) | copy-start | bytes 3076
  13.5 13.2 %copy-start.1 = (s32[128]{0:T(128)S(1)}, s32[128]{0:T(128)}, u32[]{:S(2)}) copy-start(s32[128]{0:T(128)} %param.9) | copy-start | bytes 1540
  15.5 27.5 %all-to-all-start = ((bf16[128,2,12,128]{3,1,2,0:T(2,128)(2,1)}), bf16[128,2,12,128]{3,1,2,0:T(2,128)(2,1)S(1)}, u32[]{:S(2)}, u32[]{:S(2)}) async-start(bf16[128,2,12,128]{3,1,2,0:T(2,128)(2,1)} %copy.105), calls=%async_computation | async-start | bytes 1572864 | tf_op jit(solution)/shard_map/all_to_all | solution.py:100
  49.3 11.3 %all-to-all-start.1 = ((f32[16,16,128]{2,1,0:T(8,128)}), f32[16,16,128]{2,1,0:T(8,128)S(1)}, u32[]{:S(2)}, u32[]{:S(2)}) async-start(f32[16,16,128]{2,1,0:T(8,128)} %fusion.113), calls=%async_computation.1 | async-start | bytes 262144 | tf_op jit(solution)/shard_map/all_to_all | solution.py:129

commit v8 on v7

--- a/solution.py
+++ b/solution.py
@@ -31,11 +31,11 @@
 
 
 def spread_weights(starts, weights, length):
-    tap_index = jnp.arange(TAPS, dtype=jnp.int32)
-    target = starts[:, None] + tap_index[None, :]
-    cells = jnp.arange(length, dtype=jnp.int32)
-    hits = (target[:, :, None] == cells[None, None, :]).astype(jnp.float32)
-    return jnp.sum(weights[:, :, None] * hits, axis=1)
+    cells = jnp.arange(length, dtype=jnp.int32)[None, :] - starts[:, None]
+    spread = jnp.zeros(cells.shape, weights.dtype)
+    for tap in range(TAPS):
+        spread = spread + jnp.where(cells == tap, weights[:, tap : tap + 1], 0.0)
+    return spread
 
 
 def split_three(x):
@@ -120,14 +120,12 @@
     cycle_weights = spread_weights(cycles_here - 3 - first_row, across, window)
     phi_weights = spread_weights(phis_here - 3, beside_all, NPHI)
     dense = (cycle_weights[:, :, None] * phi_weights[:, None, :]).astype(jnp.bfloat16)
-    values = jnp.dot(
-        dense.reshape(dense.shape[0], window * NPHI),
-        rows.reshape(window * NPHI, width_out),
-        preferred_element_type=jnp.float32,
+    values = lax.dot_general(
+        dense, rows, (((1, 2), (0, 1)), ((), ())), preferred_element_type=jnp.float32
     )
     values = values.reshape(owner_count, capacity, width_out)
     returned = lax.all_to_all(values, "ma", split_axis=0, concat_axis=0, tiled=True)
-    return jnp.take(returned.reshape(owner_count * capacity, width_out), flat_slot, axis=0)
+    return jnp.take(returned.reshape(owner_count * capacity, width_out), flat_slot, axis=0, mode="clip")
 
 
 def solution(mesh):

time: 62.2 us -> 59.7 us (0.960)
  other arithmetic: 5.43 us -> 3 us
    reduce_sum x2 -> x0, other arithmetic: 1.29 us -> none  [spread_weights(): return jnp.sum(weights[:, :, None] * hits, axis=1)]
    select_n x2 -> x0, other arithmetic: 0.72 us -> none  [on_device(): jnp.take(returned.reshape(owner_count * capacity, width_out), flat_slot,...]
    convert_element_type x1 -> x0, other arithmetic: 0.71 us -> none  [on_device(): (cycle_weights[:, :, None] * phi_weights[:, None, :]).astype(jnp.bfloat16)]
    dot_general x2 -> x1, matrix products: 1.3 us -> 1.46 us  [on_device(): lax.dot_general(dense, rows, (((1, 2), (0, 1)), ((), ())), preferred_elem...]
where the time goes in v8:
time: 59.7 us; the launch traced here: 59.5 us
  waiting for transfers between devices  23.8 us (40%)
  starting transfers between devices  14.7 us (25%)
  matrix products  11 us (18%)
  local copies, waits for them, and re-layouts  6.54 us (11%)
  other arithmetic  3 us (5%)
    all_to_all x1, waiting for transfers between devices, on_device(): lax.all_to_all(send, ('ma', 'band'), split_axis=0, concat_axis=0, tiled=T...  16 us
    all_to_all x1, starting transfers between devices, on_device(): lax.all_to_all(send, ('ma', 'band'), split_axis=0, concat_axis=0, tiled=T...  11.2 us
    dot_general x1, matrix products, on_device(): lax.dot_general(legendre[0], harmonics[0], (((1,), (0,)), ((), ())), pref...  9.39 us
    all_to_all x1, waiting for transfers between devices, on_device(): lax.all_to_all(values, 'ma', split_axis=0, concat_axis=0, tiled=True)  7.77 us
    all_to_all x1, starting transfers between devices, on_device(): lax.all_to_all(values, 'ma', split_axis=0, concat_axis=0, tiled=True)  3.51 us
    unnamed x24, local copies, waits for them, and re-layouts  1.7 us
    concatenate x1, local copies, waits for them, and re-layouts, on_device(): send = jnp.concatenate([windows, payload], axis=2)  1.69 us
    dot_general x1, matrix products, on_device(): lax.dot_general(dense, rows, (((1, 2), (0, 1)), ((), ())), preferred_elem...  1.46 us
  transfers between devices with their start and end apart: 2, of which 2 were waited for; matrix products, arithmetic and copies ran while one was open for 0% of the time, Pallas kernels for 0%

profile of v8, /device:TPU:0, one launch (start us, length us, event | category | flops | bytes accessed | tf_op | source)
XLA Modules:
  0.0 59.5 jit_solution(18127101618939377950)
XLA Ops:
  0.0 9.4 %fusion = f32[2,512,256]{1,2,0:T(8,128)S(1)} fusion(bf16[1,2,8192,512]{3,2,1,0:T(8,128)(2,1)} %param.8, bf16[1,8192,256]{2,1,0:T(8,128)(2,1)} %param.7), kind=kOutput, calls=%fused_computation.1 | convolution fusion | flops 4294967296 | bytes 22020096 | tf_op jit(solution)/shard_map/dot_general | solution.py:61
  9.5 0.1 copy.75
  9.7 0.1 copy.76
  9.8 0.1 copy.77
  10.0 0.1 copy.78
  10.1 0.1 copy.79
  10.2 0.1 copy.80
  10.4 0.1 copy.81
  10.5 0.1 copy.82
  10.8 0.4 fusion.143
  11.2 0.4 fusion.142
  11.6 0.2 fusion.14
  11.7 0.7 %maximum_bitcast_fusion = bf16[16,8,2,3,4,128]{5,4,1,0,2,3:T(4,128)(2,1)S(1)} fusion(bf16[8,16,1,4,2,128]{5,3,0,1,4,2:T(4,128)(2,1)S(1)} %get-tuple-element.17, bf16[8,16,1,4,2,128]{5,3,0,1,4,2:T(4,128)(2,1)S(1)} %fusion.142, bf16[8,16,1,4,2,128]{5,3,0,1,4,2:T(4,128)(2,1)S(1)} %get-tuple-element.16), kind=kLoop, calls=%fused_computation.14 | loop fusion | flops 786432 | bytes 1572864 | tf_op jit(solution)/shard_map/transpose | solution.py:76
  12.4 0.2 copy.58
  12.8 0.2 reduce_window_sum.11
  13.0 0.2 select_reduce_fusion
  13.2 0.2 convolution_convert_fusion
  13.4 0.1 copy.59
  13.5 0.1 broadcast_in_dim.158
  13.8 1.7 %copy.60 = bf16[128,2,12,128]{3,1,2,0:T(2,128)(2,1)} copy(bf16[128,2,12,128]{3,0,2,1:T(8,128)(2,1)S(1)} %fusion.8) | data formatting | bytes 1572864 | tf_op jit(solution)/shard_map/concatenate | solution.py:99
  15.4 11.2 %all-to-all-start = ((bf16[128,2,12,128]{3,1,2,0:T(2,128)(2,1)}), bf16[128,2,12,128]{3,1,2,0:T(2,128)(2,1)S(1)}, u32[]{:S(2)}, u32[]{:S(2)}) async-start(bf16[128,2,12,128]{3,1,2,0:T(2,128)(2,1)} %copy.60), calls=%async_computation | async-start | bytes 1572864 | tf_op jit(solution)/shard_map/all_to_all | solution.py:100
  26.7 0.3 cosine_convert_fusion
  26.9 16.0 %all-to-all-done = bf16[128,2,12,128]{3,1,2,0:T(2,128)(2,1)S(1)} async-done(((bf16[128,2,12,128]{3,1,2,0:T(2,128)(2,1)}), bf16[128,2,12,128]{3,1,2,0:T(2,128)(2,1)S(1)}, u32[]{:S(2)}, u32[]{:S(2)}) %all-to-all-start) | async-done | bytes 786464 | tf_op jit(solution)/shard_map/all_to_all | solution.py:100
  43.0 0.2 slice_reduce_fusion
  43.1 0.6 %reshape_squeeze.11 = bf16[16,8,16,8]{3,2,1,0:T(8,128)(2,1)S(1)} reshape(bf16[128,128]{1,0:T(8,128)(2,1)S(1)} %slice_reduce_fusion) | data formatting | bytes 65536 | tf_op jit(solution)/shard_map/reshape;squeeze | solution.py:102
  43.8 0.3 fusion.138
  44.9 0.1 fusion.68
  45.1 0.4 select_add_fusion
  45.5 1.5 %fusion.7 = f32[256,128,1]{1,0,2:T(8,128)} fusion(bf16[128,2,12,128]{3,1,2,0:T(2,128)(2,1)S(1)} %all-to-all-done, f32[256,128]{1,0:T(8,128)S(1)} %select_add_fusion, f32[256,12]{0,1:T(8,128)S(1)} %select_add_fusion.1, bf16[128,128,1]{1,0,2:T(8,128)(2,1)S(1)} %get-tuple-element.49, bf16[128,128,1]{1,0,2:T(8,128)(2,1)S(1)} %get-tuple-element.48), kind=kOutput, calls=%fused_computation.11 | convolution fusion | flops 202539008 | bytes 1126400 | tf_op jit(solution)/shard_map/dot_general | solution.py:123
  46.9 3.5 %all-to-all-start.1 = ((f32[16,16,128]{2,1,0:T(8,128)}), f32[16,16,128]{2,1,0:T(8,128)S(1)}, u32[]{:S(2)}, u32[]{:S(2)}) async-start(f32[16,16,128]{2,1,0:T(8,128)} %bitcast.47), calls=%async_computation.1 | async-start | bytes 262144 | tf_op jit(solution)/shard_map/all_to_all | solution.py:127
  50.4 7.8 %all-to-all-done.1 = f32[16,16,128]{2,1,0:T(8,128)S(1)} async-done(((f32[16,16,128]{2,1,0:T(8,128)}), f32[16,16,128]{2,1,0:T(8,128)S(1)}, u32[]{:S(2)}, u32[]{:S(2)}) %all-to-all-start.1) | async-done | bytes 131104 | tf_op jit(solution)/shard_map/all_to_all | solution.py:127
  58.2 1.2 %gather_fusion = f32[128,128]{1,0:T(8,128)} fusion(f32[256,128]{1,0:T(8,128)S(1)} %bitcast.93, s32[1024]{0:T(1024)S(1)} %pad_clamp_fusion), kind=kCustom, calls=%fused_computation | custom fusion | bytes 131584 | tf_op jit(solution)/shard_map/jit(_take)/gather | solution.py:128
  (41 shorter events, 1.5 us)
Async XLA Ops:
  10.7 1.9 %copy-start = (f32[2,128]{1,0:T(2,128)S(1)}, f32[2,128]{1,0:T(2,128)}, u32[]{:S(2)}) copy-start(f32[2,128]{1,0:T(2,128)} %param.12) | copy-start | bytes 3076
  10.7 1.9 %copy-start.2 = (s32[128]{0:T(128)S(1)}, s32[128]{0:T(128)}, u32[]{:S(2)}) copy-start(s32[128]{0:T(128)} %param.10) | copy-start | bytes 1540
  10.7 2.0 %copy-start.3 = (s32[128]{0:T(128)S(1)}, s32[128]{0:T(128)}, u32[]{:S(2)}) copy-start(s32[128]{0:T(128)} %param.11) | copy-start | bytes 1540
  12.4 14.2 %copy-start.1 = (s32[128]{0:T(128)S(1)}, s32[128]{0:T(128)}, u32[]{:S(2)}) copy-start(s32[128]{0:T(128)} %param.9) | copy-start | bytes 1540
  15.4 27.5 %all-to-all-start = ((bf16[128,2,12,128]{3,1,2,0:T(2,128)(2,1)}), bf16[128,2,12,128]{3,1,2,0:T(2,128)(2,1)S(1)}, u32[]{:S(2)}, u32[]{:S(2)}) async-start(bf16[128,2,12,128]{3,1,2,0:T(2,128)(2,1)} %copy.60), calls=%async_computation | async-start | bytes 1572864 | tf_op jit(solution)/shard_map/all_to_all | solution.py:100
  46.9 11.3 %all-to-all-start.1 = ((f32[16,16,128]{2,1,0:T(8,128)}), f32[16,16,128]{2,1,0:T(8,128)S(1)}, u32[]{:S(2)}, u32[]{:S(2)}) async-start(f32[16,16,128]{2,1,0:T(8,128)} %bitcast.47), calls=%async_computation.1 | async-start | bytes 262144 | tf_op jit(solution)/shard_map/all_to_all | solution.py:127

commit v9 on v8

--- a/solution.py
+++ b/solution.py
@@ -1,6 +1,7 @@
 import jax
 import jax.numpy as jnp
 from jax import lax
+from jax.experimental.layout import Layout, with_layout_constraint
 from jax.sharding import PartitionSpec as P
 
 NPHI = 128
@@ -97,6 +98,7 @@
     payload = payload.reshape(blocks, 1, 1, capacity * FIELDS)
     payload = jnp.concatenate([payload, jnp.zeros_like(payload)], axis=1)
     send = jnp.concatenate([windows, payload], axis=2)
+    send = with_layout_constraint(send, Layout(major_to_minor=(0, 2, 1, 3)))
     received = lax.all_to_all(send, ("ma", "band"), split_axis=0, concat_axis=0, tiled=True)
 
     points_in = received[:, 0, window - lead].reshape(owner_count, band_count, capacity, FIELDS)

time: 59.7 us -> 61.1 us (1.023)
  other arithmetic: 3 us -> 4.54 us
    concatenate x1 -> x0, local copies, waits for them, and re-layouts: 1.69 us -> none  [on_device(): send = jnp.concatenate([windows, payload], axis=2)]
    concatenate x1, other arithmetic: 0.07 us -> 1.61 us  [on_device(): send = jnp.concatenate([windows, payload], axis=2)]
    transpose x1, local copies, waits for them, and re-layouts: 0.16 us -> 1.22 us  [on_device(): windows.transpose(1, 0, 4, 2, 3, 5).reshape(blocks, 2, window, width_out)]
where the time goes in v9:
time: 61.1 us; the launch traced here: 60.9 us
  waiting for transfers between devices  23.8 us (39%)
  starting transfers between devices  14.7 us (24%)
  matrix products  11 us (18%)
  local copies, waits for them, and re-layouts  6.4 us (10%)
  other arithmetic  4.54 us (7%)
    all_to_all x1, waiting for transfers between devices, on_device(): lax.all_to_all(send, ('ma', 'band'), split_axis=0, concat_axis=0, tiled=T...  16 us
    all_to_all x1, starting transfers between devices, on_device(): lax.all_to_all(send, ('ma', 'band'), split_axis=0, concat_axis=0, tiled=T...  11.2 us
    dot_general x1, matrix products, on_device(): lax.dot_general(legendre[0], harmonics[0], (((1,), (0,)), ((), ())), pref...  9.39 us
    all_to_all x1, waiting for transfers between devices, on_device(): lax.all_to_all(values, 'ma', split_axis=0, concat_axis=0, tiled=True)  7.77 us
    all_to_all x1, starting transfers between devices, on_device(): lax.all_to_all(values, 'ma', split_axis=0, concat_axis=0, tiled=True)  3.51 us
    unnamed x24, local copies, waits for them, and re-layouts  1.7 us
    concatenate x1, other arithmetic, on_device(): send = jnp.concatenate([windows, payload], axis=2)  1.61 us
    dot_general x1, matrix products, on_device(): lax.dot_general(dense, rows, (((1, 2), (0, 1)), ((), ())), preferred_elem...  1.46 us
  transfers between devices with their start and end apart: 2, of which 2 were waited for; matrix products, arithmetic and copies ran while one was open for 0% of the time, Pallas kernels for 0%

profile of v9, /device:TPU:0, one launch (start us, length us, event | category | flops | bytes accessed | tf_op | source)
XLA Modules:
  0.0 60.9 jit_solution(2036008722988530460)
XLA Ops:
  0.0 9.4 %fusion = f32[2,512,256]{1,2,0:T(8,128)S(1)} fusion(bf16[1,2,8192,512]{3,2,1,0:T(8,128)(2,1)} %param.8, bf16[1,8192,256]{2,1,0:T(8,128)(2,1)} %param.7), kind=kOutput, calls=%fused_computation.1 | convolution fusion | flops 4294967296 | bytes 22020096 | tf_op jit(solution)/shard_map/dot_general | solution.py:62
  9.5 0.1 copy.60
  9.7 0.1 copy.61
  9.8 0.1 copy.62
  10.0 0.1 copy.63
  10.1 0.1 copy.64
  10.2 0.1 copy.65
  10.4 0.1 copy.66
  10.5 0.1 copy.67
  10.8 0.4 fusion.142
  11.2 0.4 fusion.141
  11.6 0.2 fusion.13
  11.8 0.7 %maximum_bitcast_fusion = bf16[16,8,2,3,4,128]{5,4,1,0,2,3:T(4,128)(2,1)S(1)} fusion(bf16[8,16,1,4,2,128]{5,3,0,1,4,2:T(4,128)(2,1)S(1)} %get-tuple-element.17, bf16[8,16,1,4,2,128]{5,3,0,1,4,2:T(4,128)(2,1)S(1)} %fusion.141, bf16[8,16,1,4,2,128]{5,3,0,1,4,2:T(4,128)(2,1)S(1)} %get-tuple-element.16), kind=kLoop, calls=%fused_computation.13 | loop fusion | flops 786432 | bytes 1572864 | tf_op jit(solution)/shard_map/transpose | solution.py:77
  12.4 1.2 %copy.43 = bf16[16,8,2,3,4,128]{5,2,4,3,1,0:T(2,128)(2,1)S(1)} copy(bf16[16,8,2,3,4,128]{5,4,1,0,2,3:T(4,128)(2,1)S(1)} %maximum_bitcast_fusion) | data formatting | bytes 1572864 | tf_op jit(solution)/shard_map/transpose | solution.py:77
  13.6 0.5 slice.198
  14.3 0.2 reduce_window_sum.11
  14.5 0.2 select_reduce_fusion
  14.7 0.2 convolution_convert_fusion
  14.9 0.1 copy.44
  15.0 0.1 broadcast_in_dim.158
  15.2 1.6 %fusion.7 = bf16[128,2,12,128]{3,1,2,0:T(2,128)(2,1)} fusion(bf16[128,1,1,128]{3,1,2,0:T(2,128)(2,1)S(1)} %copy.45, bf16[128,2,11,128]{3,1,2,0:T(2,128)(2,1)S(1)} %slice.198), kind=kLoop, calls=%fused_computation.12 | loop fusion | flops 2359296 | bytes 1540096 | tf_op jit(solution)/shard_map/concatenate | solution.py:100
  16.9 11.2 %all-to-all-start = ((bf16[128,2,12,128]{3,1,2,0:T(2,128)(2,1)}), bf16[128,2,12,128]{3,1,2,0:T(2,128)(2,1)S(1)}, u32[]{:S(2)}, u32[]{:S(2)}) async-start(bf16[128,2,12,128]{3,1,2,0:T(2,128)(2,1)} %fusion.7), calls=%async_computation | async-start | bytes 1572864 | tf_op jit(solution)/shard_map/all_to_all | solution.py:102
  28.1 0.3 cosine_convert_fusion
  28.3 16.0 %all-to-all-done = bf16[128,2,12,128]{3,1,2,0:T(2,128)(2,1)S(1)} async-done(((bf16[128,2,12,128]{3,1,2,0:T(2,128)(2,1)}), bf16[128,2,12,128]{3,1,2,0:T(2,128)(2,1)S(1)}, u32[]{:S(2)}, u32[]{:S(2)}) %all-to-all-start) | async-done | bytes 786464 | tf_op jit(solution)/shard_map/all_to_all | solution.py:102
  44.4 0.2 slice_reduce_fusion
  44.6 0.6 reshape_squeeze.11
  45.2 0.3 fusion.137
  46.5 0.4 select_add_fusion
  46.9 1.5 %fusion.6 = f32[256,128,1]{1,0,2:T(8,128)} fusion(bf16[128,2,12,128]{3,1,2,0:T(2,128)(2,1)S(1)} %all-to-all-done, f32[256,128]{1,0:T(8,128)S(1)} %select_add_fusion, f32[256,12]{0,1:T(8,128)S(1)} %select_add_fusion.1, bf16[128,128,1]{1,0,2:T(8,128)(2,1)S(1)} %get-tuple-element.49, bf16[128,128,1]{1,0,2:T(8,128)(2,1)S(1)} %get-tuple-element.48), kind=kOutput, calls=%fused_computation.10 | convolution fusion | flops 202539008 | bytes 1126400 | tf_op jit(solution)/shard_map/dot_general | solution.py:125
  48.3 3.5 %all-to-all-start.1 = ((f32[16,16,128]{2,1,0:T(8,128)}), f32[16,16,128]{2,1,0:T(8,128)S(1)}, u32[]{:S(2)}, u32[]{:S(2)}) async-start(f32[16,16,128]{2,1,0:T(8,128)} %bitcast.47), calls=%async_computation.1 | async-start | bytes 262144 | tf_op jit(solution)/shard_map/all_to_all | solution.py:129
  51.9 7.8 %all-to-all-done.1 = f32[16,16,128]{2,1,0:T(8,128)S(1)} async-done(((f32[16,16,128]{2,1,0:T(8,128)}), f32[16,16,128]{2,1,0:T(8,128)S(1)}, u32[]{:S(2)}, u32[]{:S(2)}) %all-to-all-start.1) | async-done | bytes 131104 | tf_op jit(solution)/shard_map/all_to_all | solution.py:129
  59.6 1.2 %gather_fusion = f32[128,128]{1,0:T(8,128)} fusion(f32[256,128]{1,0:T(8,128)S(1)} %bitcast.93, s32[1024]{0:T(1024)S(1)} %pad_clamp_fusion), kind=kCustom, calls=%fused_computation | custom fusion | bytes 131584 | tf_op jit(solution)/shard_map/jit(_take)/gather | solution.py:130
  (41 shorter events, 1.5 us)
Async XLA Ops:
  10.7 3.4 %copy-start = (f32[2,128]{1,0:T(2,128)S(1)}, f32[2,128]{1,0:T(2,128)}, u32[]{:S(2)}) copy-start(f32[2,128]{1,0:T(2,128)} %param.12) | copy-start | bytes 3076
  10.7 3.4 %copy-start.2 = (s32[128]{0:T(128)S(1)}, s32[128]{0:T(128)}, u32[]{:S(2)}) copy-start(s32[128]{0:T(128)} %param.10) | copy-start | bytes 1540
  10.7 3.5 %copy-start.3 = (s32[128]{0:T(128)S(1)}, s32[128]{0:T(128)}, u32[]{:S(2)}) copy-start(s32[128]{0:T(128)} %param.11) | copy-start | bytes 1540
  11.7 16.3 %copy-start.1 = (s32[128]{0:T(128)S(1)}, s32[128]{0:T(128)}, u32[]{:S(2)}) copy-start(s32[128]{0:T(128)} %param.9) | copy-start | bytes 1540
  16.9 27.5 %all-to-all-start = ((bf16[128,2,12,128]{3,1,2,0:T(2,128)(2,1)}), bf16[128,2,12,128]{3,1,2,0:T(2,128)(2,1)S(1)}, u32[]{:S(2)}, u32[]{:S(2)}) async-start(bf16[128,2,12,128]{3,1,2,0:T(2,128)(2,1)} %fusion.7), calls=%async_computation | async-start | bytes 1572864 | tf_op jit(solution)/shard_map/all_to_all | solution.py:102
  48.3 11.3 %all-to-all-start.1 = ((f32[16,16,128]{2,1,0:T(8,128)}), f32[16,16,128]{2,1,0:T(8,128)S(1)}, u32[]{:S(2)}, u32[]{:S(2)}) async-start(f32[16,16,128]{2,1,0:T(8,128)} %bitcast.47), calls=%async_computation.1 | async-start | bytes 262144 | tf_op jit(solution)/shard_map/all_to_all | solution.py:129

commit v10 on v8

--- a/solution.py
+++ b/solution.py
@@ -125,7 +125,14 @@
     )
     values = values.reshape(owner_count, capacity, width_out)
     returned = lax.all_to_all(values, "ma", split_axis=0, concat_axis=0, tiled=True)
-    return jnp.take(returned.reshape(owner_count * capacity, width_out), flat_slot, axis=0, mode="clip")
+    pick = (
+        flat_slot[:, None] == jnp.arange(owner_count * capacity, dtype=jnp.int32)[None, :]
+    ).astype(jnp.float32)
+    return jnp.dot(
+        pick,
+        returned.reshape(owner_count * capacity, width_out),
+        precision=lax.Precision.HIGHEST,
+    )
 
 
 def solution(mesh):

time: 59.7 us -> 57.8 us (0.968)
  blocking collectives: 0 us -> 10.4 us
  waiting for transfers between devices: 23.8 us -> 16 us
  starting transfers between devices: 14.7 us -> 11.2 us
  local copies, waits for them, and re-layouts: 6.54 us -> 5.31 us
    all_to_all x0 -> x1, blocking collectives: none -> 10.4 us  [on_device(): lax.all_to_all(values, 'ma', split_axis=0, concat_axis=0, tiled=True)]
    all_to_all x1 -> x0, waiting for transfers between devices: 7.77 us -> none  [on_device(): lax.all_to_all(values, 'ma', split_axis=0, concat_axis=0, tiled=True)]
    all_to_all x1 -> x0, starting transfers between devices: 3.51 us -> none  [on_device(): lax.all_to_all(values, 'ma', split_axis=0, concat_axis=0, tiled=True)]
    gather x1 -> x0, local copies, waits for them, and re-layouts: 1.24 us -> none  [on_device(): jnp.take(returned.reshape(owner_count * capacity, width_out), flat_slot,...]
    dot_general x0 -> x1, matrix products: none -> 0.89 us  [on_device(): jnp.dot(pick, returned.reshape(owner_count * capacity, width_out), precis...]
    dot_general x1, matrix products: 1.46 us -> 0.8 us  [on_device(): lax.dot_general(dense, rows, (((1, 2), (0, 1)), ((), ())), preferred_elem...]
  transfers between devices with their start and end apart: 2 -> 1, of which waited for: 2 -> 1; matrix products, arithmetic and copies ran while one was open for 0% -> 1% of each run, Pallas kernels for 0% -> 0%
where the time goes in v10:
time: 57.8 us; the launch traced here: 57.6 us
  waiting for transfers between devices  16 us (28%)
  matrix products  11.3 us (20%)
  starting transfers between devices  11.2 us (19%)
  blocking collectives  10.4 us (18%)
  local copies, waits for them, and re-layouts  5.31 us (9%)
  other arithmetic  2.99 us (5%)
    all_to_all x1, waiting for transfers between devices, on_device(): lax.all_to_all(send, ('ma', 'band'), split_axis=0, concat_axis=0, tiled=T...  16 us
    all_to_all x1, starting transfers between devices, on_device(): lax.all_to_all(send, ('ma', 'band'), split_axis=0, concat_axis=0, tiled=T...  11.2 us
    all_to_all x1, blocking collectives, on_device(): lax.all_to_all(values, 'ma', split_axis=0, concat_axis=0, tiled=True)  10.4 us
    dot_general x1, matrix products, on_device(): lax.dot_general(legendre[0], harmonics[0], (((1,), (0,)), ((), ())), pref...  9.39 us
    unnamed x24, local copies, waits for them, and re-layouts  1.7 us
    concatenate x1, local copies, waits for them, and re-layouts, on_device(): send = jnp.concatenate([windows, payload], axis=2)  1.7 us
  transfers between devices with their start and end apart: 1, of which 1 were waited for; matrix products, arithmetic and copies ran while one was open for 1% of the time, Pallas kernels for 0%

profile of v10, /device:TPU:0, one launch (start us, length us, event | category | flops | bytes accessed | tf_op | source)
XLA Modules:
  0.0 57.6 jit_solution(11194790569513400518)
XLA Ops:
  0.0 9.4 %fusion = f32[2,512,256]{1,2,0:T(8,128)S(1)} fusion(bf16[1,2,8192,512]{3,2,1,0:T(8,128)(2,1)} %param.8, bf16[1,8192,256]{2,1,0:T(8,128)(2,1)} %param.7), kind=kOutput, calls=%fused_computation | convolution fusion | flops 4294967296 | bytes 22020096 | tf_op jit(solution)/shard_map/dot_general | solution.py:61
  9.5 0.1 copy.75
  9.7 0.1 copy.76
  9.8 0.1 copy.77
  10.0 0.1 copy.78
  10.1 0.1 copy.79
  10.2 0.1 copy.80
  10.4 0.1 copy.81
  10.5 0.1 copy.82
  10.8 0.4 fusion.146
  11.2 0.4 fusion.145
  11.6 0.2 fusion.14
  11.7 0.7 %maximum_bitcast_fusion = bf16[16,8,2,3,4,128]{5,4,1,0,2,3:T(4,128)(2,1)S(1)} fusion(bf16[8,16,1,4,2,128]{5,3,0,1,4,2:T(4,128)(2,1)S(1)} %get-tuple-element.17, bf16[8,16,1,4,2,128]{5,3,0,1,4,2:T(4,128)(2,1)S(1)} %fusion.145, bf16[8,16,1,4,2,128]{5,3,0,1,4,2:T(4,128)(2,1)S(1)} %get-tuple-element.16), kind=kLoop, calls=%fused_computation.13 | loop fusion | flops 786432 | bytes 1572864 | tf_op jit(solution)/shard_map/transpose | solution.py:76
  12.4 0.2 copy.58
  12.8 0.2 reduce_window_sum.11
  13.0 0.2 select_reduce_fusion
  13.2 0.2 convolution_convert_fusion
  13.4 0.1 copy.59
  13.5 0.1 broadcast_in_dim.156
  13.8 1.7 %copy.60 = bf16[128,2,12,128]{3,1,2,0:T(2,128)(2,1)} copy(bf16[128,2,12,128]{3,0,2,1:T(8,128)(2,1)S(1)} %fusion.8) | data formatting | bytes 1572864 | tf_op jit(solution)/shard_map/concatenate | solution.py:99
  15.5 11.2 %all-to-all-start = ((bf16[128,2,12,128]{3,1,2,0:T(2,128)(2,1)}), bf16[128,2,12,128]{3,1,2,0:T(2,128)(2,1)S(1)}, u32[]{:S(2)}, u32[]{:S(2)}) async-start(bf16[128,2,12,128]{3,1,2,0:T(2,128)(2,1)} %copy.60), calls=%async_computation | async-start | bytes 1572864 | tf_op jit(solution)/shard_map/all_to_all | solution.py:100
  26.7 0.3 cosine_convert_fusion
  26.9 16.0 %all-to-all-done = bf16[128,2,12,128]{3,1,2,0:T(2,128)(2,1)S(1)} async-done(((bf16[128,2,12,128]{3,1,2,0:T(2,128)(2,1)}), bf16[128,2,12,128]{3,1,2,0:T(2,128)(2,1)S(1)}, u32[]{:S(2)}, u32[]{:S(2)}) %all-to-all-start) | async-done | bytes 786464 | tf_op jit(solution)/shard_map/all_to_all | solution.py:100
  43.0 0.2 slice_reduce_fusion
  43.2 0.6 %reshape_squeeze.11 = bf16[16,8,16,8]{3,2,1,0:T(8,128)(2,1)S(1)} reshape(bf16[128,128]{1,0:T(8,128)(2,1)S(1)} %slice_reduce_fusion) | data formatting | bytes 65536 | tf_op jit(solution)/shard_map/reshape;squeeze | solution.py:102
  43.8 0.3 fusion.140
  44.6 0.1 add_subtract_fusion
  44.9 0.1 fusion.70
  45.1 0.4 select_add_fusion
  45.5 0.8 %fusion.7 = f32[256,128,1]{1,0,2:T(8,128)S(1)} fusion(bf16[128,2,12,128]{3,1,2,0:T(2,128)(2,1)S(1)} %all-to-all-done, f32[256,128]{1,0:T(8,128)S(1)} %select_add_fusion, f32[256,12]{0,1:T(8,128)S(1)} %select_add_fusion.1, bf16[128,128,1]{1,0,2:T(8,128)(2,1)S(1)} %get-tuple-element.49, bf16[128,128,1]{1,0,2:T(8,128)(2,1)S(1)} %get-tuple-element.48), kind=kOutput, calls=%fused_computation.10 | convolution fusion | flops 202539008 | bytes 1126400 | tf_op jit(solution)/shard_map/dot_general | solution.py:123
  46.3 10.4 %all_to_all.10 = f32[16,16,128]{2,1,0:T(8,128)S(1)} all-to-all(f32[16,16,128]{2,1,0:T(8,128)S(1)} %bitcast.106), channel_id=1, replica_groups=mesh['ma'=16,'band'=8] {'ma'}, dimensions={0} | all-to-all | bytes 262144 | tf_op jit(solution)/shard_map/all_to_all | solution.py:127
  56.7 0.9 %fusion.24 = f32[128,128]{1,0:T(8,128)} fusion(f32[256,128]{1,0:T(8,128)S(1)} %bitcast.105, s32[128]{0:T(128)S(1)} %multiply_add_fusion.4), kind=kOutput, calls=%fused_computation.40 | convolution fusion | flops 50364416 | bytes 197120 | tf_op jit(solution)/shard_map/dot_general | solution.py:131
  (39 shorter events, 1.4 us)
Async XLA Ops:
  10.7 1.9 %copy-start = (f32[2,128]{1,0:T(2,128)S(1)}, f32[2,128]{1,0:T(2,128)}, u32[]{:S(2)}) copy-start(f32[2,128]{1,0:T(2,128)} %param.12) | copy-start | bytes 3076
  10.7 1.9 %copy-start.2 = (s32[128]{0:T(128)S(1)}, s32[128]{0:T(128)}, u32[]{:S(2)}) copy-start(s32[128]{0:T(128)} %param.10) | copy-start | bytes 1540
  10.7 2.0 %copy-start.3 = (s32[128]{0:T(128)S(1)}, s32[128]{0:T(128)}, u32[]{:S(2)}) copy-start(s32[128]{0:T(128)} %param.11) | copy-start | bytes 1540
  12.4 14.2 %copy-start.1 = (s32[128]{0:T(128)S(1)}, s32[128]{0:T(128)}, u32[]{:S(2)}) copy-start(s32[128]{0:T(128)} %param.9) | copy-start | bytes 1540
  15.5 27.5 %all-to-all-start = ((bf16[128,2,12,128]{3,1,2,0:T(2,128)(2,1)}), bf16[128,2,12,128]{3,1,2,0:T(2,128)(2,1)S(1)}, u32[]{:S(2)}, u32[]{:S(2)}) async-start(bf16[128,2,12,128]{3,1,2,0:T(2,128)(2,1)} %copy.60), calls=%async_computation | async-start | bytes 1572864 | tf_op jit(solution)/shard_map/all_to_all | solution.py:100

commit v11 on v10

--- a/solution.py
+++ b/solution.py
@@ -1,6 +1,7 @@
 import jax
 import jax.numpy as jnp
 from jax import lax
+from jax.experimental.layout import Layout, with_layout_constraint
 from jax.sharding import PartitionSpec as P
 
 NPHI = 128
@@ -61,6 +62,7 @@
     both = lax.dot_general(
         legendre[0], harmonics[0], (((1,), (0,)), ((), ())), preferred_element_type=jnp.float32
     )
+    both = with_layout_constraint(both, Layout(major_to_minor=(0, 1, 2)))
     spectra = combine_parts(
         both[0].reshape(cycle_total, 2, 2, evolutions),
         both[1].reshape(cycle_total, 2, 2, evolutions),

time: 57.8 us -> 57.5 us (level)
    unnamed x24 -> x16, local copies, waits for them, and re-layouts: 1.7 us -> 0.7 us
where the time goes in v11:
time: 57.5 us; the launch traced here: 57.3 us
  waiting for transfers between devices  16 us (28%)
  matrix products  11.3 us (20%)
  starting transfers between devices  11.2 us (19%)
  blocking collectives  10.4 us (18%)
  local copies, waits for them, and re-layouts  5.1 us (9%)
  other arithmetic  2.96 us (5%)
    all_to_all x1, waiting for transfers between devices, on_device(): lax.all_to_all(send, ('ma', 'band'), split_axis=0, concat_axis=0, tiled=T...  16 us
    all_to_all x1, starting transfers between devices, on_device(): lax.all_to_all(send, ('ma', 'band'), split_axis=0, concat_axis=0, tiled=T...  11.2 us
    all_to_all x1, blocking collectives, on_device(): lax.all_to_all(values, 'ma', split_axis=0, concat_axis=0, tiled=True)  10.4 us
    dot_general x1, matrix products, on_device(): lax.dot_general(legendre[0], harmonics[0], (((1,), (0,)), ((), ())), pref...  9.37 us
    concatenate x1, local copies, waits for them, and re-layouts, on_device(): send = jnp.concatenate([windows, payload], axis=2)  1.69 us
  transfers between devices with their start and end apart: 1, of which 1 were waited for; matrix products, arithmetic and copies ran while one was open for 1% of the time, Pallas kernels for 0%

profile of v11, /device:TPU:0, one launch (start us, length us, event | category | flops | bytes accessed | tf_op | source)
XLA Modules:
  0.0 57.3 jit_solution(11516226772474056132)
XLA Ops:
  0.0 9.4 %fusion = f32[2,512,256]{2,1,0:T(8,128)S(1)} fusion(bf16[1,2,8192,512]{3,2,1,0:T(8,128)(2,1)} %param.8, bf16[1,8192,256]{2,1,0:T(8,128)(2,1)} %param.7), kind=kOutput, calls=%fused_computation | convolution fusion | flops 4294967296 | bytes 22020096 | tf_op jit(solution)/shard_map/dot_general | solution.py:62
  9.5 0.2 copy.46
  9.7 0.2 copy.47
  9.9 0.1 fusion.23
  10.0 0.1 copy.48
  10.1 0.1 copy.49
  10.3 0.1 copy.50
  10.4 0.1 copy.51
  10.5 0.4 fusion.152
  10.9 0.4 fusion.151
  11.3 0.2 fusion.14
  11.4 0.7 %maximum_bitcast_fusion = bf16[16,8,2,3,4,128]{5,4,1,0,2,3:T(4,128)(2,1)S(1)} fusion(bf16[8,16,1,4,2,128]{5,3,0,1,4,2:T(4,128)(2,1)S(1)} %get-tuple-element.13, bf16[8,16,1,4,2,128]{5,3,0,1,4,2:T(4,128)(2,1)S(1)} %fusion.151, bf16[8,16,1,4,2,128]{5,3,0,1,4,2:T(4,128)(2,1)S(1)} %get-tuple-element.12), kind=kLoop, calls=%fused_computation.13 | loop fusion | flops 786432 | bytes 1572864 | tf_op jit(solution)/shard_map/transpose | solution.py:78
  12.1 0.2 copy.52
  12.5 0.2 reduce_window_sum.11
  12.7 0.2 select_reduce_fusion
  12.9 0.2 convolution_convert_fusion
  13.1 0.1 copy.53
  13.2 0.1 broadcast_in_dim.156
  13.4 1.7 %copy.54 = bf16[128,2,12,128]{3,1,2,0:T(2,128)(2,1)} copy(bf16[128,2,12,128]{3,0,2,1:T(8,128)(2,1)S(1)} %fusion.8) | data formatting | bytes 1572864 | tf_op jit(solution)/shard_map/concatenate | solution.py:101
  15.1 11.2 %all-to-all-start = ((bf16[128,2,12,128]{3,1,2,0:T(2,128)(2,1)}), bf16[128,2,12,128]{3,1,2,0:T(2,128)(2,1)S(1)}, u32[]{:S(2)}, u32[]{:S(2)}) async-start(bf16[128,2,12,128]{3,1,2,0:T(2,128)(2,1)} %copy.54), calls=%async_computation | async-start | bytes 1572864 | tf_op jit(solution)/shard_map/all_to_all | solution.py:102
  26.3 0.3 cosine_convert_fusion
  26.6 16.0 %all-to-all-done = bf16[128,2,12,128]{3,1,2,0:T(2,128)(2,1)S(1)} async-done(((bf16[128,2,12,128]{3,1,2,0:T(2,128)(2,1)}), bf16[128,2,12,128]{3,1,2,0:T(2,128)(2,1)S(1)}, u32[]{:S(2)}, u32[]{:S(2)}) %all-to-all-start) | async-done | bytes 786464 | tf_op jit(solution)/shard_map/all_to_all | solution.py:102
  42.7 0.2 slice_reduce_fusion
  42.8 0.6 %reshape_squeeze.11 = bf16[16,8,16,8]{3,2,1,0:T(8,128)(2,1)S(1)} reshape(bf16[128,128]{1,0:T(8,128)(2,1)S(1)} %slice_reduce_fusion) | data formatting | bytes 65536 | tf_op jit(solution)/shard_map/reshape;squeeze | solution.py:104
  43.5 0.3 fusion.146
  43.9 0.1 copy.75
  44.3 0.1 add_subtract_fusion
  44.6 0.1 fusion.78
  44.8 0.4 select_add_fusion
  45.1 0.8 %fusion.7 = f32[256,128,1]{1,0,2:T(8,128)S(1)} fusion(bf16[128,2,12,128]{3,1,2,0:T(2,128)(2,1)S(1)} %all-to-all-done, f32[256,128]{1,0:T(8,128)S(1)} %select_add_fusion, f32[256,12]{0,1:T(8,128)S(1)} %select_add_fusion.1, bf16[128,128,1]{1,0,2:T(8,128)(2,1)S(1)} %get-tuple-element.45, bf16[128,128,1]{1,0,2:T(8,128)(2,1)S(1)} %get-tuple-element.44), kind=kOutput, calls=%fused_computation.10 | convolution fusion | flops 202539008 | bytes 1126400 | tf_op jit(solution)/shard_map/dot_general | solution.py:125
  46.0 10.4 %all_to_all.10 = f32[16,16,128]{2,1,0:T(8,128)S(1)} all-to-all(f32[16,16,128]{2,1,0:T(8,128)S(1)} %bitcast.105), channel_id=1, replica_groups=mesh['ma'=16,'band'=8] {'ma'}, dimensions={0} | all-to-all | bytes 262144 | tf_op jit(solution)/shard_map/all_to_all | solution.py:129
  56.4 0.9 %fusion.32 = f32[128,128]{1,0:T(8,128)} fusion(f32[256,128]{1,0:T(8,128)S(1)} %bitcast.104, s32[128]{0:T(128)S(1)} %multiply_add_fusion.4), kind=kOutput, calls=%fused_computation.48 | convolution fusion | flops 50364416 | bytes 197120 | tf_op jit(solution)/shard_map/dot_general | solution.py:133
  (32 shorter events, 1.0 us)
Async XLA Ops:
  10.0 2.4 %copy-start = (f32[2,128]{1,0:T(2,128)S(1)}, f32[2,128]{1,0:T(2,128)}, u32[]{:S(2)}) copy-start(f32[2,128]{1,0:T(2,128)} %param.12) | copy-start | bytes 3076
  10.0 2.4 %copy-start.2 = (s32[128]{0:T(128)S(1)}, s32[128]{0:T(128)}, u32[]{:S(2)}) copy-start(s32[128]{0:T(128)} %param.10) | copy-start | bytes 1540
  10.0 2.4 %copy-start.3 = (s32[128]{0:T(128)S(1)}, s32[128]{0:T(128)}, u32[]{:S(2)}) copy-start(s32[128]{0:T(128)} %param.11) | copy-start | bytes 1540
  12.1 14.2 %copy-start.1 = (s32[128]{0:T(128)S(1)}, s32[128]{0:T(128)}, u32[]{:S(2)}) copy-start(s32[128]{0:T(128)} %param.9) | copy-start | bytes 1540
  15.1 27.5 %all-to-all-start = ((bf16[128,2,12,128]{3,1,2,0:T(2,128)(2,1)}), bf16[128,2,12,128]{3,1,2,0:T(2,128)(2,1)S(1)}, u32[]{:S(2)}, u32[]{:S(2)}) async-start(bf16[128,2,12,128]{3,1,2,0:T(2,128)(2,1)} %copy.54), calls=%async_computation | async-start | bytes 1572864 | tf_op jit(solution)/shard_map/all_to_all | solution.py:102

commit v12 on v10

--- a/solution.py
+++ b/solution.py
@@ -91,17 +91,19 @@
         + list(split_three(offsets[1])),
         axis=1,
     ).astype(jnp.bfloat16)
-    payload = jnp.dot(placement.T, table, preferred_element_type=jnp.float32)
-    payload = payload.astype(jnp.bfloat16).reshape(owner_count, 1, 1, 1, capacity * FIELDS)
+    payload = jnp.dot(table.T, placement, preferred_element_type=jnp.float32)
+    payload = payload.astype(jnp.bfloat16).reshape(FIELDS, owner_count, capacity)
+    payload = payload.transpose(1, 0, 2).reshape(owner_count, 1, 1, 1, capacity * FIELDS)
     payload = jnp.broadcast_to(payload, (owner_count, band_count, 1, 1, capacity * FIELDS))
     payload = payload.reshape(blocks, 1, 1, capacity * FIELDS)
     payload = jnp.concatenate([payload, jnp.zeros_like(payload)], axis=1)
     send = jnp.concatenate([windows, payload], axis=2)
     received = lax.all_to_all(send, ("ma", "band"), split_axis=0, concat_axis=0, tiled=True)
 
-    points_in = received[:, 0, window - lead].reshape(owner_count, band_count, capacity, FIELDS)
+    points_in = received[:, 0, window - lead].reshape(owner_count, band_count, capacity * FIELDS)
     points_in = lax.dynamic_index_in_dim(points_in, my_band, axis=1, keepdims=False)
-    points_in = points_in.reshape(owner_count * capacity, FIELDS).astype(jnp.float32)
+    points_in = points_in.reshape(owner_count, FIELDS, capacity).transpose(1, 0, 2)
+    points_in = points_in.reshape(FIELDS, owner_count * capacity).astype(jnp.float32)
 
     phase_rows = phase_table(m_values, NPHI, harmonics.shape[1])
     rows = jnp.einsum(
@@ -109,10 +111,10 @@
     )
     rows = (2.0 * rows).astype(jnp.bfloat16)
 
-    cycles_here = points_in[:, 0].astype(jnp.int32)
-    phis_here = points_in[:, 1].astype(jnp.int32)
-    offset_rows = points_in[:, 2] + (points_in[:, 3] + points_in[:, 4])
-    offset_cols = points_in[:, 5] + (points_in[:, 6] + points_in[:, 7])
+    cycles_here = points_in[0].astype(jnp.int32)
+    phis_here = points_in[1].astype(jnp.int32)
+    offset_rows = points_in[2] + (points_in[3] + points_in[4])
+    offset_cols = points_in[5] + (points_in[6] + points_in[7])
     tap_shift = jnp.arange(TAPS).astype(jnp.float32) - 3.0
     across = kernel_taps(tap_shift[None, :] - offset_rows[:, None])
     beside_all = kernel_taps(tap_shift[None, :] - offset_cols[:, None])

time: 57.8 us -> 56.5 us (0.978)
  local copies, waits for them, and re-layouts: 5.31 us -> 3.95 us
    unnamed x24 -> x17, local copies, waits for them, and re-layouts: 1.7 us -> 1.04 us
    another operation x1 -> x0, local copies, waits for them, and re-layouts: 0.61 us -> none  [on_device(): received[:, 0, window - lead]]
where the time goes in v12:
time: 56.5 us; the launch traced here: 56.3 us
  waiting for transfers between devices  16 us (28%)
  matrix products  11.3 us (20%)
  starting transfers between devices  11.2 us (20%)
  blocking collectives  10.4 us (18%)
  local copies, waits for them, and re-layouts  3.95 us (7%)
  other arithmetic  3.02 us (5%)
    all_to_all x1, waiting for transfers between devices, on_device(): lax.all_to_all(send, ('ma', 'band'), split_axis=0, concat_axis=0, tiled=T...  16 us
    all_to_all x1, starting transfers between devices, on_device(): lax.all_to_all(send, ('ma', 'band'), split_axis=0, concat_axis=0, tiled=T...  11.2 us
    all_to_all x1, blocking collectives, on_device(): lax.all_to_all(values, 'ma', split_axis=0, concat_axis=0, tiled=True)  10.4 us
    dot_general x1, matrix products, on_device(): lax.dot_general(legendre[0], harmonics[0], (((1,), (0,)), ((), ())), pref...  9.39 us
    concatenate x1, local copies, waits for them, and re-layouts, on_device(): send = jnp.concatenate([windows, payload], axis=2)  1.69 us
  transfers between devices with their start and end apart: 1, of which 1 were waited for; matrix products, arithmetic and copies ran while one was open for 1% of the time, Pallas kernels for 0%

profile of v12, /device:TPU:0, one launch (start us, length us, event | category | flops | bytes accessed | tf_op | source)
XLA Modules:
  0.0 56.3 jit_solution(3079812679778523202)
XLA Ops:
  0.0 9.4 %fusion = f32[2,512,256]{1,2,0:T(8,128)S(1)} fusion(bf16[1,2,8192,512]{3,2,1,0:T(8,128)(2,1)} %param.8, bf16[1,8192,256]{2,1,0:T(8,128)(2,1)} %param.7), kind=kOutput, calls=%fused_computation | convolution fusion | flops 4294967296 | bytes 22020096 | tf_op jit(solution)/shard_map/dot_general | solution.py:61
  9.5 0.1 copy.53
  9.7 0.1 copy.54
  9.8 0.1 copy.55
  10.0 0.1 copy.56
  10.1 0.1 copy.57
  10.2 0.1 copy.58
  10.4 0.1 copy.59
  10.5 0.1 copy.60
  10.8 0.4 fusion.154
  11.2 0.4 fusion.153
  11.6 0.2 fusion.14
  11.7 0.7 %maximum_bitcast_fusion = bf16[16,8,2,3,4,128]{5,4,1,0,2,3:T(4,128)(2,1)S(1)} fusion(bf16[8,16,1,4,2,128]{5,3,0,1,4,2:T(4,128)(2,1)S(1)} %get-tuple-element.21, bf16[8,16,1,4,2,128]{5,3,0,1,4,2:T(4,128)(2,1)S(1)} %fusion.153, bf16[8,16,1,4,2,128]{5,3,0,1,4,2:T(4,128)(2,1)S(1)} %get-tuple-element.20), kind=kLoop, calls=%fused_computation.13 | loop fusion | flops 786432 | bytes 1572864 | tf_op jit(solution)/shard_map/transpose | solution.py:76
  12.4 0.2 copy.43
  12.7 0.1 fusion.36
  12.8 0.2 reduce_window_sum.11
  13.0 0.2 select_reduce_fusion
  13.2 0.2 convolution_convert_fusion
  13.4 0.1 reshape.663
  13.5 0.1 broadcast_in_dim.156
  13.7 1.7 %copy.45 = bf16[128,2,12,128]{3,1,2,0:T(2,128)(2,1)} copy(bf16[128,2,12,128]{3,0,2,1:T(8,128)(2,1)S(1)} %fusion.8) | data formatting | bytes 1572864 | tf_op jit(solution)/shard_map/concatenate | solution.py:100
  15.4 11.2 %all-to-all-start = ((bf16[128,2,12,128]{3,1,2,0:T(2,128)(2,1)}), bf16[128,2,12,128]{3,1,2,0:T(2,128)(2,1)S(1)}, u32[]{:S(2)}, u32[]{:S(2)}) async-start(bf16[128,2,12,128]{3,1,2,0:T(2,128)(2,1)} %copy.45), calls=%async_computation | async-start | bytes 1572864 | tf_op jit(solution)/shard_map/all_to_all | solution.py:101
  26.6 0.3 cosine_convert_fusion
  26.9 16.0 %all-to-all-done = bf16[128,2,12,128]{3,1,2,0:T(2,128)(2,1)S(1)} async-done(((bf16[128,2,12,128]{3,1,2,0:T(2,128)(2,1)}), bf16[128,2,12,128]{3,1,2,0:T(2,128)(2,1)S(1)}, u32[]{:S(2)}, u32[]{:S(2)}) %all-to-all-start) | async-done | bytes 786464 | tf_op jit(solution)/shard_map/all_to_all | solution.py:101
  43.2 0.1 add.254
  43.3 0.1 add.264
  43.4 0.1 sub.184
  43.6 0.1 fusion.70
  43.8 0.4 select_add_fusion
  44.1 0.8 %fusion.7 = f32[256,128,1]{1,0,2:T(8,128)S(1)} fusion(bf16[128,2,12,128]{3,1,2,0:T(2,128)(2,1)S(1)} %all-to-all-done, f32[256,128]{1,0:T(8,128)S(1)} %select_add_fusion, f32[256,12]{0,1:T(8,128)S(1)} %select_add_fusion.1, bf16[128,128,1]{1,0,2:T(8,128)(2,1)S(1)} %get-tuple-element.45, bf16[128,128,1]{1,0,2:T(8,128)(2,1)S(1)} %get-tuple-element.44), kind=kOutput, calls=%fused_computation.10 | convolution fusion | flops 202539008 | bytes 1126400 | tf_op jit(solution)/shard_map/dot_general | solution.py:125
  45.0 10.4 %all_to_all.10 = f32[16,16,128]{2,1,0:T(8,128)S(1)} all-to-all(f32[16,16,128]{2,1,0:T(8,128)S(1)} %bitcast.108), channel_id=1, replica_groups=mesh['ma'=16,'band'=8] {'ma'}, dimensions={0} | all-to-all | bytes 262144 | tf_op jit(solution)/shard_map/all_to_all | solution.py:129
  55.4 0.9 %fusion.24 = f32[128,128]{1,0:T(8,128)} fusion(f32[256,128]{1,0:T(8,128)S(1)} %bitcast.105, s32[128]{0:T(128)S(1)} %multiply_add_fusion.4), kind=kOutput, calls=%fused_computation.38 | convolution fusion | flops 50364416 | bytes 197120 | tf_op jit(solution)/shard_map/dot_general | solution.py:133
  (34 shorter events, 0.9 us)
Async XLA Ops:
  10.7 1.9 %copy-start = (f32[2,128]{1,0:T(2,128)S(1)}, f32[2,128]{1,0:T(2,128)}, u32[]{:S(2)}) copy-start(f32[2,128]{1,0:T(2,128)} %param.12) | copy-start | bytes 3076
  10.7 1.9 %copy-start.2 = (s32[128]{0:T(128)S(1)}, s32[128]{0:T(128)}, u32[]{:S(2)}) copy-start(s32[128]{0:T(128)} %param.10) | copy-start | bytes 1540
  10.7 2.0 %copy-start.3 = (s32[128]{0:T(128)S(1)}, s32[128]{0:T(128)}, u32[]{:S(2)}) copy-start(s32[128]{0:T(128)} %param.11) | copy-start | bytes 1540
  12.4 14.2 %copy-start.1 = (s32[128]{0:T(128)S(1)}, s32[128]{0:T(128)}, u32[]{:S(2)}) copy-start(s32[128]{0:T(128)} %param.9) | copy-start | bytes 1540
  15.4 27.5 %all-to-all-start = ((bf16[128,2,12,128]{3,1,2,0:T(2,128)(2,1)}), bf16[128,2,12,128]{3,1,2,0:T(2,128)(2,1)S(1)}, u32[]{:S(2)}, u32[]{:S(2)}) async-start(bf16[128,2,12,128]{3,1,2,0:T(2,128)(2,1)} %copy.45), calls=%async_computation | async-start | bytes 1572864 | tf_op jit(solution)/shard_map/all_to_all | solution.py:101

commit v13 on v12

--- a/solution.py
+++ b/solution.py
@@ -1,6 +1,7 @@
 import jax
 import jax.numpy as jnp
 from jax import lax
+from jax.experimental.layout import Layout, with_layout_constraint
 from jax.sharding import PartitionSpec as P
 
 NPHI = 128
@@ -61,6 +62,7 @@
     both = lax.dot_general(
         legendre[0], harmonics[0], (((1,), (0,)), ((), ())), preferred_element_type=jnp.float32
     )
+    both = with_layout_constraint(both, Layout(major_to_minor=(0, 1, 2)))
     spectra = combine_parts(
         both[0].reshape(cycle_total, 2, 2, evolutions),
         both[1].reshape(cycle_total, 2, 2, evolutions),

time: 56.5 us -> 56.2 us (level)
    unnamed x17 -> x9, local copies, waits for them, and re-layouts: 1.04 us -> 0.03 us
where the time goes in v13:
time: 56.2 us; the launch traced here: 56 us
  waiting for transfers between devices  16 us (28%)
  matrix products  11.3 us (20%)
  starting transfers between devices  11.2 us (20%)
  blocking collectives  10.4 us (19%)
  local copies, waits for them, and re-layouts  3.75 us (7%)
  other arithmetic  2.99 us (5%)
    all_to_all x1, waiting for transfers between devices, on_device(): lax.all_to_all(send, ('ma', 'band'), split_axis=0, concat_axis=0, tiled=T...  16 us
    all_to_all x1, starting transfers between devices, on_device(): lax.all_to_all(send, ('ma', 'band'), split_axis=0, concat_axis=0, tiled=T...  11.2 us
    all_to_all x1, blocking collectives, on_device(): lax.all_to_all(values, 'ma', split_axis=0, concat_axis=0, tiled=True)  10.4 us
    dot_general x1, matrix products, on_device(): lax.dot_general(legendre[0], harmonics[0], (((1,), (0,)), ((), ())), pref...  9.37 us
    concatenate x1, local copies, waits for them, and re-layouts, on_device(): send = jnp.concatenate([windows, payload], axis=2)  1.69 us
  transfers between devices with their start and end apart: 1, of which 1 were waited for; matrix products, arithmetic and copies ran while one was open for 1% of the time, Pallas kernels for 0%

profile of v13, /device:TPU:0, one launch (start us, length us, event | category | flops | bytes accessed | tf_op | source)
XLA Modules:
  0.0 56.0 jit_solution(7715019075960467134)
XLA Ops:
  0.0 9.4 %fusion = f32[2,512,256]{2,1,0:T(8,128)S(1)} fusion(bf16[1,2,8192,512]{3,2,1,0:T(8,128)(2,1)} %param.8, bf16[1,8192,256]{2,1,0:T(8,128)(2,1)} %param.7), kind=kOutput, calls=%fused_computation | convolution fusion | flops 4294967296 | bytes 22020096 | tf_op jit(solution)/shard_map/dot_general | solution.py:62
  9.5 0.2 copy.31
  9.7 0.2 copy.32
  9.9 0.1 fusion.23
  10.0 0.1 copy.33
  10.1 0.1 copy.34
  10.3 0.1 copy.35
  10.4 0.1 copy.36
  10.5 0.4 fusion.160
  10.9 0.4 fusion.159
  11.3 0.2 fusion.14
  11.4 0.7 %maximum_bitcast_fusion = bf16[16,8,2,3,4,128]{5,4,1,0,2,3:T(4,128)(2,1)S(1)} fusion(bf16[8,16,1,4,2,128]{5,3,0,1,4,2:T(4,128)(2,1)S(1)} %get-tuple-element.17, bf16[8,16,1,4,2,128]{5,3,0,1,4,2:T(4,128)(2,1)S(1)} %fusion.159, bf16[8,16,1,4,2,128]{5,3,0,1,4,2:T(4,128)(2,1)S(1)} %get-tuple-element.16), kind=kLoop, calls=%fused_computation.13 | loop fusion | flops 786432 | bytes 1572864 | tf_op jit(solution)/shard_map/transpose | solution.py:78
  12.1 0.2 copy.37
  12.4 0.1 fusion.44
  12.5 0.2 reduce_window_sum.11
  12.7 0.2 select_reduce_fusion
  12.9 0.2 convolution_convert_fusion
  13.1 0.1 reshape.663
  13.2 0.1 broadcast_in_dim.156
  13.4 1.7 %copy.39 = bf16[128,2,12,128]{3,1,2,0:T(2,128)(2,1)} copy(bf16[128,2,12,128]{3,0,2,1:T(8,128)(2,1)S(1)} %fusion.8) | data formatting | bytes 1572864 | tf_op jit(solution)/shard_map/concatenate | solution.py:102
  15.1 11.2 %all-to-all-start = ((bf16[128,2,12,128]{3,1,2,0:T(2,128)(2,1)}), bf16[128,2,12,128]{3,1,2,0:T(2,128)(2,1)S(1)}, u32[]{:S(2)}, u32[]{:S(2)}) async-start(bf16[128,2,12,128]{3,1,2,0:T(2,128)(2,1)} %copy.39), calls=%async_computation | async-start | bytes 1572864 | tf_op jit(solution)/shard_map/all_to_all | solution.py:103
  26.3 0.3 cosine_convert_fusion
  26.6 16.0 %all-to-all-done = bf16[128,2,12,128]{3,1,2,0:T(2,128)(2,1)S(1)} async-done(((bf16[128,2,12,128]{3,1,2,0:T(2,128)(2,1)}), bf16[128,2,12,128]{3,1,2,0:T(2,128)(2,1)S(1)}, u32[]{:S(2)}, u32[]{:S(2)}) %all-to-all-start) | async-done | bytes 786464 | tf_op jit(solution)/shard_map/all_to_all | solution.py:103
  42.8 0.1 fusion.147
  42.9 0.1 add.254
  43.1 0.1 sub.184
  43.2 0.1 sub.193
  43.3 0.1 fusion.78
  43.5 0.4 select_add_fusion
  43.8 0.8 %fusion.7 = f32[256,128,1]{1,0,2:T(8,128)S(1)} fusion(bf16[128,2,12,128]{3,1,2,0:T(2,128)(2,1)S(1)} %all-to-all-done, f32[256,128]{1,0:T(8,128)S(1)} %select_add_fusion, f32[256,12]{0,1:T(8,128)S(1)} %select_add_fusion.1, bf16[128,128,1]{1,0,2:T(8,128)(2,1)S(1)} %get-tuple-element.41, bf16[128,128,1]{1,0,2:T(8,128)(2,1)S(1)} %get-tuple-element.40), kind=kOutput, calls=%fused_computation.10 | convolution fusion | flops 202539008 | bytes 1126400 | tf_op jit(solution)/shard_map/dot_general | solution.py:127
  44.6 10.4 %all_to_all.10 = f32[16,16,128]{2,1,0:T(8,128)S(1)} all-to-all(f32[16,16,128]{2,1,0:T(8,128)S(1)} %bitcast.107), channel_id=1, replica_groups=mesh['ma'=16,'band'=8] {'ma'}, dimensions={0} | all-to-all | bytes 262144 | tf_op jit(solution)/shard_map/all_to_all | solution.py:131
  55.1 0.9 %fusion.32 = f32[128,128]{1,0:T(8,128)} fusion(f32[256,128]{1,0:T(8,128)S(1)} %bitcast.104, s32[128]{0:T(128)S(1)} %multiply_add_fusion.4), kind=kOutput, calls=%fused_computation.46 | convolution fusion | flops 50364416 | bytes 197120 | tf_op jit(solution)/shard_map/dot_general | solution.py:135
  (27 shorter events, 0.7 us)
Async XLA Ops:
  10.0 2.4 %copy-start = (f32[2,128]{1,0:T(2,128)S(1)}, f32[2,128]{1,0:T(2,128)}, u32[]{:S(2)}) copy-start(f32[2,128]{1,0:T(2,128)} %param.12) | copy-start | bytes 3076
  10.0 2.4 %copy-start.2 = (s32[128]{0:T(128)S(1)}, s32[128]{0:T(128)}, u32[]{:S(2)}) copy-start(s32[128]{0:T(128)} %param.10) | copy-start | bytes 1540
  10.0 2.4 %copy-start.3 = (s32[128]{0:T(128)S(1)}, s32[128]{0:T(128)}, u32[]{:S(2)}) copy-start(s32[128]{0:T(128)} %param.11) | copy-start | bytes 1540
  12.1 14.2 %copy-start.1 = (s32[128]{0:T(128)S(1)}, s32[128]{0:T(128)}, u32[]{:S(2)}) copy-start(s32[128]{0:T(128)} %param.9) | copy-start | bytes 1540
  15.1 27.5 %all-to-all-start = ((bf16[128,2,12,128]{3,1,2,0:T(2,128)(2,1)}), bf16[128,2,12,128]{3,1,2,0:T(2,128)(2,1)S(1)}, u32[]{:S(2)}, u32[]{:S(2)}) async-start(bf16[128,2,12,128]{3,1,2,0:T(2,128)(2,1)} %copy.39), calls=%async_computation | async-start | bytes 1572864 | tf_op jit(solution)/shard_map/all_to_all | solution.py:103

commit v14 on v12

--- a/solution.py
+++ b/solution.py
@@ -74,7 +74,6 @@
         [padded[:, s : s + owner_count] for s in range(3)], axis=2
     )
     windows = windows.transpose(1, 0, 4, 2, 3, 5).reshape(blocks, 2, window, width_out)
-    windows = windows[:, :, lead:]
 
     owner_index = cycle_cell // cycle_depth
     one_hot = (owner_index[:, None] == jnp.arange(owner_count, dtype=jnp.int32)[None, :]).astype(
@@ -97,10 +96,10 @@
     payload = jnp.broadcast_to(payload, (owner_count, band_count, 1, 1, capacity * FIELDS))
     payload = payload.reshape(blocks, 1, 1, capacity * FIELDS)
     payload = jnp.concatenate([payload, jnp.zeros_like(payload)], axis=1)
-    send = jnp.concatenate([windows, payload], axis=2)
+    send = windows.at[:, :, :lead].set(payload)
     received = lax.all_to_all(send, ("ma", "band"), split_axis=0, concat_axis=0, tiled=True)
 
-    points_in = received[:, 0, window - lead].reshape(owner_count, band_count, capacity * FIELDS)
+    points_in = received[:, 0, 0].reshape(owner_count, band_count, capacity * FIELDS)
     points_in = lax.dynamic_index_in_dim(points_in, my_band, axis=1, keepdims=False)
     points_in = points_in.reshape(owner_count, FIELDS, capacity).transpose(1, 0, 2)
     points_in = points_in.reshape(FIELDS, owner_count * capacity).astype(jnp.float32)
@@ -118,7 +117,7 @@
     tap_shift = jnp.arange(TAPS).astype(jnp.float32) - 3.0
     across = kernel_taps(tap_shift[None, :] - offset_rows[:, None])
     beside_all = kernel_taps(tap_shift[None, :] - offset_cols[:, None])
-    first_row = (me - 1) * cycle_depth + lead
+    first_row = (me - 1) * cycle_depth
     cycle_weights = spread_weights(cycles_here - 3 - first_row, across, window)
     phi_weights = spread_weights(phis_here - 3, beside_all, NPHI)
     dense = (cycle_weights[:, :, None] * phi_weights[:, None, :]).astype(jnp.bfloat16)

time: 56.5 us -> 56.4 us (level)
    scatter x0 -> x2, local copies, waits for them, and re-layouts: none -> 1.7 us  [on_device(): send = windows.at[:, :, :lead].set(payload)]
    concatenate x1 -> x0, local copies, waits for them, and re-layouts: 1.69 us -> none  [on_device(): send = jnp.concatenate([windows, payload], axis=2)]
where the time goes in v14:
time: 56.4 us; the launch traced here: 56.2 us
  waiting for transfers between devices  16 us (28%)
  matrix products  11.3 us (20%)
  starting transfers between devices  11.2 us (20%)
  blocking collectives  10.4 us (18%)
  local copies, waits for them, and re-layouts  3.91 us (7%)
  other arithmetic  2.95 us (5%)
    all_to_all x1, waiting for transfers between devices, on_device(): lax.all_to_all(send, ('ma', 'band'), split_axis=0, concat_axis=0, tiled=T...  16 us
    all_to_all x1, starting transfers between devices, on_device(): lax.all_to_all(send, ('ma', 'band'), split_axis=0, concat_axis=0, tiled=T...  11.2 us
    all_to_all x1, blocking collectives, on_device(): lax.all_to_all(values, 'ma', split_axis=0, concat_axis=0, tiled=True)  10.4 us
    dot_general x1, matrix products, on_device(): lax.dot_general(legendre[0], harmonics[0], (((1,), (0,)), ((), ())), pref...  9.39 us
    scatter x2, local copies, waits for them, and re-layouts, on_device(): send = windows.at[:, :, :lead].set(payload)  1.7 us
  transfers between devices with their start and end apart: 1, of which 1 were waited for; matrix products, arithmetic and copies ran while one was open for 1% of the time, Pallas kernels for 0%

profile of v14, /device:TPU:0, one launch (start us, length us, event | category | flops | bytes accessed | tf_op | source)
XLA Modules:
  0.0 56.2 jit_solution(7922656372349314919)
XLA Ops:
  0.0 9.4 %fusion = f32[2,512,256]{1,2,0:T(8,128)S(1)} fusion(bf16[1,2,8192,512]{3,2,1,0:T(8,128)(2,1)} %param.10, bf16[1,8192,256]{2,1,0:T(8,128)(2,1)} %param.9), kind=kOutput, calls=%fused_computation | convolution fusion | flops 4294967296 | bytes 22020096 | tf_op jit(solution)/shard_map/dot_general | solution.py:61
  9.5 0.1 copy.53
  9.7 0.1 copy.54
  9.8 0.1 copy.55
  10.0 0.1 copy.56
  10.1 0.1 copy.57
  10.2 0.1 copy.58
  10.4 0.1 copy.59
  10.5 0.1 copy.60
  10.8 0.4 fusion.152
  11.2 0.4 fusion.151
  11.6 0.2 fusion.12
  11.7 0.7 %maximum_bitcast_fusion = bf16[16,8,2,3,4,128]{5,4,1,0,2,3:T(4,128)(2,1)S(1)} fusion(bf16[8,16,1,4,2,128]{5,3,0,1,4,2:T(4,128)(2,1)S(1)} %get-tuple-element.33, bf16[8,16,1,4,2,128]{5,3,0,1,4,2:T(4,128)(2,1)S(1)} %fusion.151, bf16[8,16,1,4,2,128]{5,3,0,1,4,2:T(4,128)(2,1)S(1)} %get-tuple-element.32), kind=kLoop, calls=%fused_computation.10 | loop fusion | flops 786432 | bytes 1572864 | tf_op jit(solution)/shard_map/transpose | solution.py:76
  12.4 0.2 copy.43
  12.7 0.1 fusion.34
  12.7 0.2 reduce_window_sum.11
  12.9 0.2 select_reduce_fusion
  13.1 0.2 convolution_convert_fusion
  13.3 0.1 reshape.700
  13.5 0.1 broadcast_in_dim.156
  13.6 1.7 %copy.45 = bf16[128,2,12,128]{3,1,2,0:T(2,128)(2,1)} copy(bf16[128,2,12,128]{3,0,2,1:T(8,128)(2,1)S(1)} %pad_dynamic-update-slice_fusion) | data formatting | bytes 1572864 | tf_op jit(solution)/shard_map/scatter | solution.py:99
  15.3 11.2 %all-to-all-start = ((bf16[128,2,12,128]{3,1,2,0:T(2,128)(2,1)}), bf16[128,2,12,128]{3,1,2,0:T(2,128)(2,1)S(1)}, u32[]{:S(2)}, u32[]{:S(2)}) async-start(bf16[128,2,12,128]{3,1,2,0:T(2,128)(2,1)} %copy.45), calls=%async_computation | async-start | bytes 1572864 | tf_op jit(solution)/shard_map/all_to_all | solution.py:100
  26.5 0.3 cosine_convert_fusion
  26.8 16.0 %all-to-all-done = bf16[128,2,12,128]{3,1,2,0:T(2,128)(2,1)S(1)} async-done(((bf16[128,2,12,128]{3,1,2,0:T(2,128)(2,1)}), bf16[128,2,12,128]{3,1,2,0:T(2,128)(2,1)S(1)}, u32[]{:S(2)}, u32[]{:S(2)}) %all-to-all-start) | async-done | bytes 786464 | tf_op jit(solution)/shard_map/all_to_all | solution.py:100
  43.1 0.1 add.252
  43.2 0.1 add.262
  43.3 0.1 sub.184
  43.5 0.1 fusion.68
  43.6 0.4 select_add_fusion
  44.0 0.8 %fusion.6 = f32[256,128,1]{1,0,2:T(8,128)S(1)} fusion(bf16[128,2,12,128]{3,1,2,0:T(2,128)(2,1)S(1)} %all-to-all-done, f32[256,128]{1,0:T(8,128)S(1)} %select_add_fusion, f32[256,12]{0,1:T(8,128)S(1)} %select_add_fusion.1, bf16[128,128,1]{1,0,2:T(8,128)(2,1)S(1)} %get-tuple-element.57, bf16[128,128,1]{1,0,2:T(8,128)(2,1)S(1)} %get-tuple-element.56), kind=kOutput, calls=%fused_computation.8 | convolution fusion | flops 202539008 | bytes 1126400 | tf_op jit(solution)/shard_map/dot_general | solution.py:124
  44.8 10.4 %all_to_all.10 = f32[16,16,128]{2,1,0:T(8,128)S(1)} all-to-all(f32[16,16,128]{2,1,0:T(8,128)S(1)} %bitcast.108), channel_id=1, replica_groups=mesh['ma'=16,'band'=8] {'ma'}, dimensions={0} | all-to-all | bytes 262144 | tf_op jit(solution)/shard_map/all_to_all | solution.py:128
  55.3 0.9 %fusion.22 = f32[128,128]{1,0:T(8,128)} fusion(f32[256,128]{1,0:T(8,128)S(1)} %bitcast.105, s32[128]{0:T(128)S(1)} %multiply_add_fusion.4), kind=kOutput, calls=%fused_computation.35 | convolution fusion | flops 50364416 | bytes 197120 | tf_op jit(solution)/shard_map/dot_general | solution.py:132
  (33 shorter events, 0.8 us)
Async XLA Ops:
  10.5 2.1 %copy-start = (f32[2,128]{1,0:T(2,128)S(1)}, f32[2,128]{1,0:T(2,128)}, u32[]{:S(2)}) copy-start(f32[2,128]{1,0:T(2,128)} %param.14) | copy-start | bytes 3076
  10.5 2.1 %copy-start.2 = (s32[128]{0:T(128)S(1)}, s32[128]{0:T(128)}, u32[]{:S(2)}) copy-start(s32[128]{0:T(128)} %param.12) | copy-start | bytes 1540
  10.5 2.1 %copy-start.3 = (s32[128]{0:T(128)S(1)}, s32[128]{0:T(128)}, u32[]{:S(2)}) copy-start(s32[128]{0:T(128)} %param.13) | copy-start | bytes 1540
  11.2 15.3 %copy-start.1 = (s32[128]{0:T(128)S(1)}, s32[128]{0:T(128)}, u32[]{:S(2)}) copy-start(s32[128]{0:T(128)} %param.11) | copy-start | bytes 1540
  15.3 27.5 %all-to-all-start = ((bf16[128,2,12,128]{3,1,2,0:T(2,128)(2,1)}), bf16[128,2,12,128]{3,1,2,0:T(2,128)(2,1)S(1)}, u32[]{:S(2)}, u32[]{:S(2)}) async-start(bf16[128,2,12,128]{3,1,2,0:T(2,128)(2,1)} %copy.45), calls=%async_computation | async-start | bytes 1572864 | tf_op jit(solution)/shard_map/all_to_all | solution.py:100

commit v15 on v14

--- a/solution.py
+++ b/solution.py
@@ -1,6 +1,7 @@
 import jax
 import jax.numpy as jnp
 from jax import lax
+from jax.experimental.layout import Layout, with_layout_constraint
 from jax.sharding import PartitionSpec as P
 
 NPHI = 128
@@ -61,6 +62,7 @@
     both = lax.dot_general(
         legendre[0], harmonics[0], (((1,), (0,)), ((), ())), preferred_element_type=jnp.float32
     )
+    both = with_layout_constraint(both, Layout(major_to_minor=(0, 1, 2)))
     spectra = combine_parts(
         both[0].reshape(cycle_total, 2, 2, evolutions),
         both[1].reshape(cycle_total, 2, 2, evolutions),

time: 56.4 us -> 56.1 us (level)
    unnamed x17 -> x9, local copies, waits for them, and re-layouts: 1.03 us -> 0.03 us
where the time goes in v15:
time: 56.1 us; the launch traced here: 55.9 us
  waiting for transfers between devices  16 us (29%)
  matrix products  11.3 us (20%)
  starting transfers between devices  11.2 us (20%)
  blocking collectives  10.4 us (19%)
  local copies, waits for them, and re-layouts  3.71 us (7%)
  other arithmetic  2.92 us (5%)
    all_to_all x1, waiting for transfers between devices, on_device(): lax.all_to_all(send, ('ma', 'band'), split_axis=0, concat_axis=0, tiled=T...  16 us
    all_to_all x1, starting transfers between devices, on_device(): lax.all_to_all(send, ('ma', 'band'), split_axis=0, concat_axis=0, tiled=T...  11.2 us
    all_to_all x1, blocking collectives, on_device(): lax.all_to_all(values, 'ma', split_axis=0, concat_axis=0, tiled=True)  10.4 us
    dot_general x1, matrix products, on_device(): lax.dot_general(legendre[0], harmonics[0], (((1,), (0,)), ((), ())), pref...  9.37 us
    scatter x2, local copies, waits for them, and re-layouts, on_device(): send = windows.at[:, :, :lead].set(payload)  1.7 us
  transfers between devices with their start and end apart: 1, of which 1 were waited for; matrix products, arithmetic and copies ran while one was open for 1% of the time, Pallas kernels for 0%

profile of v15, /device:TPU:0, one launch (start us, length us, event | category | flops | bytes accessed | tf_op | source)
XLA Modules:
  0.0 55.9 jit_solution(15072851640391172723)
XLA Ops:
  0.0 9.4 %fusion = f32[2,512,256]{2,1,0:T(8,128)S(1)} fusion(bf16[1,2,8192,512]{3,2,1,0:T(8,128)(2,1)} %param.10, bf16[1,8192,256]{2,1,0:T(8,128)(2,1)} %param.9), kind=kOutput, calls=%fused_computation | convolution fusion | flops 4294967296 | bytes 22020096 | tf_op jit(solution)/shard_map/dot_general | solution.py:62
  9.5 0.2 copy.31
  9.7 0.2 copy.32
  9.9 0.1 fusion.21
  10.0 0.1 copy.33
  10.1 0.1 copy.34
  10.3 0.1 copy.35
  10.4 0.1 copy.36
  10.5 0.4 fusion.158
  10.9 0.4 fusion.157
  11.3 0.2 fusion.12
  11.4 0.7 %maximum_bitcast_fusion = bf16[16,8,2,3,4,128]{5,4,1,0,2,3:T(4,128)(2,1)S(1)} fusion(bf16[8,16,1,4,2,128]{5,3,0,1,4,2:T(4,128)(2,1)S(1)} %get-tuple-element.29, bf16[8,16,1,4,2,128]{5,3,0,1,4,2:T(4,128)(2,1)S(1)} %fusion.157, bf16[8,16,1,4,2,128]{5,3,0,1,4,2:T(4,128)(2,1)S(1)} %get-tuple-element.28), kind=kLoop, calls=%fused_computation.10 | loop fusion | flops 786432 | bytes 1572864 | tf_op jit(solution)/shard_map/transpose | solution.py:78
  12.1 0.2 copy.37
  12.4 0.1 fusion.42
  12.4 0.2 reduce_window_sum.11
  12.6 0.2 select_reduce_fusion
  12.8 0.2 convolution_convert_fusion
  13.0 0.1 reshape.700
  13.2 0.1 broadcast_in_dim.156
  13.3 1.7 %copy.39 = bf16[128,2,12,128]{3,1,2,0:T(2,128)(2,1)} copy(bf16[128,2,12,128]{3,0,2,1:T(8,128)(2,1)S(1)} %pad_dynamic-update-slice_fusion) | data formatting | bytes 1572864 | tf_op jit(solution)/shard_map/scatter | solution.py:101
  15.0 11.2 %all-to-all-start = ((bf16[128,2,12,128]{3,1,2,0:T(2,128)(2,1)}), bf16[128,2,12,128]{3,1,2,0:T(2,128)(2,1)S(1)}, u32[]{:S(2)}, u32[]{:S(2)}) async-start(bf16[128,2,12,128]{3,1,2,0:T(2,128)(2,1)} %copy.39), calls=%async_computation | async-start | bytes 1572864 | tf_op jit(solution)/shard_map/all_to_all | solution.py:102
  26.2 0.3 cosine_convert_fusion
  26.5 16.0 %all-to-all-done = bf16[128,2,12,128]{3,1,2,0:T(2,128)(2,1)S(1)} async-done(((bf16[128,2,12,128]{3,1,2,0:T(2,128)(2,1)}), bf16[128,2,12,128]{3,1,2,0:T(2,128)(2,1)S(1)}, u32[]{:S(2)}, u32[]{:S(2)}) %all-to-all-start) | async-done | bytes 786464 | tf_op jit(solution)/shard_map/all_to_all | solution.py:102
  42.7 0.1 fusion.145
  42.8 0.1 add.252
  42.8 0.1 add.262
  43.0 0.1 sub.184
  43.2 0.1 fusion.76
  43.3 0.4 select_add_fusion
  43.7 0.8 %fusion.6 = f32[256,128,1]{1,0,2:T(8,128)S(1)} fusion(bf16[128,2,12,128]{3,1,2,0:T(2,128)(2,1)S(1)} %all-to-all-done, f32[256,128]{1,0:T(8,128)S(1)} %select_add_fusion, f32[256,12]{0,1:T(8,128)S(1)} %select_add_fusion.1, bf16[128,128,1]{1,0,2:T(8,128)(2,1)S(1)} %get-tuple-element.53, bf16[128,128,1]{1,0,2:T(8,128)(2,1)S(1)} %get-tuple-element.52), kind=kOutput, calls=%fused_computation.8 | convolution fusion | flops 202539008 | bytes 1126400 | tf_op jit(solution)/shard_map/dot_general | solution.py:126
  44.5 10.4 %all_to_all.10 = f32[16,16,128]{2,1,0:T(8,128)S(1)} all-to-all(f32[16,16,128]{2,1,0:T(8,128)S(1)} %bitcast.107), channel_id=1, replica_groups=mesh['ma'=16,'band'=8] {'ma'}, dimensions={0} | all-to-all | bytes 262144 | tf_op jit(solution)/shard_map/all_to_all | solution.py:130
  55.0 0.9 %fusion.30 = f32[128,128]{1,0:T(8,128)} fusion(f32[256,128]{1,0:T(8,128)S(1)} %bitcast.104, s32[128]{0:T(128)S(1)} %multiply_add_fusion.4), kind=kOutput, calls=%fused_computation.43 | convolution fusion | flops 50364416 | bytes 197120 | tf_op jit(solution)/shard_map/dot_general | solution.py:134
  (26 shorter events, 0.5 us)
Async XLA Ops:
  9.7 2.6 %copy-start = (f32[2,128]{1,0:T(2,128)S(1)}, f32[2,128]{1,0:T(2,128)}, u32[]{:S(2)}) copy-start(f32[2,128]{1,0:T(2,128)} %param.14) | copy-start | bytes 3076
  9.7 2.6 %copy-start.2 = (s32[128]{0:T(128)S(1)}, s32[128]{0:T(128)}, u32[]{:S(2)}) copy-start(s32[128]{0:T(128)} %param.12) | copy-start | bytes 1540
  9.7 2.7 %copy-start.3 = (s32[128]{0:T(128)S(1)}, s32[128]{0:T(128)}, u32[]{:S(2)}) copy-start(s32[128]{0:T(128)} %param.13) | copy-start | bytes 1540
  10.9 15.3 %copy-start.1 = (s32[128]{0:T(128)S(1)}, s32[128]{0:T(128)}, u32[]{:S(2)}) copy-start(s32[128]{0:T(128)} %param.11) | copy-start | bytes 1540
  15.0 27.5 %all-to-all-start = ((bf16[128,2,12,128]{3,1,2,0:T(2,128)(2,1)}), bf16[128,2,12,128]{3,1,2,0:T(2,128)(2,1)S(1)}, u32[]{:S(2)}, u32[]{:S(2)}) async-start(bf16[128,2,12,128]{3,1,2,0:T(2,128)(2,1)} %copy.39), calls=%async_computation | async-start | bytes 1572864 | tf_op jit(solution)/shard_map/all_to_all | solution.py:102

commit v16 on v15

--- a/solution.py
+++ b/solution.py
@@ -134,7 +134,7 @@
     return jnp.dot(
         pick,
         returned.reshape(owner_count * capacity, width_out),
-        precision=lax.Precision.HIGHEST,
+        precision=lax.Precision.HIGH,
     )
 
 

time: 56.1 us -> 56 us (level)
  no operation moved by 1% of the time
where the time goes in v16:
time: 56 us; the launch traced here: 55.8 us
  waiting for transfers between devices  16 us (29%)
  matrix products  11.2 us (20%)
  starting transfers between devices  11.2 us (20%)
  blocking collectives  10.4 us (19%)
  local copies, waits for them, and re-layouts  3.71 us (7%)
  other arithmetic  2.92 us (5%)
    all_to_all x1, waiting for transfers between devices, on_device(): lax.all_to_all(send, ('ma', 'band'), split_axis=0, concat_axis=0, tiled=T...  16 us
    all_to_all x1, starting transfers between devices, on_device(): lax.all_to_all(send, ('ma', 'band'), split_axis=0, concat_axis=0, tiled=T...  11.2 us
    all_to_all x1, blocking collectives, on_device(): lax.all_to_all(values, 'ma', split_axis=0, concat_axis=0, tiled=True)  10.4 us
    dot_general x1, matrix products, on_device(): lax.dot_general(legendre[0], harmonics[0], (((1,), (0,)), ((), ())), pref...  9.37 us
    scatter x2, local copies, waits for them, and re-layouts, on_device(): send = windows.at[:, :, :lead].set(payload)  1.7 us
  transfers between devices with their start and end apart: 1, of which 1 were waited for; matrix products, arithmetic and copies ran while one was open for 1% of the time, Pallas kernels for 0%

profile of v16, /device:TPU:0, one launch (start us, length us, event | category | flops | bytes accessed | tf_op | source)
XLA Modules:
  0.0 55.8 jit_solution(13297417588471964866)
XLA Ops:
  0.0 9.4 %fusion = f32[2,512,256]{2,1,0:T(8,128)S(1)} fusion(bf16[1,2,8192,512]{3,2,1,0:T(8,128)(2,1)} %param.10, bf16[1,8192,256]{2,1,0:T(8,128)(2,1)} %param.9), kind=kOutput, calls=%fused_computation | convolution fusion | flops 4294967296 | bytes 22020096 | tf_op jit(solution)/shard_map/dot_general | solution.py:62
  9.5 0.2 copy.31
  9.7 0.2 copy.32
  9.9 0.1 fusion.21
  10.0 0.1 copy.33
  10.1 0.1 copy.34
  10.3 0.1 copy.35
  10.4 0.1 copy.36
  10.5 0.4 fusion.158
  10.9 0.4 fusion.157
  11.3 0.2 fusion.12
  11.4 0.7 %maximum_bitcast_fusion = bf16[16,8,2,3,4,128]{5,4,1,0,2,3:T(4,128)(2,1)S(1)} fusion(bf16[8,16,1,4,2,128]{5,3,0,1,4,2:T(4,128)(2,1)S(1)} %get-tuple-element.29, bf16[8,16,1,4,2,128]{5,3,0,1,4,2:T(4,128)(2,1)S(1)} %fusion.157, bf16[8,16,1,4,2,128]{5,3,0,1,4,2:T(4,128)(2,1)S(1)} %get-tuple-element.28), kind=kLoop, calls=%fused_computation.10 | loop fusion | flops 786432 | bytes 1572864 | tf_op jit(solution)/shard_map/transpose | solution.py:78
  12.1 0.2 copy.37
  12.4 0.1 fusion.42
  12.4 0.2 reduce_window_sum.11
  12.6 0.2 select_reduce_fusion
  12.8 0.2 convolution_convert_fusion
  13.0 0.1 reshape.700
  13.2 0.1 broadcast_in_dim.156
  13.3 1.7 %copy.39 = bf16[128,2,12,128]{3,1,2,0:T(2,128)(2,1)} copy(bf16[128,2,12,128]{3,0,2,1:T(8,128)(2,1)S(1)} %pad_dynamic-update-slice_fusion) | data formatting | bytes 1572864 | tf_op jit(solution)/shard_map/scatter | solution.py:101
  15.0 11.2 %all-to-all-start = ((bf16[128,2,12,128]{3,1,2,0:T(2,128)(2,1)}), bf16[128,2,12,128]{3,1,2,0:T(2,128)(2,1)S(1)}, u32[]{:S(2)}, u32[]{:S(2)}) async-start(bf16[128,2,12,128]{3,1,2,0:T(2,128)(2,1)} %copy.39), calls=%async_computation | async-start | bytes 1572864 | tf_op jit(solution)/shard_map/all_to_all | solution.py:102
  26.2 0.3 cosine_convert_fusion
  26.5 16.0 %all-to-all-done = bf16[128,2,12,128]{3,1,2,0:T(2,128)(2,1)S(1)} async-done(((bf16[128,2,12,128]{3,1,2,0:T(2,128)(2,1)}), bf16[128,2,12,128]{3,1,2,0:T(2,128)(2,1)S(1)}, u32[]{:S(2)}, u32[]{:S(2)}) %all-to-all-start) | async-done | bytes 786464 | tf_op jit(solution)/shard_map/all_to_all | solution.py:102
  42.7 0.1 fusion.145
  42.8 0.1 add.252
  42.8 0.1 add.262
  43.0 0.1 sub.184
  43.2 0.1 fusion.76
  43.3 0.4 select_add_fusion
  43.7 0.8 %fusion.6 = f32[256,128,1]{1,0,2:T(8,128)S(1)} fusion(bf16[128,2,12,128]{3,1,2,0:T(2,128)(2,1)S(1)} %all-to-all-done, f32[256,128]{1,0:T(8,128)S(1)} %select_add_fusion, f32[256,12]{0,1:T(8,128)S(1)} %select_add_fusion.1, bf16[128,128,1]{1,0,2:T(8,128)(2,1)S(1)} %get-tuple-element.53, bf16[128,128,1]{1,0,2:T(8,128)(2,1)S(1)} %get-tuple-element.52), kind=kOutput, calls=%fused_computation.8 | convolution fusion | flops 202539008 | bytes 1126400 | tf_op jit(solution)/shard_map/dot_general | solution.py:126
  44.5 10.4 %all_to_all.10 = f32[16,16,128]{2,1,0:T(8,128)S(1)} all-to-all(f32[16,16,128]{2,1,0:T(8,128)S(1)} %bitcast.107), channel_id=1, replica_groups=mesh['ma'=16,'band'=8] {'ma'}, dimensions={0} | all-to-all | bytes 262144 | tf_op jit(solution)/shard_map/all_to_all | solution.py:130
  55.0 0.9 %fusion.30 = f32[128,128]{1,0:T(8,128)} fusion(f32[256,128]{1,0:T(8,128)S(1)} %bitcast.104, s32[128]{0:T(128)S(1)} %multiply_add_fusion.4), kind=kOutput, calls=%fused_computation.43 | convolution fusion | flops 25198592 | bytes 197120 | tf_op jit(solution)/shard_map/dot_general | solution.py:134
  (26 shorter events, 0.5 us)
Async XLA Ops:
  9.7 2.6 %copy-start = (f32[2,128]{1,0:T(2,128)S(1)}, f32[2,128]{1,0:T(2,128)}, u32[]{:S(2)}) copy-start(f32[2,128]{1,0:T(2,128)} %param.14) | copy-start | bytes 3076
  9.7 2.6 %copy-start.2 = (s32[128]{0:T(128)S(1)}, s32[128]{0:T(128)}, u32[]{:S(2)}) copy-start(s32[128]{0:T(128)} %param.12) | copy-start | bytes 1540
  9.7 2.7 %copy-start.3 = (s32[128]{0:T(128)S(1)}, s32[128]{0:T(128)}, u32[]{:S(2)}) copy-start(s32[128]{0:T(128)} %param.13) | copy-start | bytes 1540
  10.9 15.3 %copy-start.1 = (s32[128]{0:T(128)S(1)}, s32[128]{0:T(128)}, u32[]{:S(2)}) copy-start(s32[128]{0:T(128)} %param.11) | copy-start | bytes 1540
  15.0 27.5 %all-to-all-start = ((bf16[128,2,12,128]{3,1,2,0:T(2,128)(2,1)}), bf16[128,2,12,128]{3,1,2,0:T(2,128)(2,1)S(1)}, u32[]{:S(2)}, u32[]{:S(2)}) async-start(bf16[128,2,12,128]{3,1,2,0:T(2,128)(2,1)} %copy.39), calls=%async_computation | async-start | bytes 1572864 | tf_op jit(solution)/shard_map/all_to_all | solution.py:102

commit v17 on v15

--- a/solution.py
+++ b/solution.py
@@ -97,8 +97,7 @@
     payload = payload.transpose(1, 0, 2).reshape(owner_count, 1, 1, 1, capacity * FIELDS)
     payload = jnp.broadcast_to(payload, (owner_count, band_count, 1, 1, capacity * FIELDS))
     payload = payload.reshape(blocks, 1, 1, capacity * FIELDS)
-    payload = jnp.concatenate([payload, jnp.zeros_like(payload)], axis=1)
-    send = windows.at[:, :, :lead].set(payload)
+    send = windows.at[:, :1, :lead].set(payload)
     received = lax.all_to_all(send, ("ma", "band"), split_axis=0, concat_axis=0, tiled=True)
 
     points_in = received[:, 0, 0].reshape(owner_count, band_count, capacity * FIELDS)

time: 56.1 us -> 56 us (level)
  no operation moved by 1% of the time
where the time goes in v17:
time: 56 us; the launch traced here: 55.9 us
  waiting for transfers between devices  16 us (29%)
  matrix products  11.3 us (20%)
  starting transfers between devices  11.2 us (20%)
  blocking collectives  10.4 us (19%)
  local copies, waits for them, and re-layouts  3.7 us (7%)
  other arithmetic  2.92 us (5%)
    all_to_all x1, waiting for transfers between devices, on_device(): lax.all_to_all(send, ('ma', 'band'), split_axis=0, concat_axis=0, tiled=T...  16 us
    all_to_all x1, starting transfers between devices, on_device(): lax.all_to_all(send, ('ma', 'band'), split_axis=0, concat_axis=0, tiled=T...  11.2 us
    all_to_all x1, blocking collectives, on_device(): lax.all_to_all(values, 'ma', split_axis=0, concat_axis=0, tiled=True)  10.4 us
    dot_general x1, matrix products, on_device(): lax.dot_general(legendre[0], harmonics[0], (((1,), (0,)), ((), ())), pref...  9.37 us
    scatter x2, local copies, waits for them, and re-layouts, on_device(): send = windows.at[:, :1, :lead].set(payload)  1.7 us
  transfers between devices with their start and end apart: 1, of which 1 were waited for; matrix products, arithmetic and copies ran while one was open for 1% of the time, Pallas kernels for 0%

profile of v17, /device:TPU:0, one launch (start us, length us, event | category | flops | bytes accessed | tf_op | source)
XLA Modules:
  0.0 55.9 jit_solution(17068096029576888000)
XLA Ops:
  0.0 9.4 %fusion = f32[2,512,256]{2,1,0:T(8,128)S(1)} fusion(bf16[1,2,8192,512]{3,2,1,0:T(8,128)(2,1)} %param.10, bf16[1,8192,256]{2,1,0:T(8,128)(2,1)} %param.9), kind=kOutput, calls=%fused_computation | convolution fusion | flops 4294967296 | bytes 22020096 | tf_op jit(solution)/shard_map/dot_general | solution.py:62
  9.5 0.2 copy.31
  9.7 0.2 copy.32
  9.9 0.1 fusion.21
  10.0 0.1 copy.33
  10.1 0.1 copy.34
  10.3 0.1 copy.35
  10.4 0.1 copy.36
  10.5 0.4 fusion.158
  10.9 0.4 fusion.157
  11.3 0.2 fusion.12
  11.4 0.7 %maximum_bitcast_fusion = bf16[16,8,2,3,4,128]{5,4,1,0,2,3:T(4,128)(2,1)S(1)} fusion(bf16[8,16,1,4,2,128]{5,3,0,1,4,2:T(4,128)(2,1)S(1)} %get-tuple-element.29, bf16[8,16,1,4,2,128]{5,3,0,1,4,2:T(4,128)(2,1)S(1)} %fusion.157, bf16[8,16,1,4,2,128]{5,3,0,1,4,2:T(4,128)(2,1)S(1)} %get-tuple-element.28), kind=kLoop, calls=%fused_computation.10 | loop fusion | flops 786432 | bytes 1572864 | tf_op jit(solution)/shard_map/transpose | solution.py:78
  12.1 0.2 copy.37
  12.4 0.1 fusion.42
  12.4 0.2 reduce_window_sum.11
  12.6 0.2 select_reduce_fusion
  12.8 0.2 convolution_convert_fusion
  13.0 0.1 reshape.704
  13.2 0.1 broadcast_in_dim.155
  13.3 1.7 %copy.39 = bf16[128,2,12,128]{3,1,2,0:T(2,128)(2,1)} copy(bf16[128,2,12,128]{3,0,2,1:T(8,128)(2,1)S(1)} %bitcast_dynamic-update-slice_fusion) | data formatting | bytes 1572864 | tf_op jit(solution)/shard_map/scatter | solution.py:100
  15.0 11.2 %all-to-all-start = ((bf16[128,2,12,128]{3,1,2,0:T(2,128)(2,1)}), bf16[128,2,12,128]{3,1,2,0:T(2,128)(2,1)S(1)}, u32[]{:S(2)}, u32[]{:S(2)}) async-start(bf16[128,2,12,128]{3,1,2,0:T(2,128)(2,1)} %copy.39), calls=%async_computation | async-start | bytes 1572864 | tf_op jit(solution)/shard_map/all_to_all | solution.py:101
  26.2 0.3 cosine_convert_fusion
  26.5 16.0 %all-to-all-done = bf16[128,2,12,128]{3,1,2,0:T(2,128)(2,1)S(1)} async-done(((bf16[128,2,12,128]{3,1,2,0:T(2,128)(2,1)}), bf16[128,2,12,128]{3,1,2,0:T(2,128)(2,1)S(1)}, u32[]{:S(2)}, u32[]{:S(2)}) %all-to-all-start) | async-done | bytes 786464 | tf_op jit(solution)/shard_map/all_to_all | solution.py:101
  42.7 0.1 fusion.145
  42.8 0.1 add.250
  42.8 0.1 add.260
  43.0 0.1 sub.184
  43.2 0.1 fusion.76
  43.3 0.4 select_add_fusion
  43.7 0.8 %fusion.6 = f32[256,128,1]{1,0,2:T(8,128)S(1)} fusion(bf16[128,2,12,128]{3,1,2,0:T(2,128)(2,1)S(1)} %all-to-all-done, f32[256,128]{1,0:T(8,128)S(1)} %select_add_fusion, f32[256,12]{0,1:T(8,128)S(1)} %select_add_fusion.1, bf16[128,128,1]{1,0,2:T(8,128)(2,1)S(1)} %get-tuple-element.53, bf16[128,128,1]{1,0,2:T(8,128)(2,1)S(1)} %get-tuple-element.52), kind=kOutput, calls=%fused_computation.8 | convolution fusion | flops 202539008 | bytes 1126400 | tf_op jit(solution)/shard_map/dot_general | solution.py:125
  44.5 10.4 %all_to_all.10 = f32[16,16,128]{2,1,0:T(8,128)S(1)} all-to-all(f32[16,16,128]{2,1,0:T(8,128)S(1)} %bitcast.107), channel_id=1, replica_groups=mesh['ma'=16,'band'=8] {'ma'}, dimensions={0} | all-to-all | bytes 262144 | tf_op jit(solution)/shard_map/all_to_all | solution.py:129
  55.0 0.9 %fusion.30 = f32[128,128]{1,0:T(8,128)} fusion(f32[256,128]{1,0:T(8,128)S(1)} %bitcast.104, s32[128]{0:T(128)S(1)} %multiply_add_fusion.4), kind=kOutput, calls=%fused_computation.43 | convolution fusion | flops 50364416 | bytes 197120 | tf_op jit(solution)/shard_map/dot_general | solution.py:133
  (25 shorter events, 0.5 us)
Async XLA Ops:
  9.7 2.6 %copy-start = (f32[2,128]{1,0:T(2,128)S(1)}, f32[2,128]{1,0:T(2,128)}, u32[]{:S(2)}) copy-start(f32[2,128]{1,0:T(2,128)} %param.14) | copy-start | bytes 3076
  9.7 2.6 %copy-start.2 = (s32[128]{0:T(128)S(1)}, s32[128]{0:T(128)}, u32[]{:S(2)}) copy-start(s32[128]{0:T(128)} %param.12) | copy-start | bytes 1540
  9.7 2.7 %copy-start.3 = (s32[128]{0:T(128)S(1)}, s32[128]{0:T(128)}, u32[]{:S(2)}) copy-start(s32[128]{0:T(128)} %param.13) | copy-start | bytes 1540
  10.9 15.3 %copy-start.1 = (s32[128]{0:T(128)S(1)}, s32[128]{0:T(128)}, u32[]{:S(2)}) copy-start(s32[128]{0:T(128)} %param.11) | copy-start | bytes 1540
  15.0 27.5 %all-to-all-start = ((bf16[128,2,12,128]{3,1,2,0:T(2,128)(2,1)}), bf16[128,2,12,128]{3,1,2,0:T(2,128)(2,1)S(1)}, u32[]{:S(2)}, u32[]{:S(2)}) async-start(bf16[128,2,12,128]{3,1,2,0:T(2,128)(2,1)} %copy.39), calls=%async_computation | async-start | bytes 1572864 | tf_op jit(solution)/shard_map/all_to_all | solution.py:101
